TPU v7x, 32 devices: a whole 2x2x4 slice. The times are simulated.
32 devices in a mesh: sta: 8 (over z, x), tm: 4 (over y, core).
Axes of the slice: x: 2, y: 2, z: 4, core: 2. Of those that a mesh axis runs over, the one named last changes fastest.
Arguments:
- records: float32 [16, 1, 65536], P('sta', None, 'tm'), may hold values from -6 to 6
- pair_blocks: int32 [24, 2], P('sta'), may hold values from 0 to 7, as said below
- pair_count: int32 [8], P('sta'), may hold values from 0 to 3, as said below
Outputs:
- correlations: float32 [24, 2, 2, 2048], P('sta', None, None, 'tm')
Inputs may be any that keep to these rules, and one draw needn't show every extreme that they name: `pair_blocks`: slot q belongs to owner o = q // 3. Every slot names blocks a <= b with o <= a and b <= o + 3, both below 8; the slots in use have a < b. `pair_count`: an owner with no higher block within 3 has no slot in use.
All inputs are finite; a program needn't handle non-finite values.
Results may differ from a plain program's by a relative error of at most 0.0003.
Values sent between devices are 32-bit elements; how exact they have to be, the bound alone decides.
No kernel may reach another device: no remote copies, remote signals or barrier semaphores. Data moves between devices by JAX's collectives and lax.ppermute only.
A program may use at most 64 MiB of HBM per device.

v0:
```python
import math

import jax
import jax.numpy as jnp
from jax import lax
from jax.sharding import PartitionSpec as P

SAMPLES = 65536
FACTOR_A = 256
BAND = 32
LAGS = 4
REACH = 3


highest = lax.Precision.HIGHEST
epsilon = 1e-06


def passed_along(block, axis, distance):
    devices = range(lax.axis_size(axis))
    route = [(i - distance, i) for i in devices if i - distance in devices]
    return lax.ppermute(block, axis, route)


def angles(row_ids, col_ids, modulus):
    product = row_ids[:, None] * col_ids[None, :] % modulus
    radians = product.astype(jnp.float32) * (2.0 * math.pi / modulus)
    return (jnp.cos(radians), jnp.sin(radians))


def matmul(left_mat, right_mat):
    return jnp.dot(left_mat, right_mat, precision=highest, preferred_element_type=jnp.float32)


def local(records, pair_blocks, pair_count):
    stations, hour_count, time_cols = records.shape
    time_devices = lax.axis_size("tm")
    time_rank = lax.axis_index("tm")
    owner_id = lax.axis_index("sta")
    factor_a = FACTOR_A
    factor_b = SAMPLES // FACTOR_A
    rows_local = factor_a // time_devices
    cols_local = factor_b // time_devices
    series = stations * hour_count
    arranged = records.reshape(series, rows_local, factor_b).transpose(1, 0, 2)
    spread = lax.all_to_all(arranged, "tm", split_axis=2, concat_axis=0, tiled=True)
    index_a = jnp.arange(factor_a, dtype=jnp.int32)
    index_b = jnp.arange(factor_b, dtype=jnp.int32)
    cosine_a, sine_a = angles(index_a, index_a, factor_a)
    flat_rows = spread.reshape(factor_a, series * cols_local)
    both_a = jnp.concatenate([cosine_a, -sine_a], axis=0)
    section = matmul(both_a, flat_rows).reshape(2, factor_a, series, cols_local)
    section_real, section_imag = section[0], section[1]
    col_global = time_rank * cols_local + jnp.arange(cols_local, dtype=jnp.int32)
    cosine_t, sine_t = angles(index_a, col_global, SAMPLES)
    twisted_real = section_real * cosine_t[:, None, :] + section_imag * sine_t[:, None, :]
    twisted_imag = section_imag * cosine_t[:, None, :] - section_real * sine_t[:, None, :]
    twisted = jnp.stack([twisted_real, twisted_imag], axis=2)
    moved = lax.all_to_all(twisted, "tm", split_axis=0, concat_axis=3, tiled=True)
    cosine_b, sine_b = angles(index_b, index_b, factor_b)
    forward_b = jnp.concatenate(
        [jnp.concatenate([cosine_b, -sine_b], axis=1), jnp.concatenate([sine_b, cosine_b], axis=1)],
        axis=0,
    )
    spec = matmul(moved.reshape(rows_local * series, 2 * factor_b), forward_b)
    banded = spec.reshape(rows_local // BAND, BAND, series, 2, factor_b)
    band_power = jnp.mean(
        banded[:, :, :, 0] * banded[:, :, :, 0] + banded[:, :, :, 1] * banded[:, :, :, 1],
        axis=1,
        keepdims=True,
    )
    band_scale = lax.rsqrt(band_power + epsilon)
    whitened = (banded * band_scale[:, :, :, None]).reshape(
        rows_local, stations, hour_count, 2, factor_b
    )
    pieces = [whitened]
    for distance in range(1, REACH + 1):
        pieces.append(passed_along(whitened, "sta", -distance))
    nearby = jnp.stack(pieces)
    slot_total = pair_blocks.shape[0]
    first_off = pair_blocks[:, 0] - owner_id
    second_off = pair_blocks[:, 1] - owner_id
    left_spec = jnp.stack(
        [lax.dynamic_index_in_dim(nearby, first_off[s], 0, keepdims=False) for s in range(slot_total)]
    )
    right_spec = jnp.stack(
        [lax.dynamic_index_in_dim(nearby, second_off[s], 0, keepdims=False) for s in range(slot_total)]
    )
    left_real = left_spec[:, :, :, None, :, 0]
    left_imag = left_spec[:, :, :, None, :, 1]
    right_real = right_spec[:, :, None, :, :, 0]
    right_imag = right_spec[:, :, None, :, :, 1]
    cross_real = jnp.sum(left_real * right_real + left_imag * right_imag, axis=4)
    cross_imag = jnp.sum(left_imag * right_real - left_real * right_imag, axis=4)
    cross = jnp.concatenate([cross_real, cross_imag], axis=-1)
    inverse_b = jnp.concatenate(
        [jnp.concatenate([cosine_b, sine_b], axis=1), jnp.concatenate([-sine_b, cosine_b], axis=1)],
        axis=0,
    )
    lag = matmul(cross.reshape(-1, 2 * factor_b), inverse_b).reshape(
        slot_total, rows_local, stations, stations, 2, factor_b
    )
    lag_real, lag_imag = lag[:, :, :, :, 0], lag[:, :, :, :, 1]
    k1_ids = time_rank * rows_local + jnp.arange(rows_local, dtype=jnp.int32)
    cosine_u, sine_u = angles(k1_ids, index_b, SAMPLES)
    turn_real = lag_real * cosine_u[None, :, None, None, :] - lag_imag * sine_u[None, :, None, None, :]
    turn_imag = lag_real * sine_u[None, :, None, None, :] + lag_imag * cosine_u[None, :, None, None, :]
    lag_ids = jnp.concatenate(
        [jnp.arange(LAGS, dtype=jnp.int32), factor_a - LAGS + jnp.arange(LAGS, dtype=jnp.int32)]
    )
    cosine_l, sine_l = angles(lag_ids, k1_ids, factor_a)
    lag_weights = jnp.concatenate([cosine_l, -sine_l], axis=1).reshape(
        time_devices, 2 * LAGS // time_devices, 2 * rows_local
    )
    turned = jnp.concatenate([turn_real, turn_imag], axis=1)
    scale_out = 1.0 / math.sqrt(SAMPLES * hour_count)
    live_mask = (jnp.arange(slot_total) < pair_count[0]).astype(jnp.float32) * scale_out
    lag_block = jnp.einsum(
        "dwp,spijm->dsijwm",
        lag_weights,
        turned,
        precision=highest,
        preferred_element_type=jnp.float32,
    )
    lag_block = lag_block * live_mask[None, :, None, None, None, None]
    gathered = lax.all_to_all(lag_block, "tm", split_axis=0, concat_axis=0, tiled=True)
    total = jnp.sum(gathered, axis=0)
    return total.reshape(slot_total, stations, stations, 2 * LAGS * factor_b // time_devices)


def solution(mesh):
    placed = (P("sta", None, "tm"), P("sta", None), P("sta"))
    return jax.shard_map(
        local, mesh=mesh, in_specs=placed, out_specs=P("sta", None, None, "tm"), check_vma=False
    )
```

profile of v0, /device:TPU:10, one launch (start us, length us, event | category | flops | bytes accessed | tf_op | source)
XLA Modules:
  0.0 67.3 jit_solution(8096116514088384222)
XLA Ops:
  0.0 0.0 copy-start
  0.0 1.3 %reduce.1 = f32[2,16384]{1,0:T(2,128)S(1)} reduce(f32[2,1,16384]{2,1,0:T(1,128)} %param.3, f32[]{:T(128)} %constant.98), dimensions={1}, to_apply=%param.3.reduce_sub_computation | reduce | bytes 262148 | tf_op args[0]
  1.3 0.1 copy.48
  1.5 0.9 %reshape.278 = f32[4,1,8192]{2,1,0:T(1,128)} reshape(f32[256,2,64]{2,1,0:T(2,128)S(1)} %bitcast.101) | data formatting | bytes 262144
  2.4 3.3 %all-to-all-start = ((f32[4,1,8192]{2,1,0:T(1,128)}), f32[4,1,8192]{2,1,0:T(1,128)S(1)}, u32[]{:S(2)}, u32[]{:S(2)}) async-start(f32[4,1,8192]{2,1,0:T(1,128)} %reshape.278), calls=%async_computation | async-start | bytes 262144 | tf_op jit(solution)/shard_map/all_to_all | solution.py:46
  5.7 1.0 %fusion.24 = (f32[256,256]{0,1:T(8,128)S(1)}, f32[256,256]{0,1:T(8,128)S(1)}) fusion(), kind=kLoop, calls=%fused_computation.54 | loop fusion | flops 917504 | bytes 524288 | tf_op jit(solution)/shard_map/sin | solution.py:28
  6.7 1.0 %fusion.26 = f32[256,256]{0,1:T(8,128)S(1)} fusion(), kind=kLoop, calls=%fused_computation.56 | loop fusion | flops 983040 | bytes 262144 | tf_op jit(solution)/shard_map/neg | solution.py:51
  7.8 0.3 fusion.42
  8.8 0.0 copy-done
  8.8 0.7 %fusion.53 = (s32[1,1]{0,1:T(1,128)}, s32[1,1]{0,1:T(1,128)}, s32[1,1]{0,1:T(1,128)}, s32[1,1]{0,1:T(1,128)}, s32[1,1]{0,1:T(1,128)}, /*index=5*/s32[1,1]{0,1:T(1,128)}) fusion(s32[3,1]{0,1:T(1,128)S(1)} %get-tuple-element.27, s32[3,1]{0,1:T(1,128)S(1)} %get-tuple-element.28), kind=kLoop, calls=%fused_computation.110 | loop fusion | bytes 48 | tf_op jit(solution)/shard_map/slice | solution.py:84
  9.5 0.2 fusion.8
  9.7 0.1 pad_add_fusion
  9.8 0.5 all-to-all-done
  10.3 0.5 broadcast.325
  10.8 1.0 %reduce.2 = f32[4,8192]{1,0:T(4,128)S(1)} reduce(f32[4,1,8192]{2,1,0:T(1,128)S(1)} %all-to-all-done, f32[]{:T(128)} %broadcast.325), dimensions={1}, to_apply=%all_to_all.25.reduce_sub_computation | reduce | bytes 262148 | tf_op jit(solution)/shard_map/all_to_all | solution.py:46
  11.8 0.2 reshape.279
  12.0 0.2 copy.65
  12.2 0.2 copy.50
  12.4 0.2 reshape.268
  12.6 0.5 fusion.10
  13.1 0.3 copy.51
  13.5 1.3 %reshape.280 = f32[4,1,16384]{2,1,0:T(1,128)} reshape(f32[256,2,2,64]{3,2,1,0:T(2,128)S(1)} %copy.51) | data formatting | bytes 524288
  14.7 3.4 %all-to-all-start.1 = ((f32[4,1,16384]{2,1,0:T(1,128)}), f32[4,1,16384]{2,1,0:T(1,128)S(1)}, u32[]{:S(2)}, u32[]{:S(2)}) async-start(f32[4,1,16384]{2,1,0:T(1,128)} %reshape.280), calls=%async_computation.1 | async-start | bytes 524288 | tf_op jit(solution)/shard_map/all_to_all | solution.py:59
  18.1 0.1 fusion.48
  18.2 5.8 %all-to-all-done.1 = f32[4,1,16384]{2,1,0:T(1,128)S(1)} async-done(((f32[4,1,16384]{2,1,0:T(1,128)}), f32[4,1,16384]{2,1,0:T(1,128)S(1)}, u32[]{:S(2)}, u32[]{:S(2)}) %all-to-all-start.1) | async-done | bytes 262176 | tf_op jit(solution)/shard_map/all_to_all | solution.py:59
  24.1 1.4 %reduce.3 = f32[4,16384]{1,0:T(4,128)S(1)} reduce(f32[4,1,16384]{2,1,0:T(1,128)S(1)} %all-to-all-done.1, f32[]{:T(128)} %broadcast.325), dimensions={1}, to_apply=%all_to_all.28.reduce_sub_computation | reduce | bytes 524292 | tf_op jit(solution)/shard_map/all_to_all | solution.py:59
  25.5 0.4 reshape.281
  25.9 0.3 copy.76
  26.2 0.3 dot_general.23
  26.6 1.2 %fusion.17 = f32[2,32,2,2,256]{4,1,3,2,0:T(8,128)S(1)} fusion(f32[2,256,512,1,1]{2,1,0,4,3:T(8,128)S(1)} %bitcast.97, f32[2,32,2,512]{3,1,0,2:T(8,128)S(1)} %dot_general.23), kind=kOutput, calls=%fused_computation.41 | convolution fusion | flops 402653184 | bytes 1572864 | tf_op jit(solution)/shard_map/dot_general | solution.py:32
  27.9 1.9 %collective-permute-start.2 = (f32[64,2,1,2,256]{4,0,3,1,2:T(8,128)S(1)}, f32[64,2,1,2,256]{4,0,3,1,2:T(8,128)S(1)}, u32[]{:S(2)}, u32[]{:S(2)}) collective-permute-start(f32[64,2,1,2,256]{4,0,3,1,2:T(8,128)S(1)} %bitcast.104), channel_id=1, source_target_pairs={{12,0},{16,4},{20,8},{24,12},{28,16},{13,1},{17,5},{21,9},{25,13},... | collective-permute-start | bytes 786440 | tf_op jit(solution)/shard_map/ppermute | solution.py:22
  29.8 1.9 %collective-permute-start.1 = (f32[64,2,1,2,256]{4,0,3,1,2:T(8,128)S(1)}, f32[64,2,1,2,256]{4,0,3,1,2:T(8,128)S(1)}, u32[]{:S(2)}, u32[]{:S(2)}) collective-permute-start(f32[64,2,1,2,256]{4,0,3,1,2:T(8,128)S(1)} %bitcast.105), channel_id=1, source_target_pairs={{8,0},{12,4},{16,8},{20,12},{24,16},{28,20},{9,1},{13,5},{17,9},{2... | collective-permute-start | bytes 786440 | tf_op jit(solution)/shard_map/ppermute | solution.py:22
  31.7 2.1 %collective-permute-start = (f32[64,2,1,2,256]{4,0,3,1,2:T(8,128)S(1)}, f32[64,2,1,2,256]{4,0,3,1,2:T(8,128)S(1)}, u32[]{:S(2)}, u32[]{:S(2)}) collective-permute-start(f32[64,2,1,2,256]{4,0,3,1,2:T(8,128)S(1)} %bitcast.106), channel_id=1, source_target_pairs={{4,0},{8,4},{12,8},{16,12},{20,16},{24,20},{28,24},{5,1},{9,5},{13... | collective-permute-start | bytes 786440 | tf_op jit(solution)/shard_map/ppermute | solution.py:22
  45.5 0.3 fusion.40
  45.8 0.0 collective-permute-done.2
  45.8 0.0 collective-permute-done.1
  45.8 9.4 %collective-permute-done = f32[64,2,1,2,256]{4,0,3,1,2:T(8,128)S(1)} collective-permute-done((f32[64,2,1,2,256]{4,0,3,1,2:T(8,128)S(1)}, f32[64,2,1,2,256]{4,0,3,1,2:T(8,128)S(1)}, u32[]{:S(2)}, u32[]{:S(2)}) %collective-permute-start) | collective-permute-done | bytes 262176 | tf_op jit(solution)/shard_map/ppermute | solution.py:22
  55.2 0.1 pad_maximum_fusion.4
  55.3 0.2 constant_dynamic-slice_fusion.5
  55.5 0.1 pad_maximum_fusion.6
  55.6 0.1 slice_bitcast_fusion.4
  55.6 0.1 pad_maximum_fusion.5
  55.7 0.1 slice_bitcast_fusion.5
  55.8 0.2 multiply_add_fusion.1
  56.0 2.7 %fusion = f32[3,64,2,2,2,256]{5,1,4,3,2,0:T(8,128)S(1)} fusion(f32[2,256,512,1,1,1]{2,1,0,5,4,3:T(8,128)S(1)} %bitcast.98, f32[3,64,2,2,256]{4,1,3,2,0:T(8,128)S(1)} %get-tuple-element.8, f32[3,64,2,2,256]{4,1,3,2,0:T(8,128)S(1)} %get-tuple-element.7), kind=kOutput, calls=%fused_computation.1 | convolution fusion | flops 2416312320 | bytes 4194304 | tf_op jit(solution)/shard_map/dot_general | solution.py:32
  58.7 0.2 multiply_subtract_fusion
  58.9 0.9 %fusion.7 = f32[4,3,2,2,2,256]{5,0,4,3,2,1:T(4,128)S(1)} fusion(f32[3,64,2,2,256]{4,1,3,2,0:T(8,128)S(1)} %get-tuple-element.6, f32[3,64,2,2,256]{4,1,3,2,0:T(8,128)S(1)} %get-tuple-element.5, f32[3]{0:T(128)S(1)} %compare_select_fusion, f32[4,2,64]{2,0,1:T(4,128)S(1)} %get-tuple-element.26, f32[4,2,64]{2,0,1:T(4,128)S(1)} %get-tuple-element.25), kind=kOutput, calls=%fused_computation.13 | convolution fusion | flops 38167552 | bytes 1675276 | tf_op jit(solution)/shard_map/dwp,spijm->dsijwm/dot_general | solution.py:118
  59.8 0.1 copy.58
  59.9 6.7 %all_to_all.35 = f32[4,3,2,2,2,256]{5,4,3,2,1,0:T(2,128)S(1)} all-to-all(f32[4,3,2,2,2,256]{5,4,3,2,1,0:T(2,128)S(1)} %copy.58), channel_id=1, replica_groups=mesh['sta'=8,'tm'=4] {'tm'}, dimensions={0} | all-to-all | bytes 196608 | tf_op jit(solution)/shard_map/all_to_all | solution.py:126
  66.6 0.6 reshape.270
  (13 shorter events, 0.2 us)
Async XLA Ops:
  0.0 8.8 %copy-start = (s32[3,2]{0,1:T(2,128)S(1)}, s32[3,2]{0,1:T(2,128)}, u32[]{:S(2)}) copy-start(s32[3,2]{0,1:T(2,128)} %param.4) | copy-start | bytes 76
  2.4 7.9 %all-to-all-start = ((f32[4,1,8192]{2,1,0:T(1,128)}), f32[4,1,8192]{2,1,0:T(1,128)S(1)}, u32[]{:S(2)}, u32[]{:S(2)}) async-start(f32[4,1,8192]{2,1,0:T(1,128)} %reshape.278), calls=%async_computation | async-start | bytes 262144 | tf_op jit(solution)/shard_map/all_to_all | solution.py:46
  14.7 9.4 %all-to-all-start.1 = ((f32[4,1,16384]{2,1,0:T(1,128)}), f32[4,1,16384]{2,1,0:T(1,128)S(1)}, u32[]{:S(2)}, u32[]{:S(2)}) async-start(f32[4,1,16384]{2,1,0:T(1,128)} %reshape.280), calls=%async_computation.1 | async-start | bytes 524288 | tf_op jit(solution)/shard_map/all_to_all | solution.py:59
  27.9 17.9 %collective-permute-start.2 = (f32[64,2,1,2,256]{4,0,3,1,2:T(8,128)S(1)}, f32[64,2,1,2,256]{4,0,3,1,2:T(8,128)S(1)}, u32[]{:S(2)}, u32[]{:S(2)}) collective-permute-start(f32[64,2,1,2,256]{4,0,3,1,2:T(8,128)S(1)} %bitcast.104), channel_id=1, source_target_pairs={{12,0},{16,4},{20,8},{24,12},{28,16},{13,1},{17,5},{21,9},{25,13},... | collective-permute-start | bytes 786440 | tf_op jit(solution)/shard_map/ppermute | solution.py:22
  29.8 16.0 %collective-permute-start.1 = (f32[64,2,1,2,256]{4,0,3,1,2:T(8,128)S(1)}, f32[64,2,1,2,256]{4,0,3,1,2:T(8,128)S(1)}, u32[]{:S(2)}, u32[]{:S(2)}) collective-permute-start(f32[64,2,1,2,256]{4,0,3,1,2:T(8,128)S(1)} %bitcast.105), channel_id=1, source_target_pairs={{8,0},{12,4},{16,8},{20,12},{24,16},{28,20},{9,1},{13,5},{17,9},{2... | collective-permute-start | bytes 786440 | tf_op jit(solution)/shard_map/ppermute | solution.py:22
  31.7 23.5 %collective-permute-start = (f32[64,2,1,2,256]{4,0,3,1,2:T(8,128)S(1)}, f32[64,2,1,2,256]{4,0,3,1,2:T(8,128)S(1)}, u32[]{:S(2)}, u32[]{:S(2)}) collective-permute-start(f32[64,2,1,2,256]{4,0,3,1,2:T(8,128)S(1)} %bitcast.106), channel_id=1, source_target_pairs={{4,0},{8,4},{12,8},{16,12},{20,16},{24,20},{28,24},{5,1},{9,5},{13... | collective-permute-start | bytes 786440 | tf_op jit(solution)/shard_map/ppermute | solution.py:22
where the time goes:
time: 67.9 us; the launch traced here: 67.3 us
  waiting for transfers between devices  15.8 us (23%)
  starting transfers between devices  12.7 us (19%)
  between operations  12.6 us (19%)
  other arithmetic  7.56 us (11%)
  local copies, waits for them, and re-layouts  6.71 us (10%)
  blocking collectives  6.67 us (10%)
  matrix products  5.25 us (8%)
    ppermute x3, waiting for transfers between devices, passed_along(): return lax.ppermute(block, axis, route)  9.41 us
    all_to_all x1, blocking collectives, local(): lax.all_to_all(lag_block, 'tm', split_axis=0, concat_axis=0, tiled=True)  6.67 us
    ppermute x3, starting transfers between devices, passed_along(): return lax.ppermute(block, axis, route)  5.94 us
    all_to_all x1, waiting for transfers between devices, local(): lax.all_to_all(twisted, 'tm', split_axis=0, concat_axis=3, tiled=True)  5.84 us
    dot_general x3, matrix products, matmul(): jnp.dot(left_mat, right_mat, precision=highest, preferred_element_type=jn...  4.32 us
    all_to_all x1, starting transfers between devices, local(): lax.all_to_all(twisted, 'tm', split_axis=0, concat_axis=3, tiled=True)  3.4 us
    all_to_all x1, starting transfers between devices, local(): lax.all_to_all(arranged, 'tm', split_axis=2, concat_axis=0, tiled=True)  3.32 us
    unnamed x7, local copies, waits for them, and re-layouts  2.83 us
  transfers between devices with their start and end apart: 5, of which 3 were waited for; matrix products, arithmetic and copies ran while one was open for 6% of the time, Pallas kernels for 0%

commit v1 on v0

--- a/solution.py
+++ b/solution.py
@@ -1,6 +1,7 @@
 import math
 
 import jax
+import numpy as np
 import jax.numpy as jnp
 from jax import lax
 from jax.sharding import PartitionSpec as P
@@ -46,13 +47,30 @@
     spread = lax.all_to_all(arranged, "tm", split_axis=2, concat_axis=0, tiled=True)
     index_a = jnp.arange(factor_a, dtype=jnp.int32)
     index_b = jnp.arange(factor_b, dtype=jnp.int32)
-    cosine_a, sine_a = angles(index_a, index_a, factor_a)
+    paired = rows_local == 2 * BAND and factor_a == 2 * BAND * time_devices
+    if paired:
+        order = [
+            piece
+            for t in range(time_devices)
+            for piece in (np.arange(BAND) + BAND * t, factor_a - BAND * (t + 1) + np.arange(BAND))
+        ]
+        k1_order = jnp.asarray(np.concatenate(order).astype(np.int32))
+        k1_ids = jnp.concatenate(
+            [
+                BAND * time_rank + jnp.arange(BAND, dtype=jnp.int32),
+                factor_a - BAND * (time_rank + 1) + jnp.arange(BAND, dtype=jnp.int32),
+            ]
+        )
+    else:
+        k1_order = index_a
+        k1_ids = time_rank * rows_local + jnp.arange(rows_local, dtype=jnp.int32)
+    cosine_a, sine_a = angles(k1_order, index_a, factor_a)
     flat_rows = spread.reshape(factor_a, series * cols_local)
     both_a = jnp.concatenate([cosine_a, -sine_a], axis=0)
     section = matmul(both_a, flat_rows).reshape(2, factor_a, series, cols_local)
     section_real, section_imag = section[0], section[1]
     col_global = time_rank * cols_local + jnp.arange(cols_local, dtype=jnp.int32)
-    cosine_t, sine_t = angles(index_a, col_global, SAMPLES)
+    cosine_t, sine_t = angles(k1_order, col_global, SAMPLES)
     twisted_real = section_real * cosine_t[:, None, :] + section_imag * sine_t[:, None, :]
     twisted_imag = section_imag * cosine_t[:, None, :] - section_real * sine_t[:, None, :]
     twisted = jnp.stack([twisted_real, twisted_imag], axis=2)
@@ -70,13 +88,30 @@
         keepdims=True,
     )
     band_scale = lax.rsqrt(band_power + epsilon)
-    whitened = (banded * band_scale[:, :, :, None]).reshape(
-        rows_local, stations, hour_count, 2, factor_b
-    )
+    whitened = (banded * band_scale[:, :, :, None]).reshape(rows_local, series, 2, factor_b)
+    if paired:
+        scale_row = band_scale[:, 0].transpose(1, 0, 2)[None]
+        sent = jnp.concatenate([spec.reshape(rows_local, series, 2, factor_b)[: BAND + 1], scale_row])
+
+        def rebuilt(piece):
+            spec_part = piece[: BAND + 1]
+            scale_low = piece[BAND + 1, :, 0][None, :, None, :]
+            scale_high = piece[BAND + 1, :, 1][None, :, None, :]
+            conj_sign = jnp.asarray([1.0, -1.0], jnp.float32)[None, None, :, None]
+            mirrored = spec_part[1:BAND][::-1, :, :, ::-1] * conj_sign
+            high = jnp.concatenate([spec_part[BAND:], mirrored])
+            return jnp.concatenate([spec_part[:BAND] * scale_low, high * scale_high])
+
+    else:
+        sent = whitened
+
+        def rebuilt(piece):
+            return piece
+
     pieces = [whitened]
     for distance in range(1, REACH + 1):
-        pieces.append(passed_along(whitened, "sta", -distance))
-    nearby = jnp.stack(pieces)
+        pieces.append(rebuilt(passed_along(sent, "sta", -distance)))
+    nearby = jnp.stack(pieces).reshape(REACH + 1, rows_local, stations, hour_count, 2, factor_b)
     slot_total = pair_blocks.shape[0]
     first_off = pair_blocks[:, 0] - owner_id
     second_off = pair_blocks[:, 1] - owner_id
@@ -101,7 +136,6 @@
         slot_total, rows_local, stations, stations, 2, factor_b
     )
     lag_real, lag_imag = lag[:, :, :, :, 0], lag[:, :, :, :, 1]
-    k1_ids = time_rank * rows_local + jnp.arange(rows_local, dtype=jnp.int32)
     cosine_u, sine_u = angles(k1_ids, index_b, SAMPLES)
     turn_real = lag_real * cosine_u[None, :, None, None, :] - lag_imag * sine_u[None, :, None, None, :]
     turn_imag = lag_real * sine_u[None, :, None, None, :] + lag_imag * cosine_u[None, :, None, None, :]

time: 67.9 us -> 72.5 us (1.068)
  the two profiles are of different devices: /device:TPU:10 before, /device:TPU:2 now
where the time goes in v1:
time: 72.5 us; the launch traced here: 71.1 us
  waiting for transfers between devices  17.5 us (24%)
  between operations  13 us (18%)
  starting transfers between devices  11.4 us (16%)
  other arithmetic  9.1 us (13%)
  local copies, waits for them, and re-layouts  8.12 us (11%)
  blocking collectives  6.67 us (9%)
  matrix products  5.25 us (7%)
    ppermute x3, waiting for transfers between devices, passed_along(): return lax.ppermute(block, axis, route)  11.7 us
    all_to_all x1, blocking collectives, local(): lax.all_to_all(lag_block, 'tm', split_axis=0, concat_axis=0, tiled=True)  6.67 us
    all_to_all x1, waiting for transfers between devices, local(): lax.all_to_all(twisted, 'tm', split_axis=0, concat_axis=3, tiled=True)  5.84 us
    ppermute x3, starting transfers between devices, passed_along(): return lax.ppermute(block, axis, route)  4.69 us
    dot_general x3, matrix products, matmul(): jnp.dot(left_mat, right_mat, precision=highest, preferred_element_type=jn...  4.32 us
    all_to_all x1, starting transfers between devices, local(): lax.all_to_all(twisted, 'tm', split_axis=0, concat_axis=3, tiled=True)  3.4 us
    all_to_all x1, starting transfers between devices, local(): lax.all_to_all(arranged, 'tm', split_axis=2, concat_axis=0, tiled=True)  3.32 us
    unnamed x17, local copies, waits for them, and re-layouts  2.86 us
  transfers between devices with their start and end apart: 5, of which 3 were waited for; matrix products, arithmetic and copies ran while one was open for 8% of the time, Pallas kernels for 0%

profile of v1, /device:TPU:2, one launch (start us, length us, event | category | flops | bytes accessed | tf_op | source)
XLA Modules:
  0.0 71.1 jit_solution(2026682355220224518)
XLA Ops:
  0.0 0.0 copy-start
  0.0 1.3 %reduce.1 = f32[2,16384]{1,0:T(2,128)S(1)} reduce(f32[2,1,16384]{2,1,0:T(1,128)} %param.7, f32[]{:T(128)} %constant.110), dimensions={1}, to_apply=%param.7.reduce_sub_computation | reduce | bytes 262148 | tf_op args[0]
  1.3 0.1 copy.51
  1.5 0.9 %reshape.305 = f32[4,1,8192]{2,1,0:T(1,128)} reshape(f32[256,2,64]{2,1,0:T(2,128)S(1)} %bitcast.123) | data formatting | bytes 262144
  2.4 3.3 %all-to-all-start = ((f32[4,1,8192]{2,1,0:T(1,128)}), f32[4,1,8192]{2,1,0:T(1,128)S(1)}, u32[]{:S(2)}, u32[]{:S(2)}) async-start(f32[4,1,8192]{2,1,0:T(1,128)} %reshape.305), calls=%async_computation | async-start | bytes 262144 | tf_op jit(solution)/shard_map/all_to_all | solution.py:47
  5.7 1.0 %fusion.31 = (f32[256,256]{0,1:T(8,128)S(1)}, f32[256,256]{0,1:T(8,128)S(1)}) fusion(), kind=kLoop, calls=%fused_computation.80 | loop fusion | flops 917504 | bytes 524288 | tf_op jit(solution)/shard_map/sin | solution.py:29
  6.8 1.0 %fusion.35 = f32[256,256]{0,1:T(8,128)S(1)} fusion(), kind=kLoop, calls=%fused_computation.87 | loop fusion | flops 983040 | bytes 262144 | tf_op jit(solution)/shard_map/neg | solution.py:80
  7.7 0.0 copy-done.1
  7.8 0.7 fusion.64
  16.2 0.0 copy-done
  16.3 1.0 %fusion.33 = (f32[256,256]{0,1:T(8,128)S(1)}, f32[256,256]{0,1:T(8,128)S(1)}) fusion(s32[256]{0:T(256)S(1)} %copy-done), kind=kLoop, calls=%fused_computation.82 | loop fusion | flops 983040 | bytes 525312 | tf_op jit(solution)/shard_map/cos | solution.py:29
  17.3 0.3 fusion.48
  17.7 0.1 pad_add_fusion.1
  17.8 0.3 fusion.46
  22.7 0.1 pad_add_fusion
  22.7 0.1 fusion.11
  22.8 0.0 all-to-all-done
  22.9 0.5 broadcast.362
  23.4 1.0 %reduce.2 = f32[4,8192]{1,0:T(4,128)S(1)} reduce(f32[4,1,8192]{2,1,0:T(1,128)S(1)} %all-to-all-done, f32[]{:T(128)} %broadcast.362), dimensions={1}, to_apply=%all_to_all.25.reduce_sub_computation | reduce | bytes 262148 | tf_op jit(solution)/shard_map/all_to_all | solution.py:47
  24.4 0.2 reshape.306
  24.6 0.2 copy.67
  24.7 0.2 copy.53
  25.0 0.2 reshape.295
  25.1 0.5 fusion.14
  25.7 0.3 copy.54
  26.0 1.3 %reshape.307 = f32[4,1,16384]{2,1,0:T(1,128)} reshape(f32[256,2,2,64]{3,2,1,0:T(2,128)S(1)} %copy.54) | data formatting | bytes 524288
  27.3 3.4 %all-to-all-start.1 = ((f32[4,1,16384]{2,1,0:T(1,128)}), f32[4,1,16384]{2,1,0:T(1,128)S(1)}, u32[]{:S(2)}, u32[]{:S(2)}) async-start(f32[4,1,16384]{2,1,0:T(1,128)} %reshape.307), calls=%async_computation.1 | async-start | bytes 524288 | tf_op jit(solution)/shard_map/all_to_all | solution.py:77
  30.7 0.1 fusion.54
  30.8 5.8 %all-to-all-done.1 = f32[4,1,16384]{2,1,0:T(1,128)S(1)} async-done(((f32[4,1,16384]{2,1,0:T(1,128)}), f32[4,1,16384]{2,1,0:T(1,128)S(1)}, u32[]{:S(2)}, u32[]{:S(2)}) %all-to-all-start.1) | async-done | bytes 262176 | tf_op jit(solution)/shard_map/all_to_all | solution.py:77
  36.7 1.4 %reduce.3 = f32[4,16384]{1,0:T(4,128)S(1)} reduce(f32[4,1,16384]{2,1,0:T(1,128)S(1)} %all-to-all-done.1, f32[]{:T(128)} %broadcast.362), dimensions={1}, to_apply=%all_to_all.28.reduce_sub_computation | reduce | bytes 524292 | tf_op jit(solution)/shard_map/all_to_all | solution.py:77
  38.0 0.4 reshape.308
  38.5 0.3 copy.87
  38.8 0.3 reshape.296
  39.1 1.2 %fusion.9 = f32[128,512]{1,0:T(8,128)S(1)} fusion(f32[128,512]{1,0:T(8,128)S(1)} %reshape.296, f32[256,256]{0,1:T(8,128)S(1)} %get-tuple-element.54, f32[256,256]{0,1:T(8,128)S(1)} %get-tuple-element.53, f32[256,256]{0,1:T(8,128)S(1)} %fusion.35), kind=kOutput, calls=%fused_computation.15 | convolution fusion | flops 403439616 | bytes 1310720 | tf_op jit(solution)/shard_map/dot_general | solution.py:33
  40.3 0.2 reshape.298
  40.5 0.3 fusion.34
  40.8 0.1 slice.132
  40.9 0.0 copy-start.2
  41.0 1.3 %collective-permute-start.1 = (f32[34,2,2,256]{3,0,2,1:T(8,128)S(1)}, f32[34,2,2,256]{3,0,2,1:T(8,128)S(1)}, u32[]{:S(2)}, u32[]{:S(2)}) collective-permute-start(f32[34,2,2,256]{3,0,2,1:T(8,128)S(1)} %pad_maximum_fusion.9), channel_id=1, source_target_pairs={{8,0},{12,4},{16,8},{20,12},{24,16},{28,20},{9,1},{13,5},{17,9},{2... | collective-permute-start | bytes 417800 | tf_op jit(solution)/shard_map/ppermute | solution.py:23
  42.3 1.3 %collective-permute-start.2 = (f32[34,2,2,256]{3,0,2,1:T(8,128)S(1)}, f32[34,2,2,256]{3,0,2,1:T(8,128)S(1)}, u32[]{:S(2)}, u32[]{:S(2)}) collective-permute-start(f32[34,2,2,256]{3,0,2,1:T(8,128)S(1)} %pad_maximum_fusion.9), channel_id=1, source_target_pairs={{12,0},{16,4},{20,8},{24,12},{28,16},{13,1},{17,5},{21,9},{25,13},... | collective-permute-start | bytes 417800 | tf_op jit(solution)/shard_map/ppermute | solution.py:23
  43.6 2.1 %collective-permute-start = (f32[34,2,2,256]{3,0,2,1:T(8,128)S(1)}, f32[34,2,2,256]{3,0,2,1:T(8,128)S(1)}, u32[]{:S(2)}, u32[]{:S(2)}) collective-permute-start(f32[34,2,2,256]{3,0,2,1:T(8,128)S(1)} %pad_maximum_fusion.9), channel_id=1, source_target_pairs={{4,0},{8,4},{12,8},{16,12},{20,16},{24,20},{28,24},{5,1},{9,5},{13... | collective-permute-start | bytes 417800 | tf_op jit(solution)/shard_map/ppermute | solution.py:23
  45.7 0.2 reshape.297
  45.9 0.1 copy_multiply_fusion
  46.0 4.0 %collective-permute-done.1 = f32[34,2,2,256]{3,0,2,1:T(8,128)S(1)} collective-permute-done((f32[34,2,2,256]{3,0,2,1:T(8,128)S(1)}, f32[34,2,2,256]{3,0,2,1:T(8,128)S(1)}, u32[]{:S(2)}, u32[]{:S(2)}) %collective-permute-start.1) | collective-permute-done | bytes 139296 | tf_op jit(solution)/shard_map/ppermute | solution.py:23
  50.0 0.3 rev.10
  50.3 7.7 %collective-permute-done.2 = f32[34,2,2,256]{3,0,2,1:T(8,128)S(1)} collective-permute-done((f32[34,2,2,256]{3,0,2,1:T(8,128)S(1)}, f32[34,2,2,256]{3,0,2,1:T(8,128)S(1)}, u32[]{:S(2)}, u32[]{:S(2)}) %collective-permute-start.2) | collective-permute-done | bytes 139296 | tf_op jit(solution)/shard_map/ppermute | solution.py:23
  58.0 0.3 rev.11
  58.2 0.0 collective-permute-done
  58.3 0.3 rev.9
  58.7 0.0 copy-done.2
  58.7 0.1 broadcast_multiply_fusion.2
  59.0 0.1 pad_maximum_fusion.5
  59.1 0.2 dynamic-slice_bitcast_fusion.5
  59.3 0.1 pad_maximum_fusion.6
  59.4 0.1 slice_bitcast_fusion.5
  59.4 0.1 pad_maximum_fusion.7
  59.5 0.1 slice_bitcast_fusion.4
  59.6 0.2 multiply_add_fusion.1
  59.8 2.7 %fusion = f32[3,64,2,2,2,256]{5,1,4,3,2,0:T(8,128)S(1)} fusion(f32[2,256,512,1,1,1]{2,1,0,5,4,3:T(8,128)S(1)} %bitcast.120, f32[3,64,2,2,256]{4,1,3,2,0:T(8,128)S(1)} %get-tuple-element.8, f32[3,64,2,2,256]{4,1,3,2,0:T(8,128)S(1)} %get-tuple-element.7), kind=kOutput, calls=%fused_computation.1 | convolution fusion | flops 2416312320 | bytes 4194304 | tf_op jit(solution)/shard_map/dot_general | solution.py:33
  62.5 0.2 multiply_subtract_fusion
  62.7 0.9 %fusion.7 = f32[4,3,2,2,2,256]{5,0,4,3,2,1:T(4,128)S(1)} fusion(f32[3,64,2,2,256]{4,1,3,2,0:T(8,128)S(1)} %get-tuple-element.6, f32[3,64,2,2,256]{4,1,3,2,0:T(8,128)S(1)} %get-tuple-element.5, f32[3]{0:T(128)S(1)} %compare_select_fusion, f32[4,2,64]{2,0,1:T(4,128)S(1)} %get-tuple-element.32, f32[4,2,64]{2,0,1:T(4,128)S(1)} %get-tuple-element.31), kind=kOutput, calls=%fused_computation.13 | convolution fusion | flops 38167552 | bytes 1675276 | tf_op jit(solution)/shard_map/dwp,spijm->dsijwm/dot_general | solution.py:152
  63.7 0.1 copy.62
  63.7 6.7 %all_to_all.35 = f32[4,3,2,2,2,256]{5,4,3,2,1,0:T(2,128)S(1)} all-to-all(f32[4,3,2,2,2,256]{5,4,3,2,1,0:T(2,128)S(1)} %copy.62), channel_id=1, replica_groups=mesh['sta'=8,'tm'=4] {'tm'}, dimensions={0} | all-to-all | bytes 196608 | tf_op jit(solution)/shard_map/all_to_all | solution.py:160
  70.4 0.6 reshape.299
  (42 shorter events, 0.5 us)
Async XLA Ops:
  0.0 16.2 %copy-start = (s32[256]{0:T(256)S(1)}, s32[256]{0:T(256)}, u32[]{:S(2)}) copy-start(s32[256]{0:T(256)} %constant.105.clone) | copy-start | bytes 3076
  0.0 7.7 %copy-start.1 = (s32[3,2]{0,1:T(2,128)S(1)}, s32[3,2]{0,1:T(2,128)}, u32[]{:S(2)}) copy-start(s32[3,2]{0,1:T(2,128)} %param.8) | copy-start | bytes 76
  2.4 20.5 %all-to-all-start = ((f32[4,1,8192]{2,1,0:T(1,128)}), f32[4,1,8192]{2,1,0:T(1,128)S(1)}, u32[]{:S(2)}, u32[]{:S(2)}) async-start(f32[4,1,8192]{2,1,0:T(1,128)} %reshape.305), calls=%async_computation | async-start | bytes 262144 | tf_op jit(solution)/shard_map/all_to_all | solution.py:47
  27.3 9.4 %all-to-all-start.1 = ((f32[4,1,16384]{2,1,0:T(1,128)}), f32[4,1,16384]{2,1,0:T(1,128)S(1)}, u32[]{:S(2)}, u32[]{:S(2)}) async-start(f32[4,1,16384]{2,1,0:T(1,128)} %reshape.307), calls=%async_computation.1 | async-start | bytes 524288 | tf_op jit(solution)/shard_map/all_to_all | solution.py:77
  40.9 17.7 %copy-start.2 = (f32[2]{0:T(128)S(1)}, f32[2]{0:T(128)}, u32[]{:S(2)}) copy-start(f32[2]{0:T(128)} %constant.106.clone) | copy-start | bytes 28
  41.0 9.0 %collective-permute-start.1 = (f32[34,2,2,256]{3,0,2,1:T(8,128)S(1)}, f32[34,2,2,256]{3,0,2,1:T(8,128)S(1)}, u32[]{:S(2)}, u32[]{:S(2)}) collective-permute-start(f32[34,2,2,256]{3,0,2,1:T(8,128)S(1)} %pad_maximum_fusion.9), channel_id=1, source_target_pairs={{8,0},{12,4},{16,8},{20,12},{24,16},{28,20},{9,1},{13,5},{17,9},{2... | collective-permute-start | bytes 417800 | tf_op jit(solution)/shard_map/ppermute | solution.py:23
  42.3 15.6 %collective-permute-start.2 = (f32[34,2,2,256]{3,0,2,1:T(8,128)S(1)}, f32[34,2,2,256]{3,0,2,1:T(8,128)S(1)}, u32[]{:S(2)}, u32[]{:S(2)}) collective-permute-start(f32[34,2,2,256]{3,0,2,1:T(8,128)S(1)} %pad_maximum_fusion.9), channel_id=1, source_target_pairs={{12,0},{16,4},{20,8},{24,12},{28,16},{13,1},{17,5},{21,9},{25,13},... | collective-permute-start | bytes 417800 | tf_op jit(solution)/shard_map/ppermute | solution.py:23
  43.6 14.7 %collective-permute-start = (f32[34,2,2,256]{3,0,2,1:T(8,128)S(1)}, f32[34,2,2,256]{3,0,2,1:T(8,128)S(1)}, u32[]{:S(2)}, u32[]{:S(2)}) collective-permute-start(f32[34,2,2,256]{3,0,2,1:T(8,128)S(1)} %pad_maximum_fusion.9), channel_id=1, source_target_pairs={{4,0},{8,4},{12,8},{16,12},{20,16},{24,20},{28,24},{5,1},{9,5},{13... | collective-permute-start | bytes 417800 | tf_op jit(solution)/shard_map/ppermute | solution.py:23

commit v2 on v1

--- a/solution.py
+++ b/solution.py
@@ -1,7 +1,6 @@
 import math
 
 import jax
-import numpy as np
 import jax.numpy as jnp
 from jax import lax
 from jax.sharding import PartitionSpec as P
@@ -49,12 +48,13 @@
     index_b = jnp.arange(factor_b, dtype=jnp.int32)
     paired = rows_local == 2 * BAND and factor_a == 2 * BAND * time_devices
     if paired:
-        order = [
-            piece
-            for t in range(time_devices)
-            for piece in (np.arange(BAND) + BAND * t, factor_a - BAND * (t + 1) + np.arange(BAND))
-        ]
-        k1_order = jnp.asarray(np.concatenate(order).astype(np.int32))
+        owner_of_row = index_a // rows_local
+        place_in_row = index_a % rows_local
+        k1_order = jnp.where(
+            place_in_row < BAND,
+            BAND * owner_of_row + place_in_row,
+            factor_a - BAND * (owner_of_row + 2) + place_in_row,
+        )
         k1_ids = jnp.concatenate(
             [
                 BAND * time_rank + jnp.arange(BAND, dtype=jnp.int32),
@@ -97,7 +97,7 @@
             spec_part = piece[: BAND + 1]
             scale_low = piece[BAND + 1, :, 0][None, :, None, :]
             scale_high = piece[BAND + 1, :, 1][None, :, None, :]
-            conj_sign = jnp.asarray([1.0, -1.0], jnp.float32)[None, None, :, None]
+            conj_sign = (1 - 2 * lax.iota(jnp.int32, 2)).astype(jnp.float32)[None, None, :, None]
             mirrored = spec_part[1:BAND][::-1, :, :, ::-1] * conj_sign
             high = jnp.concatenate([spec_part[BAND:], mirrored])
             return jnp.concatenate([spec_part[:BAND] * scale_low, high * scale_high])

time: 72.5 us -> 74.3 us (1.025); the launches traced: 71.1 us -> 73.7 us
  waiting for transfers between devices: 17.5 us -> 20.5 us
    ppermute x3, waiting for transfers between devices: 11.7 us -> 14.7 us  [passed_along(): return lax.ppermute(block, axis, route)]
    unnamed x17 -> x13, local copies, waits for them, and re-layouts: 2.86 us -> 2.85 us
  transfers between devices with their start and end apart: 5 -> 5, of which waited for: 3 -> 4; matrix products, arithmetic and copies ran while one was open for 8% -> 7% of each run, Pallas kernels for 0% -> 0%
where the time goes in v2:
time: 74.3 us; the launch traced here: 73.7 us
  waiting for transfers between devices  20.5 us (28%)
  between operations  12.6 us (17%)
  starting transfers between devices  11.4 us (15%)
  other arithmetic  9.12 us (12%)
  local copies, waits for them, and re-layouts  8.13 us (11%)
  blocking collectives  6.67 us (9%)
  matrix products  5.25 us (7%)
    ppermute x3, waiting for transfers between devices, passed_along(): return lax.ppermute(block, axis, route)  14.7 us
    all_to_all x1, blocking collectives, local(): lax.all_to_all(lag_block, 'tm', split_axis=0, concat_axis=0, tiled=True)  6.67 us
    all_to_all x1, waiting for transfers between devices, local(): lax.all_to_all(twisted, 'tm', split_axis=0, concat_axis=3, tiled=True)  5.84 us
    ppermute x3, starting transfers between devices, passed_along(): return lax.ppermute(block, axis, route)  4.69 us
    dot_general x3, matrix products, matmul(): jnp.dot(left_mat, right_mat, precision=highest, preferred_element_type=jn...  4.32 us
    all_to_all x1, starting transfers between devices, local(): lax.all_to_all(twisted, 'tm', split_axis=0, concat_axis=3, tiled=True)  3.4 us
    all_to_all x1, starting transfers between devices, local(): lax.all_to_all(arranged, 'tm', split_axis=2, concat_axis=0, tiled=True)  3.32 us
    unnamed x13, local copies, waits for them, and re-layouts  2.85 us
  transfers between devices with their start and end apart: 5, of which 4 were waited for; matrix products, arithmetic and copies ran while one was open for 7% of the time, Pallas kernels for 0%

profile of v2, /device:TPU:2, one launch (start us, length us, event | category | flops | bytes accessed | tf_op | source)
XLA Modules:
  0.0 73.7 jit_solution(5561566885266259954)
XLA Ops:
  0.0 0.0 copy-start
  0.0 1.3 %reduce.1 = f32[2,16384]{1,0:T(2,128)S(1)} reduce(f32[2,1,16384]{2,1,0:T(1,128)} %param.3, f32[]{:T(128)} %constant.136), dimensions={1}, to_apply=%param.3.reduce_sub_computation | reduce | bytes 262148 | tf_op args[0]
  1.3 0.1 copy.47
  1.5 0.9 %reshape.339 = f32[4,1,8192]{2,1,0:T(1,128)} reshape(f32[256,2,64]{2,1,0:T(2,128)S(1)} %bitcast.123) | data formatting | bytes 262144
  2.4 3.3 %all-to-all-start = ((f32[4,1,8192]{2,1,0:T(1,128)}), f32[4,1,8192]{2,1,0:T(1,128)S(1)}, u32[]{:S(2)}, u32[]{:S(2)}) async-start(f32[4,1,8192]{2,1,0:T(1,128)} %reshape.339), calls=%async_computation | async-start | bytes 262144 | tf_op jit(solution)/shard_map/all_to_all | solution.py:46
  5.7 1.0 %fusion.31 = (f32[256,256]{0,1:T(8,128)S(1)}, f32[256,256]{0,1:T(8,128)S(1)}) fusion(), kind=kLoop, calls=%fused_computation.80 | loop fusion | flops 917504 | bytes 524288 | tf_op jit(solution)/shard_map/sin | solution.py:28
  6.8 1.0 %fusion.35 = f32[256,256]{0,1:T(8,128)S(1)} fusion(), kind=kLoop, calls=%fused_computation.87 | loop fusion | flops 983040 | bytes 262144 | tf_op jit(solution)/shard_map/neg | solution.py:80
  7.8 0.0 copy-done
  7.8 0.7 fusion.66
  16.1 1.0 %fusion.33 = (f32[256,256]{0,1:T(8,128)S(1)}, f32[256,256]{0,1:T(8,128)S(1)}) fusion(s32[256]{0:T(256)S(1)} %compare_select_fusion.1), kind=kLoop, calls=%fused_computation.82 | loop fusion | flops 983040 | bytes 525312 | tf_op jit(solution)/shard_map/cos | solution.py:28
  17.1 0.3 fusion.48
  17.5 0.1 pad_add_fusion.1
  17.6 0.3 fusion.46
  22.3 0.1 pad_add_fusion
  22.4 0.1 fusion.11
  22.5 0.0 all-to-all-done
  22.5 0.5 broadcast.457
  23.1 1.0 %reduce.2 = f32[4,8192]{1,0:T(4,128)S(1)} reduce(f32[4,1,8192]{2,1,0:T(1,128)S(1)} %all-to-all-done, f32[]{:T(128)} %broadcast.457), dimensions={1}, to_apply=%all_to_all.25.reduce_sub_computation | reduce | bytes 262148 | tf_op jit(solution)/shard_map/all_to_all | solution.py:46
  24.0 0.2 reshape.340
  24.3 0.2 copy.63
  24.4 0.2 copy.49
  24.6 0.2 reshape.329
  24.8 0.5 fusion.14
  25.4 0.3 copy.50
  25.7 1.3 %reshape.341 = f32[4,1,16384]{2,1,0:T(1,128)} reshape(f32[256,2,2,64]{3,2,1,0:T(2,128)S(1)} %copy.50) | data formatting | bytes 524288
  27.0 3.4 %all-to-all-start.1 = ((f32[4,1,16384]{2,1,0:T(1,128)}), f32[4,1,16384]{2,1,0:T(1,128)S(1)}, u32[]{:S(2)}, u32[]{:S(2)}) async-start(f32[4,1,16384]{2,1,0:T(1,128)} %reshape.341), calls=%async_computation.1 | async-start | bytes 524288 | tf_op jit(solution)/shard_map/all_to_all | solution.py:77
  30.4 0.1 fusion.54
  30.5 5.8 %all-to-all-done.1 = f32[4,1,16384]{2,1,0:T(1,128)S(1)} async-done(((f32[4,1,16384]{2,1,0:T(1,128)}), f32[4,1,16384]{2,1,0:T(1,128)S(1)}, u32[]{:S(2)}, u32[]{:S(2)}) %all-to-all-start.1) | async-done | bytes 262176 | tf_op jit(solution)/shard_map/all_to_all | solution.py:77
  36.4 1.4 %reduce.3 = f32[4,16384]{1,0:T(4,128)S(1)} reduce(f32[4,1,16384]{2,1,0:T(1,128)S(1)} %all-to-all-done.1, f32[]{:T(128)} %broadcast.457), dimensions={1}, to_apply=%all_to_all.28.reduce_sub_computation | reduce | bytes 524292 | tf_op jit(solution)/shard_map/all_to_all | solution.py:77
  37.7 0.4 reshape.342
  38.2 0.3 copy.83
  38.5 0.3 reshape.330
  38.8 1.2 %fusion.9 = f32[128,512]{1,0:T(8,128)S(1)} fusion(f32[128,512]{1,0:T(8,128)S(1)} %reshape.330, f32[256,256]{0,1:T(8,128)S(1)} %get-tuple-element.54, f32[256,256]{0,1:T(8,128)S(1)} %get-tuple-element.53, f32[256,256]{0,1:T(8,128)S(1)} %fusion.35), kind=kOutput, calls=%fused_computation.15 | convolution fusion | flops 403439616 | bytes 1310720 | tf_op jit(solution)/shard_map/dot_general | solution.py:32
  40.0 0.2 reshape.332
  40.2 0.3 fusion.34
  40.5 0.1 slice.132
  40.7 1.9 %collective-permute-start = (f32[34,2,2,256]{3,0,2,1:T(8,128)S(1)}, f32[34,2,2,256]{3,0,2,1:T(8,128)S(1)}, u32[]{:S(2)}, u32[]{:S(2)}) collective-permute-start(f32[34,2,2,256]{3,0,2,1:T(8,128)S(1)} %pad_maximum_fusion.9), channel_id=1, source_target_pairs={{4,0},{8,4},{12,8},{16,12},{20,16},{24,20},{28,24},{5,1},{9,5},{13... | collective-permute-start | bytes 417800 | tf_op jit(solution)/shard_map/ppermute | solution.py:22
  42.6 1.3 %collective-permute-start.1 = (f32[34,2,2,256]{3,0,2,1:T(8,128)S(1)}, f32[34,2,2,256]{3,0,2,1:T(8,128)S(1)}, u32[]{:S(2)}, u32[]{:S(2)}) collective-permute-start(f32[34,2,2,256]{3,0,2,1:T(8,128)S(1)} %pad_maximum_fusion.9), channel_id=1, source_target_pairs={{8,0},{12,4},{16,8},{20,12},{24,16},{28,20},{9,1},{13,5},{17,9},{2... | collective-permute-start | bytes 417800 | tf_op jit(solution)/shard_map/ppermute | solution.py:22
  43.9 1.5 %collective-permute-start.2 = (f32[34,2,2,256]{3,0,2,1:T(8,128)S(1)}, f32[34,2,2,256]{3,0,2,1:T(8,128)S(1)}, u32[]{:S(2)}, u32[]{:S(2)}) collective-permute-start(f32[34,2,2,256]{3,0,2,1:T(8,128)S(1)} %pad_maximum_fusion.9), channel_id=1, source_target_pairs={{12,0},{16,4},{20,8},{24,12},{28,16},{13,1},{17,5},{21,9},{25,13},... | collective-permute-start | bytes 417800 | tf_op jit(solution)/shard_map/ppermute | solution.py:22
  45.4 0.2 reshape.331
  45.6 0.1 copy_multiply_fusion
  45.6 4.9 %collective-permute-done = f32[34,2,2,256]{3,0,2,1:T(8,128)S(1)} collective-permute-done((f32[34,2,2,256]{3,0,2,1:T(8,128)S(1)}, f32[34,2,2,256]{3,0,2,1:T(8,128)S(1)}, u32[]{:S(2)}, u32[]{:S(2)}) %collective-permute-start) | collective-permute-done | bytes 139296 | tf_op jit(solution)/shard_map/ppermute | solution.py:22
  50.5 1.1 %collective-permute-done.1 = f32[34,2,2,256]{3,0,2,1:T(8,128)S(1)} collective-permute-done((f32[34,2,2,256]{3,0,2,1:T(8,128)S(1)}, f32[34,2,2,256]{3,0,2,1:T(8,128)S(1)}, u32[]{:S(2)}, u32[]{:S(2)}) %collective-permute-start.1) | collective-permute-done | bytes 139296 | tf_op jit(solution)/shard_map/ppermute | solution.py:22
  51.7 0.3 rev.10
  51.9 8.7 %collective-permute-done.2 = f32[34,2,2,256]{3,0,2,1:T(8,128)S(1)} collective-permute-done((f32[34,2,2,256]{3,0,2,1:T(8,128)S(1)}, f32[34,2,2,256]{3,0,2,1:T(8,128)S(1)}, u32[]{:S(2)}, u32[]{:S(2)}) %collective-permute-start.2) | collective-permute-done | bytes 139296 | tf_op jit(solution)/shard_map/ppermute | solution.py:22
  60.7 0.3 rev.11
  61.0 0.3 rev.9
  61.3 0.1 broadcast_multiply_fusion.2
  61.7 0.1 pad_maximum_fusion.5
  61.8 0.2 dynamic-slice_bitcast_fusion.5
  62.0 0.1 pad_maximum_fusion.6
  62.0 0.1 slice_bitcast_fusion.5
  62.1 0.1 pad_maximum_fusion.7
  62.2 0.1 slice_bitcast_fusion.4
  62.3 0.2 multiply_add_fusion.1
  62.5 2.7 %fusion = f32[3,64,2,2,2,256]{5,1,4,3,2,0:T(8,128)S(1)} fusion(f32[2,256,512,1,1,1]{2,1,0,5,4,3:T(8,128)S(1)} %bitcast.120, f32[3,64,2,2,256]{4,1,3,2,0:T(8,128)S(1)} %get-tuple-element.8, f32[3,64,2,2,256]{4,1,3,2,0:T(8,128)S(1)} %get-tuple-element.7), kind=kOutput, calls=%fused_computation.1 | convolution fusion | flops 2416312320 | bytes 4194304 | tf_op jit(solution)/shard_map/dot_general | solution.py:32
  65.2 0.2 multiply_subtract_fusion
  65.4 0.9 %fusion.7 = f32[4,3,2,2,2,256]{5,0,4,3,2,1:T(4,128)S(1)} fusion(f32[3,64,2,2,256]{4,1,3,2,0:T(8,128)S(1)} %get-tuple-element.6, f32[3,64,2,2,256]{4,1,3,2,0:T(8,128)S(1)} %get-tuple-element.5, f32[3]{0:T(128)S(1)} %compare_select_fusion, f32[4,2,64]{2,0,1:T(4,128)S(1)} %get-tuple-element.32, f32[4,2,64]{2,0,1:T(4,128)S(1)} %get-tuple-element.31), kind=kOutput, calls=%fused_computation.13 | convolution fusion | flops 38167552 | bytes 1675276 | tf_op jit(solution)/shard_map/dwp,spijm->dsijwm/dot_general | solution.py:152
  66.3 0.1 copy.58
  66.4 6.7 %all_to_all.35 = f32[4,3,2,2,2,256]{5,4,3,2,1,0:T(2,128)S(1)} all-to-all(f32[4,3,2,2,2,256]{5,4,3,2,1,0:T(2,128)S(1)} %copy.58), channel_id=1, replica_groups=mesh['sta'=8,'tm'=4] {'tm'}, dimensions={0} | all-to-all | bytes 196608 | tf_op jit(solution)/shard_map/all_to_all | solution.py:160
  73.1 0.6 reshape.333
  (43 shorter events, 0.5 us)
Async XLA Ops:
  0.0 7.8 %copy-start = (s32[3,2]{0,1:T(2,128)S(1)}, s32[3,2]{0,1:T(2,128)}, u32[]{:S(2)}) copy-start(s32[3,2]{0,1:T(2,128)} %param.4) | copy-start | bytes 76
  2.4 20.2 %all-to-all-start = ((f32[4,1,8192]{2,1,0:T(1,128)}), f32[4,1,8192]{2,1,0:T(1,128)S(1)}, u32[]{:S(2)}, u32[]{:S(2)}) async-start(f32[4,1,8192]{2,1,0:T(1,128)} %reshape.339), calls=%async_computation | async-start | bytes 262144 | tf_op jit(solution)/shard_map/all_to_all | solution.py:46
  27.0 9.4 %all-to-all-start.1 = ((f32[4,1,16384]{2,1,0:T(1,128)}), f32[4,1,16384]{2,1,0:T(1,128)S(1)}, u32[]{:S(2)}, u32[]{:S(2)}) async-start(f32[4,1,16384]{2,1,0:T(1,128)} %reshape.341), calls=%async_computation.1 | async-start | bytes 524288 | tf_op jit(solution)/shard_map/all_to_all | solution.py:77
  40.7 9.9 %collective-permute-start = (f32[34,2,2,256]{3,0,2,1:T(8,128)S(1)}, f32[34,2,2,256]{3,0,2,1:T(8,128)S(1)}, u32[]{:S(2)}, u32[]{:S(2)}) collective-permute-start(f32[34,2,2,256]{3,0,2,1:T(8,128)S(1)} %pad_maximum_fusion.9), channel_id=1, source_target_pairs={{4,0},{8,4},{12,8},{16,12},{20,16},{24,20},{28,24},{5,1},{9,5},{13... | collective-permute-start | bytes 417800 | tf_op jit(solution)/shard_map/ppermute | solution.py:22
  42.6 9.0 %collective-permute-start.1 = (f32[34,2,2,256]{3,0,2,1:T(8,128)S(1)}, f32[34,2,2,256]{3,0,2,1:T(8,128)S(1)}, u32[]{:S(2)}, u32[]{:S(2)}) collective-permute-start(f32[34,2,2,256]{3,0,2,1:T(8,128)S(1)} %pad_maximum_fusion.9), channel_id=1, source_target_pairs={{8,0},{12,4},{16,8},{20,12},{24,16},{28,20},{9,1},{13,5},{17,9},{2... | collective-permute-start | bytes 417800 | tf_op jit(solution)/shard_map/ppermute | solution.py:22
  43.9 16.7 %collective-permute-start.2 = (f32[34,2,2,256]{3,0,2,1:T(8,128)S(1)}, f32[34,2,2,256]{3,0,2,1:T(8,128)S(1)}, u32[]{:S(2)}, u32[]{:S(2)}) collective-permute-start(f32[34,2,2,256]{3,0,2,1:T(8,128)S(1)} %pad_maximum_fusion.9), channel_id=1, source_target_pairs={{12,0},{16,4},{20,8},{24,12},{28,16},{13,1},{17,5},{21,9},{25,13},... | collective-permute-start | bytes 417800 | tf_op jit(solution)/shard_map/ppermute | solution.py:22

commit v3 on v2

--- a/solution.py
+++ b/solution.py
@@ -48,13 +48,6 @@
     index_b = jnp.arange(factor_b, dtype=jnp.int32)
     paired = rows_local == 2 * BAND and factor_a == 2 * BAND * time_devices
     if paired:
-        owner_of_row = index_a // rows_local
-        place_in_row = index_a % rows_local
-        k1_order = jnp.where(
-            place_in_row < BAND,
-            BAND * owner_of_row + place_in_row,
-            factor_a - BAND * (owner_of_row + 2) + place_in_row,
-        )
         k1_ids = jnp.concatenate(
             [
                 BAND * time_rank + jnp.arange(BAND, dtype=jnp.int32),
@@ -62,18 +55,20 @@
             ]
         )
     else:
-        k1_order = index_a
         k1_ids = time_rank * rows_local + jnp.arange(rows_local, dtype=jnp.int32)
-    cosine_a, sine_a = angles(k1_order, index_a, factor_a)
+    cosine_a, sine_a = angles(index_a, index_a, factor_a)
     flat_rows = spread.reshape(factor_a, series * cols_local)
     both_a = jnp.concatenate([cosine_a, -sine_a], axis=0)
     section = matmul(both_a, flat_rows).reshape(2, factor_a, series, cols_local)
     section_real, section_imag = section[0], section[1]
     col_global = time_rank * cols_local + jnp.arange(cols_local, dtype=jnp.int32)
-    cosine_t, sine_t = angles(k1_order, col_global, SAMPLES)
+    cosine_t, sine_t = angles(index_a, col_global, SAMPLES)
     twisted_real = section_real * cosine_t[:, None, :] + section_imag * sine_t[:, None, :]
     twisted_imag = section_imag * cosine_t[:, None, :] - section_real * sine_t[:, None, :]
     twisted = jnp.stack([twisted_real, twisted_imag], axis=2)
+    if paired:
+        bands = twisted.reshape(2, time_devices, BAND, series, 2, cols_local)
+        twisted = jnp.stack([bands[0], bands[1][::-1]], axis=1).reshape(twisted.shape)
     moved = lax.all_to_all(twisted, "tm", split_axis=0, concat_axis=3, tiled=True)
     cosine_b, sine_b = angles(index_b, index_b, factor_b)
     forward_b = jnp.concatenate(

time: 74.3 us -> 73.7 us (level)
  other arithmetic: 9.12 us -> 8.35 us
    cos x4 -> x3, other arithmetic: 1.85 us -> 1 us  [angles(): return (jnp.cos(radians), jnp.sin(radians))]
where the time goes in v3:
time: 73.7 us; the launch traced here: 73.1 us
  waiting for transfers between devices  20.2 us (27%)
  between operations  12.7 us (17%)
  starting transfers between devices  11.4 us (15%)
  local copies, waits for them, and re-layouts  8.52 us (12%)
  other arithmetic  8.35 us (11%)
  blocking collectives  6.67 us (9%)
  matrix products  5.25 us (7%)
    ppermute x3, waiting for transfers between devices, passed_along(): return lax.ppermute(block, axis, route)  14.4 us
    all_to_all x1, blocking collectives, local(): lax.all_to_all(lag_block, 'tm', split_axis=0, concat_axis=0, tiled=True)  6.67 us
    all_to_all x1, waiting for transfers between devices, local(): lax.all_to_all(twisted, 'tm', split_axis=0, concat_axis=3, tiled=True)  5.84 us
    ppermute x3, starting transfers between devices, passed_along(): return lax.ppermute(block, axis, route)  4.69 us
    dot_general x3, matrix products, matmul(): jnp.dot(left_mat, right_mat, precision=highest, preferred_element_type=jn...  4.32 us
    all_to_all x1, starting transfers between devices, local(): lax.all_to_all(twisted, 'tm', split_axis=0, concat_axis=3, tiled=True)  3.4 us
    all_to_all x1, starting transfers between devices, local(): lax.all_to_all(arranged, 'tm', split_axis=2, concat_axis=0, tiled=True)  3.32 us
    unnamed x13, local copies, waits for them, and re-layouts  2.85 us
  transfers between devices with their start and end apart: 5, of which 4 were waited for; matrix products, arithmetic and copies ran while one was open for 7% of the time, Pallas kernels for 0%

profile of v3, /device:TPU:2, one launch (start us, length us, event | category | flops | bytes accessed | tf_op | source)
XLA Modules:
  0.0 73.1 jit_solution(14005607098436239)
XLA Ops:
  0.0 0.0 copy-start
  0.0 1.3 %reduce.1 = f32[2,16384]{1,0:T(2,128)S(1)} reduce(f32[2,1,16384]{2,1,0:T(1,128)} %param.3, f32[]{:T(128)} %constant.104), dimensions={1}, to_apply=%param.3.reduce_sub_computation | reduce | bytes 262148 | tf_op args[0]
  1.3 0.1 copy.40
  1.5 0.9 %reshape.307 = f32[4,1,8192]{2,1,0:T(1,128)} reshape(f32[256,2,64]{2,1,0:T(2,128)S(1)} %bitcast.128) | data formatting | bytes 262144
  2.4 3.3 %all-to-all-start = ((f32[4,1,8192]{2,1,0:T(1,128)}), f32[4,1,8192]{2,1,0:T(1,128)S(1)}, u32[]{:S(2)}, u32[]{:S(2)}) async-start(f32[4,1,8192]{2,1,0:T(1,128)} %reshape.307), calls=%async_computation | async-start | bytes 262144 | tf_op jit(solution)/shard_map/all_to_all | solution.py:46
  5.7 1.0 %fusion.31 = (f32[256,256]{0,1:T(8,128)S(1)}, f32[256,256]{0,1:T(8,128)S(1)}) fusion(), kind=kLoop, calls=%fused_computation.83 | loop fusion | flops 917504 | bytes 524288 | tf_op jit(solution)/shard_map/sin | solution.py:28
  6.7 1.0 %fusion.35 = f32[256,256]{0,1:T(8,128)S(1)} fusion(), kind=kLoop, calls=%fused_computation.87 | loop fusion | flops 983040 | bytes 262144 | tf_op jit(solution)/shard_map/neg | solution.py:61
  7.8 0.0 copy-done
  7.8 0.7 fusion.61
  16.1 0.5 fusion.42
  16.6 0.1 pad_add_fusion.1
  16.7 0.3 fusion.45
  21.5 0.1 pad_add_fusion
  21.5 0.1 fusion.11
  21.7 0.0 all-to-all-done
  21.7 0.5 broadcast.355
  22.2 1.0 %reduce.2 = f32[4,8192]{1,0:T(4,128)S(1)} reduce(f32[4,1,8192]{2,1,0:T(1,128)S(1)} %all-to-all-done, f32[]{:T(128)} %broadcast.355), dimensions={1}, to_apply=%all_to_all.25.reduce_sub_computation | reduce | bytes 262148 | tf_op jit(solution)/shard_map/all_to_all | solution.py:46
  23.2 0.2 reshape.308
  23.4 0.2 copy.60
  23.6 0.2 copy.42
  23.8 0.2 reshape.296
  24.0 0.5 fusion.14
  24.5 0.1 copy.43
  24.6 0.1 copy.44
  24.7 0.1 multiply_add_fusion.2
  24.9 0.1 pad_maximum_fusion.8
  25.0 0.4 copy.48
  25.4 1.3 %reshape.309 = f32[4,1,16384]{2,1,0:T(1,128)} reshape(f32[256,2,2,64]{3,2,1,0:T(2,128)S(1)} %copy.48) | data formatting | bytes 524288
  26.6 3.4 %all-to-all-start.1 = ((f32[4,1,16384]{2,1,0:T(1,128)}), f32[4,1,16384]{2,1,0:T(1,128)S(1)}, u32[]{:S(2)}, u32[]{:S(2)}) async-start(f32[4,1,16384]{2,1,0:T(1,128)} %reshape.309), calls=%async_computation.1 | async-start | bytes 524288 | tf_op jit(solution)/shard_map/all_to_all | solution.py:72
  30.0 0.1 fusion.51
  30.2 5.8 %all-to-all-done.1 = f32[4,1,16384]{2,1,0:T(1,128)S(1)} async-done(((f32[4,1,16384]{2,1,0:T(1,128)}), f32[4,1,16384]{2,1,0:T(1,128)S(1)}, u32[]{:S(2)}, u32[]{:S(2)}) %all-to-all-start.1) | async-done | bytes 262176 | tf_op jit(solution)/shard_map/all_to_all | solution.py:72
  36.0 1.4 %reduce.3 = f32[4,16384]{1,0:T(4,128)S(1)} reduce(f32[4,1,16384]{2,1,0:T(1,128)S(1)} %all-to-all-done.1, f32[]{:T(128)} %broadcast.355), dimensions={1}, to_apply=%all_to_all.28.reduce_sub_computation | reduce | bytes 524292 | tf_op jit(solution)/shard_map/all_to_all | solution.py:72
  37.4 0.4 reshape.310
  37.8 0.3 copy.78
  38.2 0.3 reshape.298
  38.5 1.2 %fusion.9 = f32[128,512]{1,0:T(8,128)S(1)} fusion(f32[128,512]{1,0:T(8,128)S(1)} %reshape.298, f32[256,256]{0,1:T(8,128)S(1)} %get-tuple-element.54, f32[256,256]{0,1:T(8,128)S(1)} %get-tuple-element.53, f32[256,256]{0,1:T(8,128)S(1)} %fusion.35), kind=kOutput, calls=%fused_computation.15 | convolution fusion | flops 403439616 | bytes 1310720 | tf_op jit(solution)/shard_map/dot_general | solution.py:32
  39.7 0.2 reshape.300
  39.9 0.3 fusion.34
  40.2 0.1 slice.142
  40.3 1.9 %collective-permute-start = (f32[34,2,2,256]{3,0,2,1:T(8,128)S(1)}, f32[34,2,2,256]{3,0,2,1:T(8,128)S(1)}, u32[]{:S(2)}, u32[]{:S(2)}) collective-permute-start(f32[34,2,2,256]{3,0,2,1:T(8,128)S(1)} %pad_maximum_fusion.10), channel_id=1, source_target_pairs={{4,0},{8,4},{12,8},{16,12},{20,16},{24,20},{28,24},{5,1},{9,5},{13... | collective-permute-start | bytes 417800 | tf_op jit(solution)/shard_map/ppermute | solution.py:22
  42.3 1.3 %collective-permute-start.1 = (f32[34,2,2,256]{3,0,2,1:T(8,128)S(1)}, f32[34,2,2,256]{3,0,2,1:T(8,128)S(1)}, u32[]{:S(2)}, u32[]{:S(2)}) collective-permute-start(f32[34,2,2,256]{3,0,2,1:T(8,128)S(1)} %pad_maximum_fusion.10), channel_id=1, source_target_pairs={{8,0},{12,4},{16,8},{20,12},{24,16},{28,20},{9,1},{13,5},{17,9},{2... | collective-permute-start | bytes 417800 | tf_op jit(solution)/shard_map/ppermute | solution.py:22
  43.6 1.5 %collective-permute-start.2 = (f32[34,2,2,256]{3,0,2,1:T(8,128)S(1)}, f32[34,2,2,256]{3,0,2,1:T(8,128)S(1)}, u32[]{:S(2)}, u32[]{:S(2)}) collective-permute-start(f32[34,2,2,256]{3,0,2,1:T(8,128)S(1)} %pad_maximum_fusion.10), channel_id=1, source_target_pairs={{12,0},{16,4},{20,8},{24,12},{28,16},{13,1},{17,5},{21,9},{25,13},... | collective-permute-start | bytes 417800 | tf_op jit(solution)/shard_map/ppermute | solution.py:22
  45.0 0.2 reshape.299
  45.2 0.1 copy_multiply_fusion
  45.3 4.9 %collective-permute-done = f32[34,2,2,256]{3,0,2,1:T(8,128)S(1)} collective-permute-done((f32[34,2,2,256]{3,0,2,1:T(8,128)S(1)}, f32[34,2,2,256]{3,0,2,1:T(8,128)S(1)}, u32[]{:S(2)}, u32[]{:S(2)}) %collective-permute-start) | collective-permute-done | bytes 139296 | tf_op jit(solution)/shard_map/ppermute | solution.py:22
  50.2 0.3 rev.13
  50.5 0.8 %collective-permute-done.1 = f32[34,2,2,256]{3,0,2,1:T(8,128)S(1)} collective-permute-done((f32[34,2,2,256]{3,0,2,1:T(8,128)S(1)}, f32[34,2,2,256]{3,0,2,1:T(8,128)S(1)}, u32[]{:S(2)}, u32[]{:S(2)}) %collective-permute-start.1) | collective-permute-done | bytes 139296 | tf_op jit(solution)/shard_map/ppermute | solution.py:22
  51.3 0.3 rev.14
  51.6 8.7 %collective-permute-done.2 = f32[34,2,2,256]{3,0,2,1:T(8,128)S(1)} collective-permute-done((f32[34,2,2,256]{3,0,2,1:T(8,128)S(1)}, f32[34,2,2,256]{3,0,2,1:T(8,128)S(1)}, u32[]{:S(2)}, u32[]{:S(2)}) %collective-permute-start.2) | collective-permute-done | bytes 139296 | tf_op jit(solution)/shard_map/ppermute | solution.py:22
  60.3 0.3 rev.15
  60.7 0.1 broadcast_multiply_fusion.2
  61.1 0.1 pad_maximum_fusion.5
  61.2 0.2 dynamic-slice_bitcast_fusion.5
  61.3 0.1 pad_maximum_fusion.6
  61.4 0.1 slice_bitcast_fusion.5
  61.5 0.1 pad_maximum_fusion.7
  61.5 0.1 slice_bitcast_fusion.4
  61.6 0.2 multiply_add_fusion.1
  61.8 2.7 %fusion = f32[3,64,2,2,2,256]{5,1,4,3,2,0:T(8,128)S(1)} fusion(f32[2,256,512,1,1,1]{2,1,0,5,4,3:T(8,128)S(1)} %bitcast.124, f32[3,64,2,2,256]{4,1,3,2,0:T(8,128)S(1)} %get-tuple-element.8, f32[3,64,2,2,256]{4,1,3,2,0:T(8,128)S(1)} %get-tuple-element.7), kind=kOutput, calls=%fused_computation.1 | convolution fusion | flops 2416312320 | bytes 4194304 | tf_op jit(solution)/shard_map/dot_general | solution.py:32
  64.5 0.2 multiply_subtract_fusion
  64.7 0.9 %fusion.7 = f32[4,3,2,2,2,256]{5,0,4,3,2,1:T(4,128)S(1)} fusion(f32[3,64,2,2,256]{4,1,3,2,0:T(8,128)S(1)} %get-tuple-element.6, f32[3,64,2,2,256]{4,1,3,2,0:T(8,128)S(1)} %get-tuple-element.5, f32[3]{0:T(128)S(1)} %compare_select_fusion, f32[4,2,64]{2,0,1:T(4,128)S(1)} %get-tuple-element.34, f32[4,2,64]{2,0,1:T(4,128)S(1)} %get-tuple-element.33), kind=kOutput, calls=%fused_computation.13 | convolution fusion | flops 38167552 | bytes 1675276 | tf_op jit(solution)/shard_map/dwp,spijm->dsijwm/dot_general | solution.py:147
  65.7 0.1 copy.55
  65.7 6.7 %all_to_all.35 = f32[4,3,2,2,2,256]{5,4,3,2,1,0:T(2,128)S(1)} all-to-all(f32[4,3,2,2,2,256]{5,4,3,2,1,0:T(2,128)S(1)} %copy.55), channel_id=1, replica_groups=mesh['sta'=8,'tm'=4] {'tm'}, dimensions={0} | all-to-all | bytes 196608 | tf_op jit(solution)/shard_map/all_to_all | solution.py:155
  72.5 0.6 reshape.301
  (43 shorter events, 0.5 us)
Async XLA Ops:
  0.0 7.8 %copy-start = (s32[3,2]{0,1:T(2,128)S(1)}, s32[3,2]{0,1:T(2,128)}, u32[]{:S(2)}) copy-start(s32[3,2]{0,1:T(2,128)} %param.4) | copy-start | bytes 76
  2.4 19.3 %all-to-all-start = ((f32[4,1,8192]{2,1,0:T(1,128)}), f32[4,1,8192]{2,1,0:T(1,128)S(1)}, u32[]{:S(2)}, u32[]{:S(2)}) async-start(f32[4,1,8192]{2,1,0:T(1,128)} %reshape.307), calls=%async_computation | async-start | bytes 262144 | tf_op jit(solution)/shard_map/all_to_all | solution.py:46
  26.6 9.4 %all-to-all-start.1 = ((f32[4,1,16384]{2,1,0:T(1,128)}), f32[4,1,16384]{2,1,0:T(1,128)S(1)}, u32[]{:S(2)}, u32[]{:S(2)}) async-start(f32[4,1,16384]{2,1,0:T(1,128)} %reshape.309), calls=%async_computation.1 | async-start | bytes 524288 | tf_op jit(solution)/shard_map/all_to_all | solution.py:72
  40.3 9.9 %collective-permute-start = (f32[34,2,2,256]{3,0,2,1:T(8,128)S(1)}, f32[34,2,2,256]{3,0,2,1:T(8,128)S(1)}, u32[]{:S(2)}, u32[]{:S(2)}) collective-permute-start(f32[34,2,2,256]{3,0,2,1:T(8,128)S(1)} %pad_maximum_fusion.10), channel_id=1, source_target_pairs={{4,0},{8,4},{12,8},{16,12},{20,16},{24,20},{28,24},{5,1},{9,5},{13... | collective-permute-start | bytes 417800 | tf_op jit(solution)/shard_map/ppermute | solution.py:22
  42.3 9.1 %collective-permute-start.1 = (f32[34,2,2,256]{3,0,2,1:T(8,128)S(1)}, f32[34,2,2,256]{3,0,2,1:T(8,128)S(1)}, u32[]{:S(2)}, u32[]{:S(2)}) collective-permute-start(f32[34,2,2,256]{3,0,2,1:T(8,128)S(1)} %pad_maximum_fusion.10), channel_id=1, source_target_pairs={{8,0},{12,4},{16,8},{20,12},{24,16},{28,20},{9,1},{13,5},{17,9},{2... | collective-permute-start | bytes 417800 | tf_op jit(solution)/shard_map/ppermute | solution.py:22
  43.6 16.8 %collective-permute-start.2 = (f32[34,2,2,256]{3,0,2,1:T(8,128)S(1)}, f32[34,2,2,256]{3,0,2,1:T(8,128)S(1)}, u32[]{:S(2)}, u32[]{:S(2)}) collective-permute-start(f32[34,2,2,256]{3,0,2,1:T(8,128)S(1)} %pad_maximum_fusion.10), channel_id=1, source_target_pairs={{12,0},{16,4},{20,8},{24,12},{28,16},{13,1},{17,5},{21,9},{25,13},... | collective-permute-start | bytes 417800 | tf_op jit(solution)/shard_map/ppermute | solution.py:22

commit v4 on v3

--- a/solution.py
+++ b/solution.py
@@ -89,13 +89,13 @@
         sent = jnp.concatenate([spec.reshape(rows_local, series, 2, factor_b)[: BAND + 1], scale_row])
 
         def rebuilt(piece):
-            spec_part = piece[: BAND + 1]
-            scale_low = piece[BAND + 1, :, 0][None, :, None, :]
-            scale_high = piece[BAND + 1, :, 1][None, :, None, :]
-            conj_sign = (1 - 2 * lax.iota(jnp.int32, 2)).astype(jnp.float32)[None, None, :, None]
-            mirrored = spec_part[1:BAND][::-1, :, :, ::-1] * conj_sign
-            high = jnp.concatenate([spec_part[BAND:], mirrored])
-            return jnp.concatenate([spec_part[:BAND] * scale_low, high * scale_high])
+            spec_part = piece[:, : BAND + 1]
+            scale_low = piece[:, BAND + 1, :, 0][:, None, :, None, :]
+            scale_high = piece[:, BAND + 1, :, 1][:, None, :, None, :]
+            conj_sign = (1 - 2 * lax.iota(jnp.int32, 2)).astype(jnp.float32)[None, None, None, :, None]
+            mirrored = spec_part[:, 1:BAND][:, ::-1, :, :, ::-1] * conj_sign
+            high = jnp.concatenate([spec_part[:, BAND:], mirrored], axis=1)
+            return jnp.concatenate([spec_part[:, :BAND] * scale_low, high * scale_high], axis=1)
 
     else:
         sent = whitened
@@ -103,19 +103,20 @@
         def rebuilt(piece):
             return piece
 
-    pieces = [whitened]
-    for distance in range(1, REACH + 1):
-        pieces.append(rebuilt(passed_along(sent, "sta", -distance)))
-    nearby = jnp.stack(pieces).reshape(REACH + 1, rows_local, stations, hour_count, 2, factor_b)
+    received = jnp.stack([passed_along(sent, "sta", -distance) for distance in range(1, REACH + 1)])
+    nearby = jnp.concatenate([whitened[None], rebuilt(received)]).reshape(REACH + 1, rows_local, stations, hour_count, 2, factor_b)
     slot_total = pair_blocks.shape[0]
     first_off = pair_blocks[:, 0] - owner_id
     second_off = pair_blocks[:, 1] - owner_id
-    left_spec = jnp.stack(
-        [lax.dynamic_index_in_dim(nearby, first_off[s], 0, keepdims=False) for s in range(slot_total)]
-    )
-    right_spec = jnp.stack(
-        [lax.dynamic_index_in_dim(nearby, second_off[s], 0, keepdims=False) for s in range(slot_total)]
-    )
+    def chosen(offsets):
+        pick = offsets.reshape((slot_total,) + (1,) * (nearby.ndim - 1))
+        result = jnp.broadcast_to(nearby[REACH], (slot_total,) + nearby.shape[1:])
+        for distance in range(REACH - 1, -1, -1):
+            result = jnp.where(pick == distance, nearby[distance], result)
+        return result
+
+    left_spec = chosen(first_off)
+    right_spec = chosen(second_off)
     left_real = left_spec[:, :, :, None, :, 0]
     left_imag = left_spec[:, :, :, None, :, 1]
     right_real = right_spec[:, :, None, :, :, 0]
@@ -143,7 +144,7 @@
     )
     turned = jnp.concatenate([turn_real, turn_imag], axis=1)
     scale_out = 1.0 / math.sqrt(SAMPLES * hour_count)
-    live_mask = (jnp.arange(slot_total) < pair_count[0]).astype(jnp.float32) * scale_out
+    live_mask = (jnp.arange(slot_total) < pair_count).astype(jnp.float32) * scale_out
     lag_block = jnp.einsum(
         "dwp,spijm->dsijwm",
         lag_weights,

time: 73.7 us -> 61.8 us (0.84)
  between operations: 12.7 us -> 1.17 us
  other arithmetic: 8.35 us -> 9.35 us
  waiting for transfers between devices: 20.2 us -> 19.4 us
    ppermute x3, waiting for transfers between devices: 14.4 us -> 12.9 us  [passed_along(): return lax.ppermute(block, axis, route)]
    unnamed x13 -> x10, local copies, waits for them, and re-layouts: 2.85 us -> 2.85 us
  transfers between devices with their start and end apart: 5 -> 5, of which waited for: 4 -> 5; matrix products, arithmetic and copies ran while one was open for 7% -> 6% of each run, Pallas kernels for 0% -> 0%
where the time goes in v4:
time: 61.8 us; the launch traced here: 61.4 us
  waiting for transfers between devices  19.4 us (31%)
  starting transfers between devices  11.4 us (18%)
  other arithmetic  9.35 us (15%)
  local copies, waits for them, and re-layouts  8.13 us (13%)
  blocking collectives  6.67 us (11%)
  matrix products  5.25 us (8%)
  between operations  1.17 us (2%)
    ppermute x3, waiting for transfers between devices, passed_along(): return lax.ppermute(block, axis, route)  12.9 us
    all_to_all x1, blocking collectives, local(): lax.all_to_all(lag_block, 'tm', split_axis=0, concat_axis=0, tiled=True)  6.67 us
    all_to_all x1, waiting for transfers between devices, local(): lax.all_to_all(twisted, 'tm', split_axis=0, concat_axis=3, tiled=True)  5.94 us
    ppermute x3, starting transfers between devices, passed_along(): return lax.ppermute(block, axis, route)  4.7 us
    dot_general x3, matrix products, matmul(): jnp.dot(left_mat, right_mat, precision=highest, preferred_element_type=jn...  4.32 us
    all_to_all x1, starting transfers between devices, local(): lax.all_to_all(twisted, 'tm', split_axis=0, concat_axis=3, tiled=True)  3.4 us
    all_to_all x1, starting transfers between devices, local(): lax.all_to_all(arranged, 'tm', split_axis=2, concat_axis=0, tiled=True)  3.32 us
    unnamed x10, local copies, waits for them, and re-layouts  2.85 us
  transfers between devices with their start and end apart: 5, of which 5 were waited for; matrix products, arithmetic and copies ran while one was open for 6% of the time, Pallas kernels for 0%

profile of v4, /device:TPU:2, one launch (start us, length us, event | category | flops | bytes accessed | tf_op | source)
XLA Modules:
  0.0 61.4 jit_solution(1533913714498026500)
XLA Ops:
  0.0 1.3 %reduce.1 = f32[2,16384]{1,0:T(2,128)S(1)} reduce(f32[2,1,16384]{2,1,0:T(1,128)} %param.3, f32[]{:T(128)} %constant.92), dimensions={1}, to_apply=%param.3.reduce_sub_computation | reduce | bytes 262148 | tf_op args[0]
  1.3 0.1 copy.51
  1.5 0.9 %reshape.381 = f32[4,1,8192]{2,1,0:T(1,128)} reshape(f32[256,2,64]{2,1,0:T(2,128)S(1)} %bitcast.122) | data formatting | bytes 262144
  2.4 3.3 %all-to-all-start = ((f32[4,1,8192]{2,1,0:T(1,128)}), f32[4,1,8192]{2,1,0:T(1,128)S(1)}, u32[]{:S(2)}, u32[]{:S(2)}) async-start(f32[4,1,8192]{2,1,0:T(1,128)} %reshape.381), calls=%async_computation | async-start | bytes 262144 | tf_op jit(solution)/shard_map/all_to_all | solution.py:46
  5.7 1.0 %fusion.38 = (f32[256,256]{0,1:T(8,128)S(1)}, f32[256,256]{0,1:T(8,128)S(1)}) fusion(), kind=kLoop, calls=%fused_computation.83 | loop fusion | flops 917504 | bytes 524288 | tf_op jit(solution)/shard_map/sin | solution.py:28
  6.7 1.0 %fusion.42 = f32[256,256]{0,1:T(8,128)S(1)} fusion(), kind=kLoop, calls=%fused_computation.87 | loop fusion | flops 983040 | bytes 262144 | tf_op jit(solution)/shard_map/neg | solution.py:61
  7.8 0.5 fusion.49
  8.3 0.1 pad_add_fusion.1
  8.4 0.3 fusion.52
  8.7 0.1 pad_add_fusion
  8.8 0.1 fusion.58
  9.6 0.1 fusion.11
  9.7 0.5 all-to-all-done
  10.3 0.5 broadcast.556
  10.8 1.0 %reduce.2 = f32[4,8192]{1,0:T(4,128)S(1)} reduce(f32[4,1,8192]{2,1,0:T(1,128)S(1)} %all-to-all-done, f32[]{:T(128)} %broadcast.556), dimensions={1}, to_apply=%all_to_all.25.reduce_sub_computation | reduce | bytes 262148 | tf_op jit(solution)/shard_map/all_to_all | solution.py:46
  11.8 0.2 reshape.382
  12.0 0.2 copy.72
  12.1 0.2 copy.53
  12.4 0.2 reshape.370
  12.5 0.5 fusion.14
  13.0 0.1 copy.54
  13.2 0.1 copy.55
  13.3 0.1 multiply_add_fusion.2
  13.6 0.4 copy.59
  14.0 1.3 %reshape.383 = f32[4,1,16384]{2,1,0:T(1,128)} reshape(f32[256,2,2,64]{3,2,1,0:T(2,128)S(1)} %copy.59) | data formatting | bytes 524288
  15.2 3.4 %all-to-all-start.1 = ((f32[4,1,16384]{2,1,0:T(1,128)}), f32[4,1,16384]{2,1,0:T(1,128)S(1)}, u32[]{:S(2)}, u32[]{:S(2)}) async-start(f32[4,1,16384]{2,1,0:T(1,128)} %reshape.383), calls=%async_computation.1 | async-start | bytes 524288 | tf_op jit(solution)/shard_map/all_to_all | solution.py:72
  18.7 5.9 %all-to-all-done.1 = f32[4,1,16384]{2,1,0:T(1,128)S(1)} async-done(((f32[4,1,16384]{2,1,0:T(1,128)}), f32[4,1,16384]{2,1,0:T(1,128)S(1)}, u32[]{:S(2)}, u32[]{:S(2)}) %all-to-all-start.1) | async-done | bytes 262176 | tf_op jit(solution)/shard_map/all_to_all | solution.py:72
  24.6 1.4 %reduce.3 = f32[4,16384]{1,0:T(4,128)S(1)} reduce(f32[4,1,16384]{2,1,0:T(1,128)S(1)} %all-to-all-done.1, f32[]{:T(128)} %broadcast.556), dimensions={1}, to_apply=%all_to_all.28.reduce_sub_computation | reduce | bytes 524292 | tf_op jit(solution)/shard_map/all_to_all | solution.py:72
  26.0 0.4 reshape.384
  26.4 0.3 copy.82
  26.8 0.3 reshape.372
  27.1 1.2 %fusion.9 = f32[128,512]{1,0:T(8,128)S(1)} fusion(f32[128,512]{1,0:T(8,128)S(1)} %reshape.372, f32[256,256]{0,1:T(8,128)S(1)} %get-tuple-element.41, f32[256,256]{0,1:T(8,128)S(1)} %get-tuple-element.40, f32[256,256]{0,1:T(8,128)S(1)} %fusion.42), kind=kOutput, calls=%fused_computation.15 | convolution fusion | flops 403439616 | bytes 1310720 | tf_op jit(solution)/shard_map/dot_general | solution.py:32
  28.3 0.2 reshape.374
  28.5 0.2 reshape.373
  28.7 0.3 fusion.41
  28.9 0.1 slice.102
  29.1 1.9 %collective-permute-start = (f32[34,2,2,256]{3,2,1,0:T(2,128)S(1)}, f32[34,2,2,256]{3,2,1,0:T(2,128)S(1)}, u32[]{:S(2)}, u32[]{:S(2)}) collective-permute-start(f32[34,2,2,256]{3,2,1,0:T(2,128)S(1)} %constant_dynamic-update-slice_fusion), channel_id=1, source_target_pairs={{4,0},{8,4},{12,8},{16,12},{20,16},{24,20},{28,24},{5,1},{9,5},{13... | collective-permute-start | bytes 417800 | tf_op jit(solution)/shard_map/ppermute | solution.py:22
  31.0 1.3 %collective-permute-start.1 = (f32[34,2,2,256]{3,2,1,0:T(2,128)S(1)}, f32[34,2,2,256]{3,2,1,0:T(2,128)S(1)}, u32[]{:S(2)}, u32[]{:S(2)}) collective-permute-start(f32[34,2,2,256]{3,2,1,0:T(2,128)S(1)} %constant_dynamic-update-slice_fusion), channel_id=1, source_target_pairs={{8,0},{12,4},{16,8},{20,12},{24,16},{28,20},{9,1},{13,5},{17,9},{2... | collective-permute-start | bytes 417800 | tf_op jit(solution)/shard_map/ppermute | solution.py:22
  32.3 1.5 %collective-permute-start.2 = (f32[34,2,2,256]{3,2,1,0:T(2,128)S(1)}, f32[34,2,2,256]{3,2,1,0:T(2,128)S(1)}, u32[]{:S(2)}, u32[]{:S(2)}) collective-permute-start(f32[34,2,2,256]{3,2,1,0:T(2,128)S(1)} %constant_dynamic-update-slice_fusion), channel_id=1, source_target_pairs={{12,0},{16,4},{20,8},{24,12},{28,16},{13,1},{17,5},{21,9},{25,13},... | collective-permute-start | bytes 417800 | tf_op jit(solution)/shard_map/ppermute | solution.py:22
  33.8 0.1 broadcast_multiply_fusion.1
  34.0 0.1 copy.61
  34.0 4.0 %collective-permute-done = f32[34,2,2,256]{3,2,1,0:T(2,128)S(1)} collective-permute-done((f32[34,2,2,256]{3,2,1,0:T(2,128)S(1)}, f32[34,2,2,256]{3,2,1,0:T(2,128)S(1)}, u32[]{:S(2)}, u32[]{:S(2)}) %collective-permute-start) | collective-permute-done | bytes 139296 | tf_op jit(solution)/shard_map/ppermute | solution.py:22
  38.0 1.1 %collective-permute-done.1 = f32[34,2,2,256]{3,2,1,0:T(2,128)S(1)} collective-permute-done((f32[34,2,2,256]{3,2,1,0:T(2,128)S(1)}, f32[34,2,2,256]{3,2,1,0:T(2,128)S(1)}, u32[]{:S(2)}, u32[]{:S(2)}) %collective-permute-start.1) | collective-permute-done | bytes 139296 | tf_op jit(solution)/shard_map/ppermute | solution.py:22
  39.1 7.8 %collective-permute-done.2 = f32[34,2,2,256]{3,2,1,0:T(2,128)S(1)} collective-permute-done((f32[34,2,2,256]{3,2,1,0:T(2,128)S(1)}, f32[34,2,2,256]{3,2,1,0:T(2,128)S(1)}, u32[]{:S(2)}, u32[]{:S(2)}) %collective-permute-start.2) | collective-permute-done | bytes 139296 | tf_op jit(solution)/shard_map/ppermute | solution.py:22
  47.0 0.2 pad_maximum_fusion.6
  47.2 0.1 slice.126
  47.3 0.1 slice_multiply_fusion
  47.4 1.1 %rev.7 = f32[3,31,2,2,256]{4,3,2,1,0:T(2,128)S(1)} reverse(f32[3,31,2,2,256]{4,3,2,1,0:T(2,128)S(1)} %slice.126), dimensions={1,4} | reverse | bytes 761856 | tf_op jit(solution)/shard_map/rev | solution.py:96
  48.5 0.2 broadcast_multiply_fusion
  48.7 0.2 fusion.19
  48.9 0.4 fusion.30
  49.3 0.1 copy.63
  49.4 0.1 copy.64
  49.4 0.1 copy.65
  49.5 0.3 select_select_fusion.1
  49.8 0.1 slice_bitcast_fusion.5
  49.8 0.1 slice_bitcast_fusion.4
  49.9 0.2 multiply_add_fusion.1
  50.1 2.7 %fusion = f32[3,64,2,2,2,256]{5,1,4,3,2,0:T(8,128)S(1)} fusion(f32[2,256,512,1,1,1]{2,1,0,5,4,3:T(8,128)S(1)} %bitcast.109, f32[3,64,2,2,256]{4,1,3,2,0:T(8,128)S(1)} %get-tuple-element.8, f32[3,64,2,2,256]{4,1,3,2,0:T(8,128)S(1)} %get-tuple-element.7), kind=kOutput, calls=%fused_computation.1 | convolution fusion | flops 2416312320 | bytes 4194304 | tf_op jit(solution)/shard_map/dot_general | solution.py:32
  52.8 0.2 multiply_subtract_fusion
  53.0 0.9 %fusion.7 = f32[4,3,2,2,2,256]{5,0,4,3,2,1:T(4,128)S(1)} fusion(f32[3,64,2,2,256]{4,1,3,2,0:T(8,128)S(1)} %get-tuple-element.6, f32[3,64,2,2,256]{4,1,3,2,0:T(8,128)S(1)} %get-tuple-element.5, f32[3]{0:T(128)S(1)} %compare_select_fusion, f32[4,2,64]{2,0,1:T(4,128)S(1)} %get-tuple-element.29, f32[4,2,64]{2,0,1:T(4,128)S(1)} %get-tuple-element.28), kind=kOutput, calls=%fused_computation.13 | convolution fusion | flops 38167552 | bytes 1675276 | tf_op jit(solution)/shard_map/dwp,spijm->dsijwm/dot_general | solution.py:148
  54.0 0.1 copy.67
  54.0 6.7 %all_to_all.35 = f32[4,3,2,2,2,256]{5,4,3,2,1,0:T(2,128)S(1)} all-to-all(f32[4,3,2,2,2,256]{5,4,3,2,1,0:T(2,128)S(1)} %copy.67), channel_id=1, replica_groups=mesh['sta'=8,'tm'=4] {'tm'}, dimensions={0} | all-to-all | bytes 196608 | tf_op jit(solution)/shard_map/all_to_all | solution.py:156
  60.7 0.6 %reshape.375 = f32[3,2,2,512]{3,2,1,0:T(2,128)} reshape(f32[3,2,2,2,256]{4,3,2,1,0:T(2,128)S(1)} %reduce_sum.20) | data formatting | bytes 49152 | tf_op jit(solution)/shard_map/reshape | solution.py:158
  (23 shorter events, 0.4 us)
Async XLA Ops:
  2.4 7.9 %all-to-all-start = ((f32[4,1,8192]{2,1,0:T(1,128)}), f32[4,1,8192]{2,1,0:T(1,128)S(1)}, u32[]{:S(2)}, u32[]{:S(2)}) async-start(f32[4,1,8192]{2,1,0:T(1,128)} %reshape.381), calls=%async_computation | async-start | bytes 262144 | tf_op jit(solution)/shard_map/all_to_all | solution.py:46
  13.5 5.1 %copy-start = (s32[3,2]{0,1:T(2,128)S(1)}, s32[3,2]{0,1:T(2,128)}, u32[]{:S(2)}) copy-start(s32[3,2]{0,1:T(2,128)} %param.4) | copy-start | bytes 76
  15.2 9.4 %all-to-all-start.1 = ((f32[4,1,16384]{2,1,0:T(1,128)}), f32[4,1,16384]{2,1,0:T(1,128)S(1)}, u32[]{:S(2)}, u32[]{:S(2)}) async-start(f32[4,1,16384]{2,1,0:T(1,128)} %reshape.383), calls=%async_computation.1 | async-start | bytes 524288 | tf_op jit(solution)/shard_map/all_to_all | solution.py:72
  29.1 9.0 %collective-permute-start = (f32[34,2,2,256]{3,2,1,0:T(2,128)S(1)}, f32[34,2,2,256]{3,2,1,0:T(2,128)S(1)}, u32[]{:S(2)}, u32[]{:S(2)}) collective-permute-start(f32[34,2,2,256]{3,2,1,0:T(2,128)S(1)} %constant_dynamic-update-slice_fusion), channel_id=1, source_target_pairs={{4,0},{8,4},{12,8},{16,12},{20,16},{24,20},{28,24},{5,1},{9,5},{13... | collective-permute-start | bytes 417800 | tf_op jit(solution)/shard_map/ppermute | solution.py:22
  31.0 8.1 %collective-permute-start.1 = (f32[34,2,2,256]{3,2,1,0:T(2,128)S(1)}, f32[34,2,2,256]{3,2,1,0:T(2,128)S(1)}, u32[]{:S(2)}, u32[]{:S(2)}) collective-permute-start(f32[34,2,2,256]{3,2,1,0:T(2,128)S(1)} %constant_dynamic-update-slice_fusion), channel_id=1, source_target_pairs={{8,0},{12,4},{16,8},{20,12},{24,16},{28,20},{9,1},{13,5},{17,9},{2... | collective-permute-start | bytes 417800 | tf_op jit(solution)/shard_map/ppermute | solution.py:22
  32.3 14.6 %collective-permute-start.2 = (f32[34,2,2,256]{3,2,1,0:T(2,128)S(1)}, f32[34,2,2,256]{3,2,1,0:T(2,128)S(1)}, u32[]{:S(2)}, u32[]{:S(2)}) collective-permute-start(f32[34,2,2,256]{3,2,1,0:T(2,128)S(1)} %constant_dynamic-update-slice_fusion), channel_id=1, source_target_pairs={{12,0},{16,4},{20,8},{24,12},{28,16},{13,1},{17,5},{21,9},{25,13},... | collective-permute-start | bytes 417800 | tf_op jit(solution)/shard_map/ppermute | solution.py:22

commit v5 on v4

--- a/solution.py
+++ b/solution.py
@@ -68,8 +68,24 @@
     twisted = jnp.stack([twisted_real, twisted_imag], axis=2)
     if paired:
         bands = twisted.reshape(2, time_devices, BAND, series, 2, cols_local)
-        twisted = jnp.stack([bands[0], bands[1][::-1]], axis=1).reshape(twisted.shape)
-    moved = lax.all_to_all(twisted, "tm", split_axis=0, concat_axis=3, tiled=True)
+        grouped = jnp.stack([bands[0], bands[1][::-1]], axis=1)
+        outgoing = grouped.reshape(time_devices, rows_local, series, 2, cols_local)[:, : BAND + 1]
+        incoming = lax.all_to_all(outgoing, "tm", split_axis=0, concat_axis=4, tiled=True).reshape(
+            BAND + 1, series, 2, factor_b
+        )
+        phase_cos, phase_sin = angles(jnp.ones((1,), jnp.int32), index_b, factor_b)
+        source = incoming[1:BAND][::-1]
+        source_real, source_imag = source[:, :, 0], source[:, :, 1]
+        mirror = jnp.stack(
+            [
+                source_real * phase_cos - source_imag * phase_sin,
+                -(source_real * phase_sin + source_imag * phase_cos),
+            ],
+            axis=2,
+        )
+        moved = jnp.concatenate([incoming, mirror])
+    else:
+        moved = lax.all_to_all(twisted, "tm", split_axis=0, concat_axis=3, tiled=True)
     cosine_b, sine_b = angles(index_b, index_b, factor_b)
     forward_b = jnp.concatenate(
         [jnp.concatenate([cosine_b, -sine_b], axis=1), jnp.concatenate([sine_b, cosine_b], axis=1)],

time: 61.8 us -> 59.6 us (0.964)
  waiting for transfers between devices: 19.4 us -> 17.9 us
  local copies, waits for them, and re-layouts: 8.13 us -> 7.41 us
    all_to_all x1, waiting for transfers between devices: 5.94 us -> 4.6 us  [local(): lax.all_to_all(outgoing, 'tm', split_axis=0, concat_axis=4, tiled=True)]
    unnamed x10 -> x11, local copies, waits for them, and re-layouts: 2.85 us -> 2.34 us
where the time goes in v5:
time: 59.6 us; the launch traced here: 59.1 us
  waiting for transfers between devices  17.9 us (30%)
  starting transfers between devices  11.3 us (19%)
  other arithmetic  9.32 us (16%)
  local copies, waits for them, and re-layouts  7.41 us (12%)
  blocking collectives  6.67 us (11%)
  matrix products  5.25 us (9%)
  between operations  1.22 us (2%)
    ppermute x3, waiting for transfers between devices, passed_along(): return lax.ppermute(block, axis, route)  12.8 us
    all_to_all x1, blocking collectives, local(): lax.all_to_all(lag_block, 'tm', split_axis=0, concat_axis=0, tiled=True)  6.67 us
    ppermute x3, starting transfers between devices, passed_along(): return lax.ppermute(block, axis, route)  4.7 us
    all_to_all x1, waiting for transfers between devices, local(): lax.all_to_all(outgoing, 'tm', split_axis=0, concat_axis=4, tiled=True)  4.6 us
    dot_general x3, matrix products, matmul(): jnp.dot(left_mat, right_mat, precision=highest, preferred_element_type=jn...  4.32 us
    all_to_all x1, starting transfers between devices, local(): lax.all_to_all(outgoing, 'tm', split_axis=0, concat_axis=4, tiled=True)  3.33 us
    all_to_all x1, starting transfers between devices, local(): lax.all_to_all(arranged, 'tm', split_axis=2, concat_axis=0, tiled=True)  3.32 us
    unnamed x11, local copies, waits for them, and re-layouts  2.34 us
  transfers between devices with their start and end apart: 5, of which 5 were waited for; matrix products, arithmetic and copies ran while one was open for 6% of the time, Pallas kernels for 0%

profile of v5, /device:TPU:2, one launch (start us, length us, event | category | flops | bytes accessed | tf_op | source)
XLA Modules:
  0.0 59.1 jit_solution(5792164417694526504)
XLA Ops:
  0.0 1.3 %reduce.1 = f32[2,16384]{1,0:T(2,128)S(1)} reduce(f32[2,1,16384]{2,1,0:T(1,128)} %param.3, f32[]{:T(128)} %constant.102), dimensions={1}, to_apply=%param.3.reduce_sub_computation | reduce | bytes 262148 | tf_op args[0]
  1.3 0.1 copy.60
  1.5 0.9 %reshape.413 = f32[4,1,8192]{2,1,0:T(1,128)} reshape(f32[256,2,64]{2,1,0:T(2,128)S(1)} %bitcast.124) | data formatting | bytes 262144
  2.4 3.3 %all-to-all-start = ((f32[4,1,8192]{2,1,0:T(1,128)}), f32[4,1,8192]{2,1,0:T(1,128)S(1)}, u32[]{:S(2)}, u32[]{:S(2)}) async-start(f32[4,1,8192]{2,1,0:T(1,128)} %reshape.413), calls=%async_computation | async-start | bytes 262144 | tf_op jit(solution)/shard_map/all_to_all | solution.py:46
  5.7 1.0 %fusion.38 = (f32[256,256]{0,1:T(8,128)S(1)}, f32[256,256]{0,1:T(8,128)S(1)}) fusion(), kind=kLoop, calls=%fused_computation.83 | loop fusion | flops 917504 | bytes 524288 | tf_op jit(solution)/shard_map/sin | solution.py:28
  6.7 1.0 %fusion.42 = f32[256,256]{0,1:T(8,128)S(1)} fusion(), kind=kLoop, calls=%fused_computation.87 | loop fusion | flops 983040 | bytes 262144 | tf_op jit(solution)/shard_map/neg | solution.py:61
  7.8 0.5 fusion.49
  8.4 0.1 pad_add_fusion.1
  8.4 0.3 fusion.52
  8.8 0.1 pad_add_fusion
  8.9 0.1 fusion.58
  9.7 0.1 fusion.11
  9.8 0.5 all-to-all-done
  10.3 0.5 broadcast.615
  10.8 1.0 %reduce.2 = f32[4,8192]{1,0:T(4,128)S(1)} reduce(f32[4,1,8192]{2,1,0:T(1,128)S(1)} %all-to-all-done, f32[]{:T(128)} %broadcast.615), dimensions={1}, to_apply=%all_to_all.25.reduce_sub_computation | reduce | bytes 262148 | tf_op jit(solution)/shard_map/all_to_all | solution.py:46
  11.8 0.2 reshape.414
  12.0 0.2 copy.84
  12.2 0.2 copy.62
  12.4 0.2 reshape.400
  12.6 0.5 fusion.14
  13.1 0.1 copy.63
  13.2 0.1 copy.64
  13.3 0.1 multiply_add_fusion.2
  13.6 0.1 copy.68
  13.7 0.9 %reshape.415 = f32[4,1,8448]{2,1,0:T(1,128)} reshape(f32[4,33,2,2,64]{4,3,2,1,0:T(2,128)S(1)} %copy.68) | data formatting | bytes 270336
  14.7 3.3 %all-to-all-start.1 = ((f32[4,1,8448]{2,1,0:T(1,128)}), f32[4,1,8448]{2,1,0:T(1,128)S(1)}, u32[]{:S(2)}, u32[]{:S(2)}) async-start(f32[4,1,8448]{2,1,0:T(1,128)} %reshape.415), calls=%async_computation.1 | async-start | bytes 270336 | tf_op jit(solution)/shard_map/all_to_all | solution.py:73
  18.0 4.6 %all-to-all-done.1 = f32[4,1,8448]{2,1,0:T(1,128)S(1)} async-done(((f32[4,1,8448]{2,1,0:T(1,128)}), f32[4,1,8448]{2,1,0:T(1,128)S(1)}, u32[]{:S(2)}, u32[]{:S(2)}) %all-to-all-start.1) | async-done | bytes 135200 | tf_op jit(solution)/shard_map/all_to_all | solution.py:73
  22.6 1.0 %reduce.3 = f32[4,8448]{1,0:T(4,128)S(1)} reduce(f32[4,1,8448]{2,1,0:T(1,128)S(1)} %all-to-all-done.1, f32[]{:T(128)} %broadcast.615), dimensions={1}, to_apply=%all_to_all.28.reduce_sub_computation | reduce | bytes 270340 | tf_op jit(solution)/shard_map/all_to_all | solution.py:73
  23.6 0.2 reshape.416
  23.9 0.1 copy.69
  24.0 0.1 copy.85
  24.0 0.2 reshape.411
  24.2 0.1 fusion.69
  24.3 0.2 reshape.402
  24.6 0.1 multiply_subtract_fusion.3
  24.7 0.2 maximum_maximum_fusion
  24.9 1.2 %fusion.9 = f32[128,512]{1,0:T(8,128)S(1)} fusion(f32[128,512]{1,0:T(8,128)S(1)} %bitcast.135, f32[256,256]{0,1:T(8,128)S(1)} %get-tuple-element.45, f32[256,256]{0,1:T(8,128)S(1)} %get-tuple-element.44, f32[256,256]{0,1:T(8,128)S(1)} %fusion.42), kind=kOutput, calls=%fused_computation.15 | convolution fusion | flops 403439616 | bytes 1310720 | tf_op jit(solution)/shard_map/dot_general | solution.py:32
  26.1 0.2 reshape.405
  26.3 0.2 reshape.404
  26.5 0.3 fusion.41
  26.8 0.1 slice.130
  26.9 1.9 %collective-permute-start = (f32[34,2,2,256]{3,2,1,0:T(2,128)S(1)}, f32[34,2,2,256]{3,2,1,0:T(2,128)S(1)}, u32[]{:S(2)}, u32[]{:S(2)}) collective-permute-start(f32[34,2,2,256]{3,2,1,0:T(2,128)S(1)} %constant_dynamic-update-slice_fusion), channel_id=1, source_target_pairs={{4,0},{8,4},{12,8},{16,12},{20,16},{24,20},{28,24},{5,1},{9,5},{13... | collective-permute-start | bytes 417800 | tf_op jit(solution)/shard_map/ppermute | solution.py:22
  28.8 1.3 %collective-permute-start.1 = (f32[34,2,2,256]{3,2,1,0:T(2,128)S(1)}, f32[34,2,2,256]{3,2,1,0:T(2,128)S(1)}, u32[]{:S(2)}, u32[]{:S(2)}) collective-permute-start(f32[34,2,2,256]{3,2,1,0:T(2,128)S(1)} %constant_dynamic-update-slice_fusion), channel_id=1, source_target_pairs={{8,0},{12,4},{16,8},{20,12},{24,16},{28,20},{9,1},{13,5},{17,9},{2... | collective-permute-start | bytes 417800 | tf_op jit(solution)/shard_map/ppermute | solution.py:22
  30.1 1.5 %collective-permute-start.2 = (f32[34,2,2,256]{3,2,1,0:T(2,128)S(1)}, f32[34,2,2,256]{3,2,1,0:T(2,128)S(1)}, u32[]{:S(2)}, u32[]{:S(2)}) collective-permute-start(f32[34,2,2,256]{3,2,1,0:T(2,128)S(1)} %constant_dynamic-update-slice_fusion), channel_id=1, source_target_pairs={{12,0},{16,4},{20,8},{24,12},{28,16},{13,1},{17,5},{21,9},{25,13},... | collective-permute-start | bytes 417800 | tf_op jit(solution)/shard_map/ppermute | solution.py:22
  31.6 0.1 broadcast_multiply_fusion.1
  31.9 4.0 %collective-permute-done = f32[34,2,2,256]{3,2,1,0:T(2,128)S(1)} collective-permute-done((f32[34,2,2,256]{3,2,1,0:T(2,128)S(1)}, f32[34,2,2,256]{3,2,1,0:T(2,128)S(1)}, u32[]{:S(2)}, u32[]{:S(2)}) %collective-permute-start) | collective-permute-done | bytes 139296 | tf_op jit(solution)/shard_map/ppermute | solution.py:22
  35.8 1.1 %collective-permute-done.1 = f32[34,2,2,256]{3,2,1,0:T(2,128)S(1)} collective-permute-done((f32[34,2,2,256]{3,2,1,0:T(2,128)S(1)}, f32[34,2,2,256]{3,2,1,0:T(2,128)S(1)}, u32[]{:S(2)}, u32[]{:S(2)}) %collective-permute-start.1) | collective-permute-done | bytes 139296 | tf_op jit(solution)/shard_map/ppermute | solution.py:22
  36.9 7.8 %collective-permute-done.2 = f32[34,2,2,256]{3,2,1,0:T(2,128)S(1)} collective-permute-done((f32[34,2,2,256]{3,2,1,0:T(2,128)S(1)}, f32[34,2,2,256]{3,2,1,0:T(2,128)S(1)}, u32[]{:S(2)}, u32[]{:S(2)}) %collective-permute-start.2) | collective-permute-done | bytes 139296 | tf_op jit(solution)/shard_map/ppermute | solution.py:22
  44.7 0.2 pad_maximum_fusion.6
  44.9 0.1 slice.158
  45.0 0.1 slice_multiply_fusion
  45.2 1.1 %rev.8 = f32[3,31,2,2,256]{4,3,2,1,0:T(2,128)S(1)} reverse(f32[3,31,2,2,256]{4,3,2,1,0:T(2,128)S(1)} %slice.158), dimensions={1,4} | reverse | bytes 761856 | tf_op jit(solution)/shard_map/rev | solution.py:112
  46.3 0.2 broadcast_multiply_fusion
  46.5 0.2 fusion.19
  46.7 0.4 fusion.30
  47.2 0.3 select_select_fusion.1
  47.5 0.1 slice_bitcast_fusion.5
  47.7 0.2 multiply_add_fusion.1
  47.9 2.7 %fusion = f32[3,64,2,2,2,256]{5,1,4,3,2,0:T(8,128)S(1)} fusion(f32[2,256,512,1,1,1]{2,1,0,5,4,3:T(8,128)S(1)} %bitcast.111, f32[3,64,2,2,256]{4,1,3,2,0:T(8,128)S(1)} %get-tuple-element.8, f32[3,64,2,2,256]{4,1,3,2,0:T(8,128)S(1)} %get-tuple-element.7), kind=kOutput, calls=%fused_computation.1 | convolution fusion | flops 2416312320 | bytes 4194304 | tf_op jit(solution)/shard_map/dot_general | solution.py:32
  50.6 0.2 multiply_subtract_fusion
  50.8 0.9 %fusion.7 = f32[4,3,2,2,2,256]{5,0,4,3,2,1:T(4,128)S(1)} fusion(f32[3,64,2,2,256]{4,1,3,2,0:T(8,128)S(1)} %get-tuple-element.6, f32[3,64,2,2,256]{4,1,3,2,0:T(8,128)S(1)} %get-tuple-element.5, f32[3]{0:T(128)S(1)} %compare_select_fusion, f32[4,2,64]{2,0,1:T(4,128)S(1)} %get-tuple-element.33, f32[4,2,64]{2,0,1:T(4,128)S(1)} %get-tuple-element.32), kind=kOutput, calls=%fused_computation.13 | convolution fusion | flops 38167552 | bytes 1675276 | tf_op jit(solution)/shard_map/dwp,spijm->dsijwm/dot_general | solution.py:164
  51.7 0.1 copy.79
  51.8 6.7 %all_to_all.35 = f32[4,3,2,2,2,256]{5,4,3,2,1,0:T(2,128)S(1)} all-to-all(f32[4,3,2,2,2,256]{5,4,3,2,1,0:T(2,128)S(1)} %copy.79), channel_id=1, replica_groups=mesh['sta'=8,'tm'=4] {'tm'}, dimensions={0} | all-to-all | bytes 196608 | tf_op jit(solution)/shard_map/all_to_all | solution.py:172
  58.5 0.6 %reshape.406 = f32[3,2,2,512]{3,2,1,0:T(2,128)} reshape(f32[3,2,2,2,256]{4,3,2,1,0:T(2,128)S(1)} %reduce_sum.20) | data formatting | bytes 49152 | tf_op jit(solution)/shard_map/reshape | solution.py:174
  (32 shorter events, 0.7 us)
Async XLA Ops:
  0.0 9.6 %copy-start = (s32[3,2]{0,1:T(2,128)S(1)}, s32[3,2]{0,1:T(2,128)}, u32[]{:S(2)}) copy-start(s32[3,2]{0,1:T(2,128)} %param.4) | copy-start | bytes 76
  2.4 7.9 %all-to-all-start = ((f32[4,1,8192]{2,1,0:T(1,128)}), f32[4,1,8192]{2,1,0:T(1,128)S(1)}, u32[]{:S(2)}, u32[]{:S(2)}) async-start(f32[4,1,8192]{2,1,0:T(1,128)} %reshape.413), calls=%async_computation | async-start | bytes 262144 | tf_op jit(solution)/shard_map/all_to_all | solution.py:46
  14.7 7.9 %all-to-all-start.1 = ((f32[4,1,8448]{2,1,0:T(1,128)}), f32[4,1,8448]{2,1,0:T(1,128)S(1)}, u32[]{:S(2)}, u32[]{:S(2)}) async-start(f32[4,1,8448]{2,1,0:T(1,128)} %reshape.415), calls=%async_computation.1 | async-start | bytes 270336 | tf_op jit(solution)/shard_map/all_to_all | solution.py:73
  26.9 8.9 %collective-permute-start = (f32[34,2,2,256]{3,2,1,0:T(2,128)S(1)}, f32[34,2,2,256]{3,2,1,0:T(2,128)S(1)}, u32[]{:S(2)}, u32[]{:S(2)}) collective-permute-start(f32[34,2,2,256]{3,2,1,0:T(2,128)S(1)} %constant_dynamic-update-slice_fusion), channel_id=1, source_target_pairs={{4,0},{8,4},{12,8},{16,12},{20,16},{24,20},{28,24},{5,1},{9,5},{13... | collective-permute-start | bytes 417800 | tf_op jit(solution)/shard_map/ppermute | solution.py:22
  28.8 8.1 %collective-permute-start.1 = (f32[34,2,2,256]{3,2,1,0:T(2,128)S(1)}, f32[34,2,2,256]{3,2,1,0:T(2,128)S(1)}, u32[]{:S(2)}, u32[]{:S(2)}) collective-permute-start(f32[34,2,2,256]{3,2,1,0:T(2,128)S(1)} %constant_dynamic-update-slice_fusion), channel_id=1, source_target_pairs={{8,0},{12,4},{16,8},{20,12},{24,16},{28,20},{9,1},{13,5},{17,9},{2... | collective-permute-start | bytes 417800 | tf_op jit(solution)/shard_map/ppermute | solution.py:22
  30.1 14.6 %collective-permute-start.2 = (f32[34,2,2,256]{3,2,1,0:T(2,128)S(1)}, f32[34,2,2,256]{3,2,1,0:T(2,128)S(1)}, u32[]{:S(2)}, u32[]{:S(2)}) collective-permute-start(f32[34,2,2,256]{3,2,1,0:T(2,128)S(1)} %constant_dynamic-update-slice_fusion), channel_id=1, source_target_pairs={{12,0},{16,4},{20,8},{24,12},{28,16},{13,1},{17,5},{21,9},{25,13},... | collective-permute-start | bytes 417800 | tf_op jit(solution)/shard_map/ppermute | solution.py:22

commit v6 on v5

--- a/solution.py
+++ b/solution.py
@@ -12,7 +12,7 @@
 REACH = 3
 
 
-highest = lax.Precision.HIGHEST
+highest = lax.Precision.HIGH
 epsilon = 1e-06
 
 
@@ -119,8 +119,8 @@
         def rebuilt(piece):
             return piece
 
-    received = jnp.stack([passed_along(sent, "sta", -distance) for distance in range(1, REACH + 1)])
-    nearby = jnp.concatenate([whitened[None], rebuilt(received)]).reshape(REACH + 1, rows_local, stations, hour_count, 2, factor_b)
+    received = [rebuilt(passed_along(sent, "sta", -distance)[None]) for distance in range(1, REACH + 1)]
+    nearby = jnp.concatenate([whitened[None]] + received).reshape(REACH + 1, rows_local, stations, hour_count, 2, factor_b)
     slot_total = pair_blocks.shape[0]
     first_off = pair_blocks[:, 0] - owner_id
     second_off = pair_blocks[:, 1] - owner_id

time: 59.6 us -> 57.3 us (0.961)
  matrix products: 5.25 us -> 2.89 us
    dot_general x3, matrix products: 4.32 us -> 2.4 us  [matmul(): jnp.dot(left_mat, right_mat, precision=highest, preferred_element_type=jn...]
    rev x1 -> x3, local copies, waits for them, and re-layouts: 1.09 us -> 1.33 us  [rebuilt(): mirrored = spec_part[:, 1:BAND][:, ::-1, :, :, ::-1] * conj_sign]
    unnamed x11 -> x15, local copies, waits for them, and re-layouts: 2.34 us -> 2.34 us
where the time goes in v6:
time: 57.3 us; the launch traced here: 56.8 us
  waiting for transfers between devices  17.8 us (31%)
  starting transfers between devices  11.3 us (20%)
  other arithmetic  9.1 us (16%)
  local copies, waits for them, and re-layouts  7.61 us (13%)
  blocking collectives  6.67 us (12%)
  matrix products  2.89 us (5%)
  between operations  1.36 us (2%)
    ppermute x3, waiting for transfers between devices, passed_along(): return lax.ppermute(block, axis, route)  12.8 us
    all_to_all x1, blocking collectives, local(): lax.all_to_all(lag_block, 'tm', split_axis=0, concat_axis=0, tiled=True)  6.67 us
    ppermute x3, starting transfers between devices, passed_along(): return lax.ppermute(block, axis, route)  4.7 us
    all_to_all x1, waiting for transfers between devices, local(): lax.all_to_all(outgoing, 'tm', split_axis=0, concat_axis=4, tiled=True)  4.6 us
    all_to_all x1, starting transfers between devices, local(): lax.all_to_all(outgoing, 'tm', split_axis=0, concat_axis=4, tiled=True)  3.33 us
    all_to_all x1, starting transfers between devices, local(): lax.all_to_all(arranged, 'tm', split_axis=2, concat_axis=0, tiled=True)  3.32 us
    dot_general x3, matrix products, matmul(): jnp.dot(left_mat, right_mat, precision=highest, preferred_element_type=jn...  2.4 us
    unnamed x15, local copies, waits for them, and re-layouts  2.34 us
  transfers between devices with their start and end apart: 5, of which 5 were waited for; matrix products, arithmetic and copies ran while one was open for 6% of the time, Pallas kernels for 0%

profile of v6, /device:TPU:2, one launch (start us, length us, event | category | flops | bytes accessed | tf_op | source)
XLA Modules:
  0.0 56.8 jit_solution(17195214462041545765)
XLA Ops:
  0.0 1.3 %reduce.1 = f32[2,16384]{1,0:T(2,128)S(1)} reduce(f32[2,1,16384]{2,1,0:T(1,128)} %param.3, f32[]{:T(128)} %constant.102), dimensions={1}, to_apply=%param.3.reduce_sub_computation | reduce | bytes 262148 | tf_op args[0]
  1.3 0.1 copy.60
  1.5 0.9 %reshape.511 = f32[4,1,8192]{2,1,0:T(1,128)} reshape(f32[256,2,64]{2,1,0:T(2,128)S(1)} %bitcast.127) | data formatting | bytes 262144
  2.4 3.3 %all-to-all-start = ((f32[4,1,8192]{2,1,0:T(1,128)}), f32[4,1,8192]{2,1,0:T(1,128)S(1)}, u32[]{:S(2)}, u32[]{:S(2)}) async-start(f32[4,1,8192]{2,1,0:T(1,128)} %reshape.511), calls=%async_computation | async-start | bytes 262144 | tf_op jit(solution)/shard_map/all_to_all | solution.py:46
  5.7 1.0 %fusion.31 = (f32[256,256]{0,1:T(8,128)S(1)}, f32[256,256]{0,1:T(8,128)S(1)}) fusion(), kind=kLoop, calls=%fused_computation.75 | loop fusion | flops 917504 | bytes 524288 | tf_op jit(solution)/shard_map/sin | solution.py:28
  6.8 1.0 %fusion.35 = f32[256,256]{0,1:T(8,128)S(1)} fusion(), kind=kLoop, calls=%fused_computation.79 | loop fusion | flops 983040 | bytes 262144 | tf_op jit(solution)/shard_map/neg | solution.py:61
  7.8 0.5 fusion.42
  8.4 0.1 pad_add_fusion.1
  8.4 0.3 fusion.45
  8.8 0.1 pad_add_fusion
  8.9 0.1 fusion.51
  9.7 0.1 fusion.11
  9.8 0.5 all-to-all-done
  10.3 0.5 broadcast.638
  10.8 1.0 %reduce.2 = f32[4,8192]{1,0:T(4,128)S(1)} reduce(f32[4,1,8192]{2,1,0:T(1,128)S(1)} %all-to-all-done, f32[]{:T(128)} %broadcast.638), dimensions={1}, to_apply=%all_to_all.25.reduce_sub_computation | reduce | bytes 262148 | tf_op jit(solution)/shard_map/all_to_all | solution.py:46
  11.8 0.2 reshape.512
  12.0 0.2 copy.84
  12.2 0.2 copy.62
  12.4 0.2 reshape.498
  12.6 0.3 fusion.14
  12.9 0.1 copy.63
  13.0 0.1 copy.64
  13.2 0.1 multiply_add_fusion.2
  13.4 0.1 copy.68
  13.6 0.9 %reshape.513 = f32[4,1,8448]{2,1,0:T(1,128)} reshape(f32[4,33,2,2,64]{4,3,2,1,0:T(2,128)S(1)} %copy.68) | data formatting | bytes 270336
  14.5 3.3 %all-to-all-start.1 = ((f32[4,1,8448]{2,1,0:T(1,128)}), f32[4,1,8448]{2,1,0:T(1,128)S(1)}, u32[]{:S(2)}, u32[]{:S(2)}) async-start(f32[4,1,8448]{2,1,0:T(1,128)} %reshape.513), calls=%async_computation.1 | async-start | bytes 270336 | tf_op jit(solution)/shard_map/all_to_all | solution.py:73
  17.9 4.6 %all-to-all-done.1 = f32[4,1,8448]{2,1,0:T(1,128)S(1)} async-done(((f32[4,1,8448]{2,1,0:T(1,128)}), f32[4,1,8448]{2,1,0:T(1,128)S(1)}, u32[]{:S(2)}, u32[]{:S(2)}) %all-to-all-start.1) | async-done | bytes 135200 | tf_op jit(solution)/shard_map/all_to_all | solution.py:73
  22.5 1.0 %reduce.3 = f32[4,8448]{1,0:T(4,128)S(1)} reduce(f32[4,1,8448]{2,1,0:T(1,128)S(1)} %all-to-all-done.1, f32[]{:T(128)} %broadcast.638), dimensions={1}, to_apply=%all_to_all.28.reduce_sub_computation | reduce | bytes 270340 | tf_op jit(solution)/shard_map/all_to_all | solution.py:73
  23.5 0.2 reshape.514
  23.7 0.1 copy.69
  23.8 0.1 copy.85
  23.9 0.2 reshape.509
  24.1 0.1 fusion.65
  24.2 0.2 reshape.500
  24.4 0.1 multiply_subtract_fusion.3
  24.5 0.2 maximum_maximum_fusion
  24.7 0.6 %fusion.9 = f32[128,512]{1,0:T(8,128)S(1)} fusion(f32[128,512]{1,0:T(8,128)S(1)} %bitcast.150, f32[256,256]{0,1:T(8,128)S(1)} %get-tuple-element.49, f32[256,256]{0,1:T(8,128)S(1)} %get-tuple-element.48, f32[256,256]{0,1:T(8,128)S(1)} %fusion.35), kind=kOutput, calls=%fused_computation.15 | convolution fusion | flops 202113024 | bytes 1310720 | tf_op jit(solution)/shard_map/dot_general | solution.py:32
  25.4 0.2 reshape.503
  25.6 0.2 reshape.502
  25.8 0.3 fusion.34
  26.1 0.1 slice.159
  26.2 1.9 %collective-permute-start = (f32[34,2,2,256]{3,2,1,0:T(2,128)S(1)}, f32[34,2,2,256]{3,2,1,0:T(2,128)S(1)}, u32[]{:S(2)}, u32[]{:S(2)}) collective-permute-start(f32[34,2,2,256]{3,2,1,0:T(2,128)S(1)} %constant_dynamic-update-slice_fusion), channel_id=1, source_target_pairs={{4,0},{8,4},{12,8},{16,12},{20,16},{24,20},{28,24},{5,1},{9,5},{13... | collective-permute-start | bytes 417800 | tf_op jit(solution)/shard_map/ppermute | solution.py:22
  28.1 1.3 %collective-permute-start.1 = (f32[34,2,2,256]{3,2,1,0:T(2,128)S(1)}, f32[34,2,2,256]{3,2,1,0:T(2,128)S(1)}, u32[]{:S(2)}, u32[]{:S(2)}) collective-permute-start(f32[34,2,2,256]{3,2,1,0:T(2,128)S(1)} %constant_dynamic-update-slice_fusion), channel_id=1, source_target_pairs={{8,0},{12,4},{16,8},{20,12},{24,16},{28,20},{9,1},{13,5},{17,9},{2... | collective-permute-start | bytes 417800 | tf_op jit(solution)/shard_map/ppermute | solution.py:22
  29.4 1.5 %collective-permute-start.2 = (f32[34,2,2,256]{3,2,1,0:T(2,128)S(1)}, f32[34,2,2,256]{3,2,1,0:T(2,128)S(1)}, u32[]{:S(2)}, u32[]{:S(2)}) collective-permute-start(f32[34,2,2,256]{3,2,1,0:T(2,128)S(1)} %constant_dynamic-update-slice_fusion), channel_id=1, source_target_pairs={{12,0},{16,4},{20,8},{24,12},{28,16},{13,1},{17,5},{21,9},{25,13},... | collective-permute-start | bytes 417800 | tf_op jit(solution)/shard_map/ppermute | solution.py:22
  30.9 0.1 broadcast_multiply_fusion
  31.2 4.0 %collective-permute-done = f32[34,2,2,256]{3,2,1,0:T(2,128)S(1)} collective-permute-done((f32[34,2,2,256]{3,2,1,0:T(2,128)S(1)}, f32[34,2,2,256]{3,2,1,0:T(2,128)S(1)}, u32[]{:S(2)}, u32[]{:S(2)}) %collective-permute-start) | collective-permute-done | bytes 139296 | tf_op jit(solution)/shard_map/ppermute | solution.py:22
  35.1 1.1 %collective-permute-done.1 = f32[34,2,2,256]{3,2,1,0:T(2,128)S(1)} collective-permute-done((f32[34,2,2,256]{3,2,1,0:T(2,128)S(1)}, f32[34,2,2,256]{3,2,1,0:T(2,128)S(1)}, u32[]{:S(2)}, u32[]{:S(2)}) %collective-permute-start.1) | collective-permute-done | bytes 139296 | tf_op jit(solution)/shard_map/ppermute | solution.py:22
  36.3 7.7 %collective-permute-done.2 = f32[34,2,2,256]{3,2,1,0:T(2,128)S(1)} collective-permute-done((f32[34,2,2,256]{3,2,1,0:T(2,128)S(1)}, f32[34,2,2,256]{3,2,1,0:T(2,128)S(1)}, u32[]{:S(2)}, u32[]{:S(2)}) %collective-permute-start.2) | collective-permute-done | bytes 139296 | tf_op jit(solution)/shard_map/ppermute | solution.py:22
  44.1 0.4 rev.14
  44.6 0.4 rev.15
  45.0 0.4 rev.16
  45.5 0.2 broadcast_multiply_fusion.3
  45.7 0.1 maximum_multiply_fusion
  45.7 0.1 maximum_bitcast_fusion.8
  46.0 0.1 maximum_multiply_fusion.1
  46.1 0.1 maximum_bitcast_fusion.9
  46.4 0.1 maximum_bitcast_fusion.10
  46.6 0.3 select_select_fusion.1
  47.0 0.2 multiply_add_fusion.1
  47.2 1.4 %fusion = f32[3,64,2,2,2,256]{5,1,4,3,2,0:T(8,128)S(1)} fusion(f32[2,256,512,1,1,1]{2,1,0,5,4,3:T(8,128)S(1)} %bitcast.123, f32[3,64,2,2,256]{4,1,3,2,0:T(8,128)S(1)} %get-tuple-element.8, f32[3,64,2,2,256]{4,1,3,2,0:T(8,128)S(1)} %get-tuple-element.7), kind=kOutput, calls=%fused_computation.1 | convolution fusion | flops 1208352768 | bytes 4194304 | tf_op jit(solution)/shard_map/dot_general | solution.py:32
  48.7 0.2 multiply_subtract_fusion
  48.9 0.5 fusion.7
  49.5 6.7 %all_to_all.35 = f32[4,3,2,2,2,256]{5,4,3,2,1,0:T(2,128)S(1)} all-to-all(f32[4,3,2,2,2,256]{5,4,3,2,1,0:T(2,128)S(1)} %copy.79), channel_id=1, replica_groups=mesh['sta'=8,'tm'=4] {'tm'}, dimensions={0} | all-to-all | bytes 196608 | tf_op jit(solution)/shard_map/all_to_all | solution.py:172
  56.2 0.6 %reshape.504 = f32[3,2,2,512]{3,2,1,0:T(2,128)} reshape(f32[3,2,2,2,256]{4,3,2,1,0:T(2,128)S(1)} %reduce_sum.20) | data formatting | bytes 49152 | tf_op jit(solution)/shard_map/reshape | solution.py:174
  (50 shorter events, 1.1 us)
Async XLA Ops:
  0.0 9.7 %copy-start = (s32[3,2]{0,1:T(2,128)S(1)}, s32[3,2]{0,1:T(2,128)}, u32[]{:S(2)}) copy-start(s32[3,2]{0,1:T(2,128)} %param.4) | copy-start | bytes 76
  2.4 7.9 %all-to-all-start = ((f32[4,1,8192]{2,1,0:T(1,128)}), f32[4,1,8192]{2,1,0:T(1,128)S(1)}, u32[]{:S(2)}, u32[]{:S(2)}) async-start(f32[4,1,8192]{2,1,0:T(1,128)} %reshape.511), calls=%async_computation | async-start | bytes 262144 | tf_op jit(solution)/shard_map/all_to_all | solution.py:46
  14.5 7.9 %all-to-all-start.1 = ((f32[4,1,8448]{2,1,0:T(1,128)}), f32[4,1,8448]{2,1,0:T(1,128)S(1)}, u32[]{:S(2)}, u32[]{:S(2)}) async-start(f32[4,1,8448]{2,1,0:T(1,128)} %reshape.513), calls=%async_computation.1 | async-start | bytes 270336 | tf_op jit(solution)/shard_map/all_to_all | solution.py:73
  26.2 8.9 %collective-permute-start = (f32[34,2,2,256]{3,2,1,0:T(2,128)S(1)}, f32[34,2,2,256]{3,2,1,0:T(2,128)S(1)}, u32[]{:S(2)}, u32[]{:S(2)}) collective-permute-start(f32[34,2,2,256]{3,2,1,0:T(2,128)S(1)} %constant_dynamic-update-slice_fusion), channel_id=1, source_target_pairs={{4,0},{8,4},{12,8},{16,12},{20,16},{24,20},{28,24},{5,1},{9,5},{13... | collective-permute-start | bytes 417800 | tf_op jit(solution)/shard_map/ppermute | solution.py:22
  28.1 8.1 %collective-permute-start.1 = (f32[34,2,2,256]{3,2,1,0:T(2,128)S(1)}, f32[34,2,2,256]{3,2,1,0:T(2,128)S(1)}, u32[]{:S(2)}, u32[]{:S(2)}) collective-permute-start(f32[34,2,2,256]{3,2,1,0:T(2,128)S(1)} %constant_dynamic-update-slice_fusion), channel_id=1, source_target_pairs={{8,0},{12,4},{16,8},{20,12},{24,16},{28,20},{9,1},{13,5},{17,9},{2... | collective-permute-start | bytes 417800 | tf_op jit(solution)/shard_map/ppermute | solution.py:22
  29.4 14.6 %collective-permute-start.2 = (f32[34,2,2,256]{3,2,1,0:T(2,128)S(1)}, f32[34,2,2,256]{3,2,1,0:T(2,128)S(1)}, u32[]{:S(2)}, u32[]{:S(2)}) collective-permute-start(f32[34,2,2,256]{3,2,1,0:T(2,128)S(1)} %constant_dynamic-update-slice_fusion), channel_id=1, source_target_pairs={{12,0},{16,4},{20,8},{24,12},{28,16},{13,1},{17,5},{21,9},{25,13},... | collective-permute-start | bytes 417800 | tf_op jit(solution)/shard_map/ppermute | solution.py:22

commit v7 on v6

--- a/solution.py
+++ b/solution.py
@@ -33,7 +33,7 @@
 
 
 def local(records, pair_blocks, pair_count):
-    stations, hour_count, time_cols = records.shape
+    stations, hour_count, _ = records.shape
     time_devices = lax.axis_size("tm")
     time_rank = lax.axis_index("tm")
     owner_id = lax.axis_index("sta")
@@ -119,11 +119,15 @@
         def rebuilt(piece):
             return piece
 
-    received = [rebuilt(passed_along(sent, "sta", -distance)[None]) for distance in range(1, REACH + 1)]
+    arrived = {}
+    for distance in range(REACH, 0, -1):
+        arrived[distance] = passed_along(sent, "sta", -distance)
+    received = [rebuilt(arrived[distance][None]) for distance in range(1, REACH + 1)]
     nearby = jnp.concatenate([whitened[None]] + received).reshape(REACH + 1, rows_local, stations, hour_count, 2, factor_b)
     slot_total = pair_blocks.shape[0]
     first_off = pair_blocks[:, 0] - owner_id
     second_off = pair_blocks[:, 1] - owner_id
+
     def chosen(offsets):
         pick = offsets.reshape((slot_total,) + (1,) * (nearby.ndim - 1))
         result = jnp.broadcast_to(nearby[REACH], (slot_total,) + nearby.shape[1:])
@@ -176,6 +180,4 @@
 
 def solution(mesh):
     placed = (P("sta", None, "tm"), P("sta", None), P("sta"))
-    return jax.shard_map(
-        local, mesh=mesh, in_specs=placed, out_specs=P("sta", None, None, "tm"), check_vma=False
-    )
+    return jax.shard_map(local, mesh=mesh, in_specs=placed, out_specs=P("sta", None, None, "tm"), check_vma=False)

time: 57.3 us -> 57.3 us (level)
  no operation moved by 1% of the time
where the time goes in v7:
time: 57.3 us; the launch traced here: 56.8 us
  waiting for transfers between devices  17.8 us (31%)
  starting transfers between devices  11.3 us (20%)
  other arithmetic  9.1 us (16%)
  local copies, waits for them, and re-layouts  7.61 us (13%)
  blocking collectives  6.67 us (12%)
  matrix products  2.89 us (5%)
  between operations  1.36 us (2%)
    ppermute x3, waiting for transfers between devices, passed_along(): return lax.ppermute(block, axis, route)  12.8 us
    all_to_all x1, blocking collectives, local(): lax.all_to_all(lag_block, 'tm', split_axis=0, concat_axis=0, tiled=True)  6.67 us
    ppermute x3, starting transfers between devices, passed_along(): return lax.ppermute(block, axis, route)  4.7 us
    all_to_all x1, waiting for transfers between devices, local(): lax.all_to_all(outgoing, 'tm', split_axis=0, concat_axis=4, tiled=True)  4.6 us
    all_to_all x1, starting transfers between devices, local(): lax.all_to_all(outgoing, 'tm', split_axis=0, concat_axis=4, tiled=True)  3.33 us
    all_to_all x1, starting transfers between devices, local(): lax.all_to_all(arranged, 'tm', split_axis=2, concat_axis=0, tiled=True)  3.32 us
    dot_general x3, matrix products, matmul(): jnp.dot(left_mat, right_mat, precision=highest, preferred_element_type=jn...  2.4 us
    unnamed x15, local copies, waits for them, and re-layouts  2.34 us
  transfers between devices with their start and end apart: 5, of which 5 were waited for; matrix products, arithmetic and copies ran while one was open for 6% of the time, Pallas kernels for 0%

profile of v7, /device:TPU:2, one launch (start us, length us, event | category | flops | bytes accessed | tf_op | source)
XLA Modules:
  0.0 56.8 jit_solution(17195214462041545765)
XLA Ops:
  0.0 1.3 %reduce.1 = f32[2,16384]{1,0:T(2,128)S(1)} reduce(f32[2,1,16384]{2,1,0:T(1,128)} %param.3, f32[]{:T(128)} %constant.102), dimensions={1}, to_apply=%param.3.reduce_sub_computation | reduce | bytes 262148 | tf_op args[0]
  1.3 0.1 copy.60
  1.5 0.9 %reshape.511 = f32[4,1,8192]{2,1,0:T(1,128)} reshape(f32[256,2,64]{2,1,0:T(2,128)S(1)} %bitcast.127) | data formatting | bytes 262144
  2.4 3.3 %all-to-all-start = ((f32[4,1,8192]{2,1,0:T(1,128)}), f32[4,1,8192]{2,1,0:T(1,128)S(1)}, u32[]{:S(2)}, u32[]{:S(2)}) async-start(f32[4,1,8192]{2,1,0:T(1,128)} %reshape.511), calls=%async_computation | async-start | bytes 262144 | tf_op jit(solution)/shard_map/all_to_all | solution.py:46
  5.7 1.0 %fusion.31 = (f32[256,256]{0,1:T(8,128)S(1)}, f32[256,256]{0,1:T(8,128)S(1)}) fusion(), kind=kLoop, calls=%fused_computation.75 | loop fusion | flops 917504 | bytes 524288 | tf_op jit(solution)/shard_map/sin | solution.py:28
  6.8 1.0 %fusion.35 = f32[256,256]{0,1:T(8,128)S(1)} fusion(), kind=kLoop, calls=%fused_computation.79 | loop fusion | flops 983040 | bytes 262144 | tf_op jit(solution)/shard_map/neg | solution.py:61
  7.8 0.5 fusion.42
  8.4 0.1 pad_add_fusion.1
  8.4 0.3 fusion.45
  8.8 0.1 pad_add_fusion
  8.9 0.1 fusion.51
  9.7 0.1 fusion.11
  9.8 0.5 all-to-all-done
  10.3 0.5 broadcast.638
  10.8 1.0 %reduce.2 = f32[4,8192]{1,0:T(4,128)S(1)} reduce(f32[4,1,8192]{2,1,0:T(1,128)S(1)} %all-to-all-done, f32[]{:T(128)} %broadcast.638), dimensions={1}, to_apply=%all_to_all.25.reduce_sub_computation | reduce | bytes 262148 | tf_op jit(solution)/shard_map/all_to_all | solution.py:46
  11.8 0.2 reshape.512
  12.0 0.2 copy.84
  12.2 0.2 copy.62
  12.4 0.2 reshape.498
  12.6 0.3 fusion.14
  12.9 0.1 copy.63
  13.0 0.1 copy.64
  13.2 0.1 multiply_add_fusion.2
  13.4 0.1 copy.68
  13.6 0.9 %reshape.513 = f32[4,1,8448]{2,1,0:T(1,128)} reshape(f32[4,33,2,2,64]{4,3,2,1,0:T(2,128)S(1)} %copy.68) | data formatting | bytes 270336
  14.5 3.3 %all-to-all-start.1 = ((f32[4,1,8448]{2,1,0:T(1,128)}), f32[4,1,8448]{2,1,0:T(1,128)S(1)}, u32[]{:S(2)}, u32[]{:S(2)}) async-start(f32[4,1,8448]{2,1,0:T(1,128)} %reshape.513), calls=%async_computation.1 | async-start | bytes 270336 | tf_op jit(solution)/shard_map/all_to_all | solution.py:73
  17.9 4.6 %all-to-all-done.1 = f32[4,1,8448]{2,1,0:T(1,128)S(1)} async-done(((f32[4,1,8448]{2,1,0:T(1,128)}), f32[4,1,8448]{2,1,0:T(1,128)S(1)}, u32[]{:S(2)}, u32[]{:S(2)}) %all-to-all-start.1) | async-done | bytes 135200 | tf_op jit(solution)/shard_map/all_to_all | solution.py:73
  22.5 1.0 %reduce.3 = f32[4,8448]{1,0:T(4,128)S(1)} reduce(f32[4,1,8448]{2,1,0:T(1,128)S(1)} %all-to-all-done.1, f32[]{:T(128)} %broadcast.638), dimensions={1}, to_apply=%all_to_all.28.reduce_sub_computation | reduce | bytes 270340 | tf_op jit(solution)/shard_map/all_to_all | solution.py:73
  23.5 0.2 reshape.514
  23.7 0.1 copy.69
  23.8 0.1 copy.85
  23.9 0.2 reshape.509
  24.1 0.1 fusion.65
  24.2 0.2 reshape.500
  24.4 0.1 multiply_subtract_fusion.3
  24.5 0.2 maximum_maximum_fusion
  24.7 0.6 %fusion.9 = f32[128,512]{1,0:T(8,128)S(1)} fusion(f32[128,512]{1,0:T(8,128)S(1)} %bitcast.150, f32[256,256]{0,1:T(8,128)S(1)} %get-tuple-element.49, f32[256,256]{0,1:T(8,128)S(1)} %get-tuple-element.48, f32[256,256]{0,1:T(8,128)S(1)} %fusion.35), kind=kOutput, calls=%fused_computation.15 | convolution fusion | flops 202113024 | bytes 1310720 | tf_op jit(solution)/shard_map/dot_general | solution.py:32
  25.4 0.2 reshape.503
  25.6 0.2 reshape.502
  25.8 0.3 fusion.34
  26.1 0.1 slice.159
  26.2 1.9 %collective-permute-start = (f32[34,2,2,256]{3,2,1,0:T(2,128)S(1)}, f32[34,2,2,256]{3,2,1,0:T(2,128)S(1)}, u32[]{:S(2)}, u32[]{:S(2)}) collective-permute-start(f32[34,2,2,256]{3,2,1,0:T(2,128)S(1)} %constant_dynamic-update-slice_fusion), channel_id=1, source_target_pairs={{4,0},{8,4},{12,8},{16,12},{20,16},{24,20},{28,24},{5,1},{9,5},{13... | collective-permute-start | bytes 417800 | tf_op jit(solution)/shard_map/ppermute | solution.py:22
  28.1 1.3 %collective-permute-start.1 = (f32[34,2,2,256]{3,2,1,0:T(2,128)S(1)}, f32[34,2,2,256]{3,2,1,0:T(2,128)S(1)}, u32[]{:S(2)}, u32[]{:S(2)}) collective-permute-start(f32[34,2,2,256]{3,2,1,0:T(2,128)S(1)} %constant_dynamic-update-slice_fusion), channel_id=1, source_target_pairs={{8,0},{12,4},{16,8},{20,12},{24,16},{28,20},{9,1},{13,5},{17,9},{2... | collective-permute-start | bytes 417800 | tf_op jit(solution)/shard_map/ppermute | solution.py:22
  29.4 1.5 %collective-permute-start.2 = (f32[34,2,2,256]{3,2,1,0:T(2,128)S(1)}, f32[34,2,2,256]{3,2,1,0:T(2,128)S(1)}, u32[]{:S(2)}, u32[]{:S(2)}) collective-permute-start(f32[34,2,2,256]{3,2,1,0:T(2,128)S(1)} %constant_dynamic-update-slice_fusion), channel_id=1, source_target_pairs={{12,0},{16,4},{20,8},{24,12},{28,16},{13,1},{17,5},{21,9},{25,13},... | collective-permute-start | bytes 417800 | tf_op jit(solution)/shard_map/ppermute | solution.py:22
  30.9 0.1 broadcast_multiply_fusion
  31.2 4.0 %collective-permute-done = f32[34,2,2,256]{3,2,1,0:T(2,128)S(1)} collective-permute-done((f32[34,2,2,256]{3,2,1,0:T(2,128)S(1)}, f32[34,2,2,256]{3,2,1,0:T(2,128)S(1)}, u32[]{:S(2)}, u32[]{:S(2)}) %collective-permute-start) | collective-permute-done | bytes 139296 | tf_op jit(solution)/shard_map/ppermute | solution.py:22
  35.1 1.1 %collective-permute-done.1 = f32[34,2,2,256]{3,2,1,0:T(2,128)S(1)} collective-permute-done((f32[34,2,2,256]{3,2,1,0:T(2,128)S(1)}, f32[34,2,2,256]{3,2,1,0:T(2,128)S(1)}, u32[]{:S(2)}, u32[]{:S(2)}) %collective-permute-start.1) | collective-permute-done | bytes 139296 | tf_op jit(solution)/shard_map/ppermute | solution.py:22
  36.3 7.7 %collective-permute-done.2 = f32[34,2,2,256]{3,2,1,0:T(2,128)S(1)} collective-permute-done((f32[34,2,2,256]{3,2,1,0:T(2,128)S(1)}, f32[34,2,2,256]{3,2,1,0:T(2,128)S(1)}, u32[]{:S(2)}, u32[]{:S(2)}) %collective-permute-start.2) | collective-permute-done | bytes 139296 | tf_op jit(solution)/shard_map/ppermute | solution.py:22
  44.1 0.4 rev.14
  44.6 0.4 rev.15
  45.0 0.4 rev.16
  45.5 0.2 broadcast_multiply_fusion.3
  45.7 0.1 maximum_multiply_fusion
  45.7 0.1 maximum_bitcast_fusion.8
  46.0 0.1 maximum_multiply_fusion.1
  46.1 0.1 maximum_bitcast_fusion.9
  46.4 0.1 maximum_bitcast_fusion.10
  46.6 0.3 select_select_fusion.1
  47.0 0.2 multiply_add_fusion.1
  47.2 1.4 %fusion = f32[3,64,2,2,2,256]{5,1,4,3,2,0:T(8,128)S(1)} fusion(f32[2,256,512,1,1,1]{2,1,0,5,4,3:T(8,128)S(1)} %bitcast.123, f32[3,64,2,2,256]{4,1,3,2,0:T(8,128)S(1)} %get-tuple-element.8, f32[3,64,2,2,256]{4,1,3,2,0:T(8,128)S(1)} %get-tuple-element.7), kind=kOutput, calls=%fused_computation.1 | convolution fusion | flops 1208352768 | bytes 4194304 | tf_op jit(solution)/shard_map/dot_general | solution.py:32
  48.7 0.2 multiply_subtract_fusion
  48.9 0.5 fusion.7
  49.5 6.7 %all_to_all.35 = f32[4,3,2,2,2,256]{5,4,3,2,1,0:T(2,128)S(1)} all-to-all(f32[4,3,2,2,2,256]{5,4,3,2,1,0:T(2,128)S(1)} %copy.79), channel_id=1, replica_groups=mesh['sta'=8,'tm'=4] {'tm'}, dimensions={0} | all-to-all | bytes 196608 | tf_op jit(solution)/shard_map/all_to_all | solution.py:176
  56.2 0.6 %reshape.504 = f32[3,2,2,512]{3,2,1,0:T(2,128)} reshape(f32[3,2,2,2,256]{4,3,2,1,0:T(2,128)S(1)} %reduce_sum.20) | data formatting | bytes 49152 | tf_op jit(solution)/shard_map/reshape | solution.py:178
  (50 shorter events, 1.1 us)
Async XLA Ops:
  0.0 9.7 %copy-start = (s32[3,2]{0,1:T(2,128)S(1)}, s32[3,2]{0,1:T(2,128)}, u32[]{:S(2)}) copy-start(s32[3,2]{0,1:T(2,128)} %param.4) | copy-start | bytes 76
  2.4 7.9 %all-to-all-start = ((f32[4,1,8192]{2,1,0:T(1,128)}), f32[4,1,8192]{2,1,0:T(1,128)S(1)}, u32[]{:S(2)}, u32[]{:S(2)}) async-start(f32[4,1,8192]{2,1,0:T(1,128)} %reshape.511), calls=%async_computation | async-start | bytes 262144 | tf_op jit(solution)/shard_map/all_to_all | solution.py:46
  14.5 7.9 %all-to-all-start.1 = ((f32[4,1,8448]{2,1,0:T(1,128)}), f32[4,1,8448]{2,1,0:T(1,128)S(1)}, u32[]{:S(2)}, u32[]{:S(2)}) async-start(f32[4,1,8448]{2,1,0:T(1,128)} %reshape.513), calls=%async_computation.1 | async-start | bytes 270336 | tf_op jit(solution)/shard_map/all_to_all | solution.py:73
  26.2 8.9 %collective-permute-start = (f32[34,2,2,256]{3,2,1,0:T(2,128)S(1)}, f32[34,2,2,256]{3,2,1,0:T(2,128)S(1)}, u32[]{:S(2)}, u32[]{:S(2)}) collective-permute-start(f32[34,2,2,256]{3,2,1,0:T(2,128)S(1)} %constant_dynamic-update-slice_fusion), channel_id=1, source_target_pairs={{4,0},{8,4},{12,8},{16,12},{20,16},{24,20},{28,24},{5,1},{9,5},{13... | collective-permute-start | bytes 417800 | tf_op jit(solution)/shard_map/ppermute | solution.py:22
  28.1 8.1 %collective-permute-start.1 = (f32[34,2,2,256]{3,2,1,0:T(2,128)S(1)}, f32[34,2,2,256]{3,2,1,0:T(2,128)S(1)}, u32[]{:S(2)}, u32[]{:S(2)}) collective-permute-start(f32[34,2,2,256]{3,2,1,0:T(2,128)S(1)} %constant_dynamic-update-slice_fusion), channel_id=1, source_target_pairs={{8,0},{12,4},{16,8},{20,12},{24,16},{28,20},{9,1},{13,5},{17,9},{2... | collective-permute-start | bytes 417800 | tf_op jit(solution)/shard_map/ppermute | solution.py:22
  29.4 14.6 %collective-permute-start.2 = (f32[34,2,2,256]{3,2,1,0:T(2,128)S(1)}, f32[34,2,2,256]{3,2,1,0:T(2,128)S(1)}, u32[]{:S(2)}, u32[]{:S(2)}) collective-permute-start(f32[34,2,2,256]{3,2,1,0:T(2,128)S(1)} %constant_dynamic-update-slice_fusion), channel_id=1, source_target_pairs={{12,0},{16,4},{20,8},{24,12},{28,16},{13,1},{17,5},{21,9},{25,13},... | collective-permute-start | bytes 417800 | tf_op jit(solution)/shard_map/ppermute | solution.py:22

commit v8 on v7

--- a/solution.py
+++ b/solution.py
@@ -103,27 +103,12 @@
     if paired:
         scale_row = band_scale[:, 0].transpose(1, 0, 2)[None]
         sent = jnp.concatenate([spec.reshape(rows_local, series, 2, factor_b)[: BAND + 1], scale_row])
-
-        def rebuilt(piece):
-            spec_part = piece[:, : BAND + 1]
-            scale_low = piece[:, BAND + 1, :, 0][:, None, :, None, :]
-            scale_high = piece[:, BAND + 1, :, 1][:, None, :, None, :]
-            conj_sign = (1 - 2 * lax.iota(jnp.int32, 2)).astype(jnp.float32)[None, None, None, :, None]
-            mirrored = spec_part[:, 1:BAND][:, ::-1, :, :, ::-1] * conj_sign
-            high = jnp.concatenate([spec_part[:, BAND:], mirrored], axis=1)
-            return jnp.concatenate([spec_part[:, :BAND] * scale_low, high * scale_high], axis=1)
-
     else:
         sent = whitened
-
-        def rebuilt(piece):
-            return piece
-
     arrived = {}
     for distance in range(REACH, 0, -1):
         arrived[distance] = passed_along(sent, "sta", -distance)
-    received = [rebuilt(arrived[distance][None]) for distance in range(1, REACH + 1)]
-    nearby = jnp.concatenate([whitened[None]] + received).reshape(REACH + 1, rows_local, stations, hour_count, 2, factor_b)
+    nearby = jnp.stack([sent] + [arrived[distance] for distance in range(1, REACH + 1)])
     slot_total = pair_blocks.shape[0]
     first_off = pair_blocks[:, 0] - owner_id
     second_off = pair_blocks[:, 1] - owner_id
@@ -135,8 +120,22 @@
             result = jnp.where(pick == distance, nearby[distance], result)
         return result
 
-    left_spec = chosen(first_off)
-    right_spec = chosen(second_off)
+    def domain(block):
+        if not paired:
+            return block
+        spec_part = block[:, : BAND + 1]
+        scale_low = block[:, BAND + 1, :, 0][:, None, :, None, :]
+        scale_high = block[:, BAND + 1, :, 1]
+        scale_turned = scale_high[:, :, ::-1][:, None, :, None, :]
+        conj_sign = (1 - 2 * lax.iota(jnp.int32, 2)).astype(jnp.float32)[None, None, None, :, None]
+        low = spec_part[:, :BAND] * scale_low
+        middle = spec_part[:, BAND:] * scale_high[:, None, :, None, :]
+        high = spec_part[:, 1:BAND] * conj_sign * scale_turned
+        return jnp.concatenate([low, middle, high], axis=1)
+
+    spec_shape = (slot_total, rows_local, stations, hour_count, 2, factor_b)
+    left_spec = domain(chosen(first_off)).reshape(spec_shape)
+    right_spec = domain(chosen(second_off)).reshape(spec_shape)
     left_real = left_spec[:, :, :, None, :, 0]
     left_imag = left_spec[:, :, :, None, :, 1]
     right_real = right_spec[:, :, None, :, :, 0]
@@ -144,21 +143,31 @@
     cross_real = jnp.sum(left_real * right_real + left_imag * right_imag, axis=4)
     cross_imag = jnp.sum(left_imag * right_real - left_real * right_imag, axis=4)
     cross = jnp.concatenate([cross_real, cross_imag], axis=-1)
-    inverse_b = jnp.concatenate(
-        [jnp.concatenate([cosine_b, sine_b], axis=1), jnp.concatenate([-sine_b, cosine_b], axis=1)],
-        axis=0,
-    )
-    lag = matmul(cross.reshape(-1, 2 * factor_b), inverse_b).reshape(
-        slot_total, rows_local, stations, stations, 2, factor_b
-    )
+
+    def inverse_of(cosines, sines):
+        return jnp.concatenate(
+            [jnp.concatenate([cosines, sines], axis=1), jnp.concatenate([-sines, cosines], axis=1)],
+            axis=0,
+        )
+
+    lag_shape = (slot_total, -1, stations, stations, 2, factor_b)
+    if paired:
+        cosine_r, sine_r = angles(factor_b - 1 - index_b, index_b, factor_b)
+        lag_low = matmul(cross[:, : BAND + 1].reshape(-1, 2 * factor_b), inverse_of(cosine_b, sine_b))
+        lag_high = matmul(cross[:, BAND + 1 :].reshape(-1, 2 * factor_b), inverse_of(cosine_r, sine_r))
+        lag = jnp.concatenate([lag_low.reshape(lag_shape), lag_high.reshape(lag_shape)], axis=1)
+        row_ids = jnp.concatenate([k1_ids[: BAND + 1], k1_ids[BAND + 1 :][::-1]])
+    else:
+        lag = matmul(cross.reshape(-1, 2 * factor_b), inverse_of(cosine_b, sine_b)).reshape(lag_shape)
+        row_ids = k1_ids
     lag_real, lag_imag = lag[:, :, :, :, 0], lag[:, :, :, :, 1]
-    cosine_u, sine_u = angles(k1_ids, index_b, SAMPLES)
+    cosine_u, sine_u = angles(row_ids, index_b, SAMPLES)
     turn_real = lag_real * cosine_u[None, :, None, None, :] - lag_imag * sine_u[None, :, None, None, :]
     turn_imag = lag_real * sine_u[None, :, None, None, :] + lag_imag * cosine_u[None, :, None, None, :]
     lag_ids = jnp.concatenate(
         [jnp.arange(LAGS, dtype=jnp.int32), factor_a - LAGS + jnp.arange(LAGS, dtype=jnp.int32)]
     )
-    cosine_l, sine_l = angles(lag_ids, k1_ids, factor_a)
+    cosine_l, sine_l = angles(lag_ids, row_ids, factor_a)
     lag_weights = jnp.concatenate([cosine_l, -sine_l], axis=1).reshape(
         time_devices, 2 * LAGS // time_devices, 2 * rows_local
     )

time: 57.3 us -> 59.9 us (1.045)
  other arithmetic: 9.1 us -> 12.1 us
    cos x3 -> x4, other arithmetic: 1 us -> 3.3 us  [angles(): return (jnp.cos(radians), jnp.sin(radians))]
    sin x2 -> x3, other arithmetic: 1.08 us -> 2.65 us  [angles(): return (jnp.cos(radians), jnp.sin(radians))]
    neg x1 -> x0, other arithmetic: 0.98 us -> none  [local(): both_a = jnp.concatenate([cosine_a, -sine_a], axis=0)]
    rev x3, local copies, waits for them, and re-layouts: 1.33 us -> 0.51 us  [the longest x2 0.41 us: domain(): scale_turned = scale_high[:, :, ::-1][:, None, :, None, :]]
    unnamed x15 -> x37, local copies, waits for them, and re-layouts: 2.34 us -> 2.81 us
    dot_general x3 -> x4, matrix products: 2.4 us -> 2.78 us  [matmul(): jnp.dot(left_mat, right_mat, precision=highest, preferred_element_type=jn...]
  transfers between devices with their start and end apart: 5 -> 5, of which waited for: 5 -> 4; matrix products, arithmetic and copies ran while one was open for 6% -> 12% of each run, Pallas kernels for 0% -> 0%
where the time goes in v8:
time: 59.9 us; the launch traced here: 59.3 us
  waiting for transfers between devices  17.4 us (29%)
  other arithmetic  12.1 us (20%)
  starting transfers between devices  11.3 us (19%)
  local copies, waits for them, and re-layouts  7.06 us (12%)
  blocking collectives  6.67 us (11%)
  matrix products  3.28 us (5%)
  between operations  1.42 us (2%)
    ppermute x3, waiting for transfers between devices, passed_along(): return lax.ppermute(block, axis, route)  12.8 us
    all_to_all x1, blocking collectives, local(): lax.all_to_all(lag_block, 'tm', split_axis=0, concat_axis=0, tiled=True)  6.67 us
    ppermute x3, starting transfers between devices, passed_along(): return lax.ppermute(block, axis, route)  4.69 us
    all_to_all x1, waiting for transfers between devices, local(): lax.all_to_all(outgoing, 'tm', split_axis=0, concat_axis=4, tiled=True)  4.6 us
    all_to_all x1, starting transfers between devices, local(): lax.all_to_all(outgoing, 'tm', split_axis=0, concat_axis=4, tiled=True)  3.33 us
    all_to_all x1, starting transfers between devices, local(): lax.all_to_all(arranged, 'tm', split_axis=2, concat_axis=0, tiled=True)  3.32 us
    cos x4, other arithmetic, angles(): return (jnp.cos(radians), jnp.sin(radians))  3.3 us
    unnamed x37, local copies, waits for them, and re-layouts  2.81 us
  transfers between devices with their start and end apart: 5, of which 4 were waited for; matrix products, arithmetic and copies ran while one was open for 12% of the time, Pallas kernels for 0%

profile of v8, /device:TPU:2, one launch (start us, length us, event | category | flops | bytes accessed | tf_op | source)
XLA Modules:
  0.0 59.3 jit_solution(13792669352347680132)
XLA Ops:
  0.0 1.3 %reduce.1 = f32[2,16384]{1,0:T(2,128)S(1)} reduce(f32[2,1,16384]{2,1,0:T(1,128)} %param.3, f32[]{:T(128)} %constant.108), dimensions={1}, to_apply=%param.3.reduce_sub_computation | reduce | bytes 262148 | tf_op args[0]
  1.3 0.1 copy.57
  1.5 0.9 %reshape.363 = f32[4,1,8192]{2,1,0:T(1,128)} reshape(f32[256,2,64]{2,1,0:T(2,128)S(1)} %bitcast.130) | data formatting | bytes 262144
  2.4 3.3 %all-to-all-start = ((f32[4,1,8192]{2,1,0:T(1,128)}), f32[4,1,8192]{2,1,0:T(1,128)S(1)}, u32[]{:S(2)}, u32[]{:S(2)}) async-start(f32[4,1,8192]{2,1,0:T(1,128)} %reshape.363), calls=%async_computation | async-start | bytes 262144 | tf_op jit(solution)/shard_map/all_to_all | solution.py:46
  5.7 1.0 %fusion.48 = (f32[256,256]{0,1:T(8,128)S(1)}, f32[256,256]{0,1:T(8,128)S(1)}) fusion(), kind=kLoop, calls=%fused_computation.93 | loop fusion | flops 983040 | bytes 524288 | tf_op jit(solution)/shard_map/cos | solution.py:28
  6.8 1.0 %fusion.47 = f32[256,256]{0,1:T(8,128)S(1)} fusion(), kind=kLoop, calls=%fused_computation.92 | loop fusion | flops 917504 | bytes 262144 | tf_op jit(solution)/shard_map/sin | solution.py:28
  7.8 0.5 fusion.61
  8.3 1.0 %fusion.49 = (f32[256,256]{0,1:T(8,128)S(1)}, f32[256,256]{0,1:T(8,128)S(1)}, f32[256,256]{0,1:T(8,128)S(1)}) fusion(s32[256]{0:T(256)S(1)} %iota_subtract_fusion), kind=kLoop, calls=%fused_computation.94 | loop fusion | flops 983040 | bytes 787456 | tf_op jit(solution)/shard_map/sin | solution.py:28
  9.4 0.1 slice.160
  9.5 0.1 pad_add_fusion.1
  9.5 0.1 rev.16
  9.6 0.1 pad_add_fusion.2
  9.7 1.0 %fusion.64 = (f32[64,256]{1,0:T(8,128)}, f32[64,256]{1,0:T(8,128)}) fusion(s32[64]{0:T(128)S(1)} %pad_add_fusion.2), kind=kLoop, calls=%fused_computation.114 | loop fusion | flops 229376 | bytes 131328 | tf_op jit(solution)/shard_map/cos | solution.py:28
  10.7 0.1 pad_add_fusion
  10.8 0.7 %fusion.70 = (f32[4,2,64]{2,0,1:T(4,128)}, f32[4,2,64]{2,0,1:T(4,128)}) fusion(s32[64]{0:T(128)S(1)} %pad_add_fusion.2, s32[4,2]{0,1:T(2,128)S(1)} %pad_add_fusion), kind=kLoop, calls=%fused_computation.136 | loop fusion | flops 7680 | bytes 4384 | tf_op jit(solution)/shard_map/cos | solution.py:28
  12.2 0.6 %compare_bitcast_fusion.5 = (pred[3]{0:T(512)(128)(4,1)}, pred[3]{0:T(512)(128)(4,1)}, pred[3]{0:T(512)(128)(4,1)}, pred[3]{0:T(512)(128)(4,1)}, pred[3]{0:T(512)(128)(4,1)}, /*index=5*/pred[3]{0:T(512)(128)(4,1)}) fusion(s32[]{:T(128)S(6)} %axis_index.23, s32[3,2]{0,1:T(2,128)S(1)} %copy-done.12), kind=kLoop, calls=%fused_computation.144 | loop fusion | flops 24 | bytes 46 | tf_op jit(solution)/shard_map/eq | solution.py:120
  12.8 0.1 fusion.8
  12.9 0.6 %fusion.73 = (f32[256]{0:T(256)}, f32[256]{0:T(256)}) fusion(), kind=kLoop, calls=%fused_computation.157 | loop fusion | flops 2048 | bytes 2048 | tf_op jit(solution)/shard_map/sin | solution.py:28
  13.5 0.6 broadcast.492
  14.1 1.0 %reduce.2 = f32[4,8192]{1,0:T(4,128)S(1)} reduce(f32[4,1,8192]{2,1,0:T(1,128)S(1)} %all-to-all-done, f32[]{:T(128)} %broadcast.492), dimensions={1}, to_apply=%all_to_all.25.reduce_sub_computation | reduce | bytes 262148 | tf_op jit(solution)/shard_map/all_to_all | solution.py:46
  15.1 0.2 reshape.364
  15.3 0.2 copy.83
  15.5 0.2 copy.59
  15.7 0.2 reshape.347
  15.9 0.3 fusion.22
  16.2 0.1 copy.60
  16.4 0.1 copy.61
  16.8 0.1 copy.65
  16.9 0.9 %reshape.365 = f32[4,1,8448]{2,1,0:T(1,128)} reshape(f32[4,33,2,2,64]{4,3,2,1,0:T(2,128)S(1)} %copy.65) | data formatting | bytes 270336
  17.8 3.3 %all-to-all-start.1 = ((f32[4,1,8448]{2,1,0:T(1,128)}), f32[4,1,8448]{2,1,0:T(1,128)S(1)}, u32[]{:S(2)}, u32[]{:S(2)}) async-start(f32[4,1,8448]{2,1,0:T(1,128)} %reshape.365), calls=%async_computation.1 | async-start | bytes 270336 | tf_op jit(solution)/shard_map/all_to_all | solution.py:73
  21.2 4.6 %all-to-all-done.1 = f32[4,1,8448]{2,1,0:T(1,128)S(1)} async-done(((f32[4,1,8448]{2,1,0:T(1,128)}), f32[4,1,8448]{2,1,0:T(1,128)S(1)}, u32[]{:S(2)}, u32[]{:S(2)}) %all-to-all-start.1) | async-done | bytes 135200 | tf_op jit(solution)/shard_map/all_to_all | solution.py:73
  25.8 1.0 %reduce.3 = f32[4,8448]{1,0:T(4,128)S(1)} reduce(f32[4,1,8448]{2,1,0:T(1,128)S(1)} %all-to-all-done.1, f32[]{:T(128)} %broadcast.492), dimensions={1}, to_apply=%all_to_all.28.reduce_sub_computation | reduce | bytes 270340 | tf_op jit(solution)/shard_map/all_to_all | solution.py:73
  26.8 0.2 reshape.366
  27.1 0.1 copy.66
  27.2 0.1 copy.84
  27.2 0.2 reshape.361
  27.4 0.1 fusion.83
  27.6 0.2 reshape.349
  27.8 0.1 multiply_subtract_fusion.3
  27.9 0.2 maximum_maximum_fusion.1
  28.1 0.6 %fusion.6 = f32[128,512]{1,0:T(8,128)S(1)} fusion(f32[128,512]{1,0:T(8,128)S(1)} %bitcast.140, f32[256,256]{0,1:T(8,128)S(1)} %get-tuple-element.48, f32[256,256]{0,1:T(8,128)S(1)} %fusion.47, f32[256,256]{0,1:T(8,128)S(1)} %get-tuple-element.49), kind=kOutput, calls=%fused_computation.15 | convolution fusion | flops 202113024 | bytes 1310720 | tf_op jit(solution)/shard_map/dot_general | solution.py:32
  28.8 0.2 reshape.351
  29.0 0.1 slice.138
  29.1 0.3 fusion.52
  29.4 1.9 %collective-permute-start = (f32[34,2,2,256]{3,2,1,0:T(2,128)S(1)}, f32[34,2,2,256]{3,2,1,0:T(2,128)S(1)}, u32[]{:S(2)}, u32[]{:S(2)}) collective-permute-start(f32[34,2,2,256]{3,2,1,0:T(2,128)S(1)} %constant_dynamic-update-slice_fusion), channel_id=1, source_target_pairs={{4,0},{8,4},{12,8},{16,12},{20,16},{24,20},{28,24},{5,1},{9,5},{13... | collective-permute-start | bytes 417800 | tf_op jit(solution)/shard_map/ppermute | solution.py:22
  31.3 1.3 %collective-permute-start.1 = (f32[34,2,2,256]{3,2,1,0:T(2,128)S(1)}, f32[34,2,2,256]{3,2,1,0:T(2,128)S(1)}, u32[]{:S(2)}, u32[]{:S(2)}) collective-permute-start(f32[34,2,2,256]{3,2,1,0:T(2,128)S(1)} %constant_dynamic-update-slice_fusion), channel_id=1, source_target_pairs={{8,0},{12,4},{16,8},{20,12},{24,16},{28,20},{9,1},{13,5},{17,9},{2... | collective-permute-start | bytes 417800 | tf_op jit(solution)/shard_map/ppermute | solution.py:22
  32.6 1.5 %collective-permute-start.2 = (f32[34,2,2,256]{3,2,1,0:T(2,128)S(1)}, f32[34,2,2,256]{3,2,1,0:T(2,128)S(1)}, u32[]{:S(2)}, u32[]{:S(2)}) collective-permute-start(f32[34,2,2,256]{3,2,1,0:T(2,128)S(1)} %constant_dynamic-update-slice_fusion), channel_id=1, source_target_pairs={{12,0},{16,4},{20,8},{24,12},{28,16},{13,1},{17,5},{21,9},{25,13},... | collective-permute-start | bytes 417800 | tf_op jit(solution)/shard_map/ppermute | solution.py:22
  34.1 0.1 maximum_maximum_fusion
  34.3 4.0 %collective-permute-done = f32[34,2,2,256]{3,2,1,0:T(2,128)S(1)} collective-permute-done((f32[34,2,2,256]{3,2,1,0:T(2,128)S(1)}, f32[34,2,2,256]{3,2,1,0:T(2,128)S(1)}, u32[]{:S(2)}, u32[]{:S(2)}) %collective-permute-start) | collective-permute-done | bytes 139296 | tf_op jit(solution)/shard_map/ppermute | solution.py:22
  38.4 1.1 %collective-permute-done.1 = f32[34,2,2,256]{3,2,1,0:T(2,128)S(1)} collective-permute-done((f32[34,2,2,256]{3,2,1,0:T(2,128)S(1)}, f32[34,2,2,256]{3,2,1,0:T(2,128)S(1)}, u32[]{:S(2)}, u32[]{:S(2)}) %collective-permute-start.1) | collective-permute-done | bytes 139296 | tf_op jit(solution)/shard_map/ppermute | solution.py:22
  39.5 7.8 %collective-permute-done.2 = f32[34,2,2,256]{3,2,1,0:T(2,128)S(1)} collective-permute-done((f32[34,2,2,256]{3,2,1,0:T(2,128)S(1)}, f32[34,2,2,256]{3,2,1,0:T(2,128)S(1)}, u32[]{:S(2)}, u32[]{:S(2)}) %collective-permute-start.2) | collective-permute-done | bytes 139296 | tf_op jit(solution)/shard_map/ppermute | solution.py:22
  47.3 0.2 select_select_fusion.1
  47.6 0.2 rev.14
  47.8 0.2 rev.15
  48.1 0.2 fusion.27
  48.3 0.1 maximum_bitcast_fusion.6
  48.6 0.2 multiply_add_fusion.1
  48.8 1.0 %fusion.13 = f32[3,33,2,2,2,256]{5,1,4,3,2,0:T(8,128)S(1)} fusion(f32[2,256,512,1,1,1]{2,1,0,5,4,3:T(8,128)S(1)} %bitcast.125, f32[3,64,2,2,256]{4,1,3,2,0:T(8,128)S(1)} %get-tuple-element.7, f32[3,64,2,2,256]{4,1,3,2,0:T(8,128)S(1)} %get-tuple-element.8), kind=kOutput, calls=%fused_computation.22 | convolution fusion | flops 623056896 | bytes 3432448 | tf_op jit(solution)/shard_map/dot_general | solution.py:32
  49.8 0.8 %fusion.19 = f32[3,31,2,2,2,256]{5,1,4,3,2,0:T(8,128)S(1)} fusion(f32[2,256,512,1,1,1]{2,1,0,5,4,3:T(8,128)S(1)} %bitcast.126, f32[3,64,2,2,256]{4,1,3,2,0:T(8,128)S(1)} %get-tuple-element.8, f32[3,64,2,2,256]{4,1,3,2,0:T(8,128)S(1)} %get-tuple-element.7), kind=kOutput, calls=%fused_computation.29 | convolution fusion | flops 585295872 | bytes 3383296 | tf_op jit(solution)/shard_map/dot_general | solution.py:32
  50.7 0.3 multiply_subtract_fusion
  51.0 0.4 copy-done.2
  51.4 0.5 fusion.4
  52.0 6.7 %all_to_all.35 = f32[4,3,2,2,2,256]{5,4,3,2,1,0:T(2,128)S(1)} all-to-all(f32[4,3,2,2,2,256]{5,4,3,2,1,0:T(2,128)S(1)} %copy.76), channel_id=1, replica_groups=mesh['sta'=8,'tm'=4] {'tm'}, dimensions={0} | all-to-all | bytes 196608 | tf_op jit(solution)/shard_map/all_to_all | solution.py:185
  58.7 0.6 %reshape.354 = f32[3,2,2,512]{3,2,1,0:T(2,128)} reshape(f32[3,2,2,2,256]{4,3,2,1,0:T(2,128)S(1)} %reduce_sum.20) | data formatting | bytes 49152 | tf_op jit(solution)/shard_map/reshape | solution.py:187
  (65 shorter events, 1.0 us)
Async XLA Ops:
  2.4 11.1 %all-to-all-start = ((f32[4,1,8192]{2,1,0:T(1,128)}), f32[4,1,8192]{2,1,0:T(1,128)S(1)}, u32[]{:S(2)}, u32[]{:S(2)}) async-start(f32[4,1,8192]{2,1,0:T(1,128)} %reshape.363), calls=%async_computation | async-start | bytes 262144 | tf_op jit(solution)/shard_map/all_to_all | solution.py:46
  5.7 6.5 %copy-start.12 = (s32[3,2]{0,1:T(2,128)S(1)}, s32[3,2]{0,1:T(2,128)}, u32[]{:S(2)}) copy-start(s32[3,2]{0,1:T(2,128)} %param.4) | copy-start | bytes 76
  17.8 7.9 %all-to-all-start.1 = ((f32[4,1,8448]{2,1,0:T(1,128)}), f32[4,1,8448]{2,1,0:T(1,128)S(1)}, u32[]{:S(2)}, u32[]{:S(2)}) async-start(f32[4,1,8448]{2,1,0:T(1,128)} %reshape.365), calls=%async_computation.1 | async-start | bytes 270336 | tf_op jit(solution)/shard_map/all_to_all | solution.py:73
  27.1 0.7 %copy-start.4 = (f32[256]{0:T(256)S(1)}, f32[256]{0:T(256)}, u32[]{:S(2)}) copy-start(f32[256]{0:T(256)} %get-tuple-element.50) | copy-start | bytes 3076
  27.1 0.7 %copy-start.5 = (f32[256]{0:T(256)S(1)}, f32[256]{0:T(256)}, u32[]{:S(2)}) copy-start(f32[256]{0:T(256)} %get-tuple-element.51) | copy-start | bytes 3076
  29.4 8.9 %collective-permute-start = (f32[34,2,2,256]{3,2,1,0:T(2,128)S(1)}, f32[34,2,2,256]{3,2,1,0:T(2,128)S(1)}, u32[]{:S(2)}, u32[]{:S(2)}) collective-permute-start(f32[34,2,2,256]{3,2,1,0:T(2,128)S(1)} %constant_dynamic-update-slice_fusion), channel_id=1, source_target_pairs={{4,0},{8,4},{12,8},{16,12},{20,16},{24,20},{28,24},{5,1},{9,5},{13... | collective-permute-start | bytes 417800 | tf_op jit(solution)/shard_map/ppermute | solution.py:22
  31.3 8.1 %collective-permute-start.1 = (f32[34,2,2,256]{3,2,1,0:T(2,128)S(1)}, f32[34,2,2,256]{3,2,1,0:T(2,128)S(1)}, u32[]{:S(2)}, u32[]{:S(2)}) collective-permute-start(f32[34,2,2,256]{3,2,1,0:T(2,128)S(1)} %constant_dynamic-update-slice_fusion), channel_id=1, source_target_pairs={{8,0},{12,4},{16,8},{20,12},{24,16},{28,20},{9,1},{13,5},{17,9},{2... | collective-permute-start | bytes 417800 | tf_op jit(solution)/shard_map/ppermute | solution.py:22
  32.6 14.6 %collective-permute-start.2 = (f32[34,2,2,256]{3,2,1,0:T(2,128)S(1)}, f32[34,2,2,256]{3,2,1,0:T(2,128)S(1)}, u32[]{:S(2)}, u32[]{:S(2)}) collective-permute-start(f32[34,2,2,256]{3,2,1,0:T(2,128)S(1)} %constant_dynamic-update-slice_fusion), channel_id=1, source_target_pairs={{12,0},{16,4},{20,8},{24,12},{28,16},{13,1},{17,5},{21,9},{25,13},... | collective-permute-start | bytes 417800 | tf_op jit(solution)/shard_map/ppermute | solution.py:22
  34.2 13.0 %copy-start.6 = (pred[3]{0:T(512)(128)(4,1)S(1)}, pred[3]{0:T(512)(128)(4,1)}, u32[]{:S(2)}) copy-start(pred[3]{0:T(512)(128)(4,1)} %get-tuple-element.31) | copy-start | bytes 13
  34.2 13.0 %copy-start.7 = (pred[3]{0:T(512)(128)(4,1)S(1)}, pred[3]{0:T(512)(128)(4,1)}, u32[]{:S(2)}) copy-start(pred[3]{0:T(512)(128)(4,1)} %get-tuple-element.32) | copy-start | bytes 13
  34.2 13.0 %copy-start.8 = (pred[3]{0:T(512)(128)(4,1)S(1)}, pred[3]{0:T(512)(128)(4,1)}, u32[]{:S(2)}) copy-start(pred[3]{0:T(512)(128)(4,1)} %get-tuple-element.33) | copy-start | bytes 13
  34.3 13.0 %copy-start.9 = (pred[3]{0:T(512)(128)(4,1)S(1)}, pred[3]{0:T(512)(128)(4,1)}, u32[]{:S(2)}) copy-start(pred[3]{0:T(512)(128)(4,1)} %get-tuple-element.34) | copy-start | bytes 13
  34.3 13.0 %copy-start.10 = (pred[3]{0:T(512)(128)(4,1)S(1)}, pred[3]{0:T(512)(128)(4,1)}, u32[]{:S(2)}) copy-start(pred[3]{0:T(512)(128)(4,1)} %get-tuple-element.35) | copy-start | bytes 13
  34.3 13.0 %copy-start.11 = (pred[3]{0:T(512)(128)(4,1)S(1)}, pred[3]{0:T(512)(128)(4,1)}, u32[]{:S(2)}) copy-start(pred[3]{0:T(512)(128)(4,1)} %get-tuple-element.36) | copy-start | bytes 13
  49.8 0.9 %copy-start = (f32[64,256]{1,0:T(8,128)S(1)}, f32[64,256]{1,0:T(8,128)}, u32[]{:S(2)}) copy-start(f32[64,256]{1,0:T(8,128)} %get-tuple-element.44) | copy-start | bytes 196612
  49.8 0.9 %copy-start.1 = (f32[64,256]{1,0:T(8,128)S(1)}, f32[64,256]{1,0:T(8,128)}, u32[]{:S(2)}) copy-start(f32[64,256]{1,0:T(8,128)} %get-tuple-element.45) | copy-start | bytes 196612
  50.7 0.7 %copy-start.2 = (f32[4,2,64]{2,0,1:T(4,128)S(1)}, f32[4,2,64]{2,0,1:T(4,128)}, u32[]{:S(2)}) copy-start(f32[4,2,64]{2,0,1:T(4,128)} %get-tuple-element.29) | copy-start | bytes 6148
  50.7 0.7 %copy-start.3 = (f32[4,2,64]{2,0,1:T(4,128)S(1)}, f32[4,2,64]{2,0,1:T(4,128)}, u32[]{:S(2)}) copy-start(f32[4,2,64]{2,0,1:T(4,128)} %get-tuple-element.30) | copy-start | bytes 6148

commit v9 on v8

--- a/solution.py
+++ b/solution.py
@@ -73,7 +73,8 @@
         incoming = lax.all_to_all(outgoing, "tm", split_axis=0, concat_axis=4, tiled=True).reshape(
             BAND + 1, series, 2, factor_b
         )
-        phase_cos, phase_sin = angles(jnp.ones((1,), jnp.int32), index_b, factor_b)
+        unit_row = lax.optimization_barrier((jnp.ones((1,), jnp.int32), spread))[0]
+        phase_cos, phase_sin = angles(unit_row, index_b, factor_b)
         source = incoming[1:BAND][::-1]
         source_real, source_imag = source[:, :, 0], source[:, :, 1]
         mirror = jnp.stack(
@@ -105,6 +106,11 @@
         sent = jnp.concatenate([spec.reshape(rows_local, series, 2, factor_b)[: BAND + 1], scale_row])
     else:
         sent = whitened
+    if paired:
+        row_ids = jnp.concatenate([k1_ids[: BAND + 1], k1_ids[BAND + 1 :][::-1]])
+    else:
+        row_ids = k1_ids
+    row_ids, turned_index = lax.optimization_barrier((row_ids, factor_b - 1 - index_b, sent))[:2]
     arrived = {}
     for distance in range(REACH, 0, -1):
         arrived[distance] = passed_along(sent, "sta", -distance)
@@ -152,14 +158,12 @@
 
     lag_shape = (slot_total, -1, stations, stations, 2, factor_b)
     if paired:
-        cosine_r, sine_r = angles(factor_b - 1 - index_b, index_b, factor_b)
+        cosine_r, sine_r = angles(turned_index, index_b, factor_b)
         lag_low = matmul(cross[:, : BAND + 1].reshape(-1, 2 * factor_b), inverse_of(cosine_b, sine_b))
         lag_high = matmul(cross[:, BAND + 1 :].reshape(-1, 2 * factor_b), inverse_of(cosine_r, sine_r))
         lag = jnp.concatenate([lag_low.reshape(lag_shape), lag_high.reshape(lag_shape)], axis=1)
-        row_ids = jnp.concatenate([k1_ids[: BAND + 1], k1_ids[BAND + 1 :][::-1]])
     else:
         lag = matmul(cross.reshape(-1, 2 * factor_b), inverse_of(cosine_b, sine_b)).reshape(lag_shape)
-        row_ids = k1_ids
     lag_real, lag_imag = lag[:, :, :, :, 0], lag[:, :, :, :, 1]
     cosine_u, sine_u = angles(row_ids, index_b, SAMPLES)
     turn_real = lag_real * cosine_u[None, :, None, None, :] - lag_imag * sine_u[None, :, None, None, :]

time: 59.9 us -> 55.8 us (0.932)
  other arithmetic: 12.1 us -> 9.65 us
  waiting for transfers between devices: 17.4 us -> 16.6 us
    ppermute x3, waiting for transfers between devices: 12.8 us -> 11.4 us  [passed_along(): return lax.ppermute(block, axis, route)]
    cos x4, other arithmetic: 3.3 us -> 2.04 us  [angles(): return (jnp.cos(radians), jnp.sin(radians))]
    all_to_all x1, waiting for transfers between devices: 0.01 us -> 0.76 us  [local(): lax.all_to_all(arranged, 'tm', split_axis=2, concat_axis=0, tiled=True)]
    unnamed x37 -> x13, local copies, waits for them, and re-layouts: 2.81 us -> 2.35 us
  transfers between devices with their start and end apart: 5 -> 5, of which waited for: 4 -> 5; matrix products, arithmetic and copies ran while one was open for 12% -> 9% of each run, Pallas kernels for 0% -> 0%
where the time goes in v9:
time: 55.8 us; the launch traced here: 55.4 us
  waiting for transfers between devices  16.6 us (30%)
  starting transfers between devices  11.3 us (20%)
  other arithmetic  9.65 us (17%)
  blocking collectives  6.67 us (12%)
  local copies, waits for them, and re-layouts  6.53 us (12%)
  matrix products  3.28 us (6%)
  between operations  1.26 us (2%)
    ppermute x3, waiting for transfers between devices, passed_along(): return lax.ppermute(block, axis, route)  11.4 us
    all_to_all x1, blocking collectives, local(): lax.all_to_all(lag_block, 'tm', split_axis=0, concat_axis=0, tiled=True)  6.67 us
    ppermute x3, starting transfers between devices, passed_along(): return lax.ppermute(block, axis, route)  4.7 us
    all_to_all x1, waiting for transfers between devices, local(): lax.all_to_all(outgoing, 'tm', split_axis=0, concat_axis=4, tiled=True)  4.53 us
    all_to_all x1, starting transfers between devices, local(): lax.all_to_all(outgoing, 'tm', split_axis=0, concat_axis=4, tiled=True)  3.33 us
    all_to_all x1, starting transfers between devices, local(): lax.all_to_all(arranged, 'tm', split_axis=2, concat_axis=0, tiled=True)  3.32 us
    dot_general x4, matrix products, matmul(): jnp.dot(left_mat, right_mat, precision=highest, preferred_element_type=jn...  2.78 us
    unnamed x13, local copies, waits for them, and re-layouts  2.35 us
  transfers between devices with their start and end apart: 5, of which 5 were waited for; matrix products, arithmetic and copies ran while one was open for 9% of the time, Pallas kernels for 0%

profile of v9, /device:TPU:2, one launch (start us, length us, event | category | flops | bytes accessed | tf_op | source)
XLA Modules:
  0.0 55.4 jit_solution(16388946225017321117)
XLA Ops:
  0.0 1.3 %reduce.1 = f32[2,16384]{1,0:T(2,128)S(1)} reduce(f32[2,1,16384]{2,1,0:T(1,128)} %param.3, f32[]{:T(128)} %constant.109), dimensions={1}, to_apply=%param.3.reduce_sub_computation | reduce | bytes 262148 | tf_op args[0]
  1.3 0.1 copy.57
  1.5 0.9 %reshape.370 = f32[4,1,8192]{2,1,0:T(1,128)} reshape(f32[256,2,64]{2,1,0:T(2,128)S(1)} %bitcast.131) | data formatting | bytes 262144
  2.4 3.3 %all-to-all-start = ((f32[4,1,8192]{2,1,0:T(1,128)}), f32[4,1,8192]{2,1,0:T(1,128)S(1)}, u32[]{:S(2)}, u32[]{:S(2)}) async-start(f32[4,1,8192]{2,1,0:T(1,128)} %reshape.370), calls=%async_computation | async-start | bytes 262144 | tf_op jit(solution)/shard_map/all_to_all | solution.py:46
  5.7 1.0 %fusion.48 = (f32[256,256]{0,1:T(8,128)S(1)}, f32[256,256]{0,1:T(8,128)S(1)}) fusion(), kind=kLoop, calls=%fused_computation.93 | loop fusion | flops 983040 | bytes 524288 | tf_op jit(solution)/shard_map/cos | solution.py:28
  6.8 1.0 %fusion.47 = f32[256,256]{0,1:T(8,128)S(1)} fusion(), kind=kLoop, calls=%fused_computation.92 | loop fusion | flops 917504 | bytes 262144 | tf_op jit(solution)/shard_map/sin | solution.py:28
  7.8 0.5 fusion.61
  8.4 0.1 slice.159
  8.5 0.1 pad_add_fusion.1
  8.6 0.1 rev.16
  9.3 0.1 pad_add_fusion
  9.4 0.1 fusion.8
  9.5 0.8 %all-to-all-done = f32[4,1,8192]{2,1,0:T(1,128)S(1)} async-done(((f32[4,1,8192]{2,1,0:T(1,128)}), f32[4,1,8192]{2,1,0:T(1,128)S(1)}, u32[]{:S(2)}, u32[]{:S(2)}) %all-to-all-start) | async-done | bytes 131104 | tf_op jit(solution)/shard_map/all_to_all | solution.py:46
  10.3 0.5 broadcast.512
  10.8 1.0 %reduce.2 = f32[4,8192]{1,0:T(4,128)S(1)} reduce(f32[4,1,8192]{2,1,0:T(1,128)S(1)} %all-to-all-done, f32[]{:T(128)} %broadcast.512), dimensions={1}, to_apply=%all_to_all.25.reduce_sub_computation | reduce | bytes 262148 | tf_op jit(solution)/shard_map/all_to_all | solution.py:46
  11.8 0.2 reshape.371
  12.0 0.2 copy.83
  12.2 0.2 copy.59
  12.4 0.2 reshape.354
  12.6 0.3 fusion.22
  12.9 0.1 copy.60
  13.0 0.1 copy.61
  13.2 0.1 multiply_add_fusion.2
  13.5 0.1 copy.65
  13.6 0.9 %reshape.372 = f32[4,1,8448]{2,1,0:T(1,128)} reshape(f32[4,33,2,2,64]{4,3,2,1,0:T(2,128)S(1)} %copy.65) | data formatting | bytes 270336
  14.5 3.3 %all-to-all-start.1 = ((f32[4,1,8448]{2,1,0:T(1,128)}), f32[4,1,8448]{2,1,0:T(1,128)S(1)}, u32[]{:S(2)}, u32[]{:S(2)}) async-start(f32[4,1,8448]{2,1,0:T(1,128)} %reshape.372), calls=%async_computation.1 | async-start | bytes 270336 | tf_op jit(solution)/shard_map/all_to_all | solution.py:73
  17.9 0.1 pad_add_fusion.2
  17.9 4.5 %all-to-all-done.1 = f32[4,1,8448]{2,1,0:T(1,128)S(1)} async-done(((f32[4,1,8448]{2,1,0:T(1,128)}), f32[4,1,8448]{2,1,0:T(1,128)S(1)}, u32[]{:S(2)}, u32[]{:S(2)}) %all-to-all-start.1) | async-done | bytes 135200 | tf_op jit(solution)/shard_map/all_to_all | solution.py:73
  22.5 1.0 %reduce.3 = f32[4,8448]{1,0:T(4,128)S(1)} reduce(f32[4,1,8448]{2,1,0:T(1,128)S(1)} %all-to-all-done.1, f32[]{:T(128)} %broadcast.512), dimensions={1}, to_apply=%all_to_all.28.reduce_sub_computation | reduce | bytes 270340 | tf_op jit(solution)/shard_map/all_to_all | solution.py:73
  23.5 0.2 reshape.373
  23.7 0.1 copy.66
  23.8 0.1 copy.84
  23.9 0.2 reshape.368
  24.1 0.1 fusion.84
  24.2 0.2 reshape.356
  24.4 0.1 multiply_subtract_fusion.3
  24.6 0.2 maximum_maximum_fusion.1
  24.8 0.7 %fusion.6 = f32[128,512]{1,0:T(8,128)S(1)} fusion(f32[128,512]{1,0:T(8,128)S(1)} %bitcast.141, f32[256,256]{0,1:T(8,128)S(1)} %get-tuple-element.52, f32[256,256]{0,1:T(8,128)S(1)} %fusion.47, f32[256,256]{0,1:T(8,128)S(1)} %get-tuple-element.53), kind=kOutput, calls=%fused_computation.15 | convolution fusion | flops 202113024 | bytes 1310720 | tf_op jit(solution)/shard_map/dot_general | solution.py:32
  25.4 0.2 reshape.358
  25.6 0.1 slice.138
  25.7 0.3 fusion.52
  26.0 1.9 %collective-permute-start = (f32[34,2,2,256]{3,2,1,0:T(2,128)S(1)}, f32[34,2,2,256]{3,2,1,0:T(2,128)S(1)}, u32[]{:S(2)}, u32[]{:S(2)}) collective-permute-start(f32[34,2,2,256]{3,2,1,0:T(2,128)S(1)} %constant_dynamic-update-slice_fusion), channel_id=1, source_target_pairs={{4,0},{8,4},{12,8},{16,12},{20,16},{24,20},{28,24},{5,1},{9,5},{13... | collective-permute-start | bytes 417800 | tf_op jit(solution)/shard_map/ppermute | solution.py:22
  28.0 1.3 %collective-permute-start.1 = (f32[34,2,2,256]{3,2,1,0:T(2,128)S(1)}, f32[34,2,2,256]{3,2,1,0:T(2,128)S(1)}, u32[]{:S(2)}, u32[]{:S(2)}) collective-permute-start(f32[34,2,2,256]{3,2,1,0:T(2,128)S(1)} %constant_dynamic-update-slice_fusion), channel_id=1, source_target_pairs={{8,0},{12,4},{16,8},{20,12},{24,16},{28,20},{9,1},{13,5},{17,9},{2... | collective-permute-start | bytes 417800 | tf_op jit(solution)/shard_map/ppermute | solution.py:22
  29.3 1.5 %collective-permute-start.2 = (f32[34,2,2,256]{3,2,1,0:T(2,128)S(1)}, f32[34,2,2,256]{3,2,1,0:T(2,128)S(1)}, u32[]{:S(2)}, u32[]{:S(2)}) collective-permute-start(f32[34,2,2,256]{3,2,1,0:T(2,128)S(1)} %constant_dynamic-update-slice_fusion), channel_id=1, source_target_pairs={{12,0},{16,4},{20,8},{24,12},{28,16},{13,1},{17,5},{21,9},{25,13},... | collective-permute-start | bytes 417800 | tf_op jit(solution)/shard_map/ppermute | solution.py:22
  30.7 1.0 %fusion.49 = (f32[256,256]{0,1:T(8,128)S(1)}, f32[256,256]{0,1:T(8,128)S(1)}, f32[256,256]{0,1:T(8,128)S(1)}) fusion(s32[256]{0:T(256)S(1)} %iota_subtract_fusion), kind=kLoop, calls=%fused_computation.94 | loop fusion | flops 983040 | bytes 787456 | tf_op jit(solution)/shard_map/sin | solution.py:28
  31.8 0.3 fusion.64
  32.1 0.1 fusion.70
  32.3 0.1 maximum_maximum_fusion
  32.4 2.5 %collective-permute-done = f32[34,2,2,256]{3,2,1,0:T(2,128)S(1)} collective-permute-done((f32[34,2,2,256]{3,2,1,0:T(2,128)S(1)}, f32[34,2,2,256]{3,2,1,0:T(2,128)S(1)}, u32[]{:S(2)}, u32[]{:S(2)}) %collective-permute-start) | collective-permute-done | bytes 139296 | tf_op jit(solution)/shard_map/ppermute | solution.py:22
  35.0 1.1 %collective-permute-done.1 = f32[34,2,2,256]{3,2,1,0:T(2,128)S(1)} collective-permute-done((f32[34,2,2,256]{3,2,1,0:T(2,128)S(1)}, f32[34,2,2,256]{3,2,1,0:T(2,128)S(1)}, u32[]{:S(2)}, u32[]{:S(2)}) %collective-permute-start.1) | collective-permute-done | bytes 139296 | tf_op jit(solution)/shard_map/ppermute | solution.py:22
  36.1 7.7 %collective-permute-done.2 = f32[34,2,2,256]{3,2,1,0:T(2,128)S(1)} collective-permute-done((f32[34,2,2,256]{3,2,1,0:T(2,128)S(1)}, f32[34,2,2,256]{3,2,1,0:T(2,128)S(1)}, u32[]{:S(2)}, u32[]{:S(2)}) %collective-permute-start.2) | collective-permute-done | bytes 139296 | tf_op jit(solution)/shard_map/ppermute | solution.py:22
  43.9 0.2 select_select_fusion.1
  44.1 0.2 rev.14
  44.4 0.2 rev.15
  44.6 0.2 fusion.27
  44.8 0.1 maximum_bitcast_fusion.6
  45.0 0.1 maximum_bitcast_fusion.7
  45.1 0.2 multiply_add_fusion.1
  45.4 1.0 %fusion.13 = f32[3,33,2,2,2,256]{5,1,4,3,2,0:T(8,128)S(1)} fusion(f32[2,256,512,1,1,1]{2,1,0,5,4,3:T(8,128)S(1)} %bitcast.126, f32[3,64,2,2,256]{4,1,3,2,0:T(8,128)S(1)} %get-tuple-element.11, f32[3,64,2,2,256]{4,1,3,2,0:T(8,128)S(1)} %get-tuple-element.12), kind=kOutput, calls=%fused_computation.22 | convolution fusion | flops 623056896 | bytes 3432448 | tf_op jit(solution)/shard_map/dot_general | solution.py:32
  46.4 0.8 %fusion.19 = f32[3,31,2,2,2,256]{5,1,4,3,2,0:T(8,128)S(1)} fusion(f32[2,256,512,1,1,1]{2,1,0,5,4,3:T(8,128)S(1)} %bitcast.127, f32[3,64,2,2,256]{4,1,3,2,0:T(8,128)S(1)} %get-tuple-element.12, f32[3,64,2,2,256]{4,1,3,2,0:T(8,128)S(1)} %get-tuple-element.11), kind=kOutput, calls=%fused_computation.29 | convolution fusion | flops 585295872 | bytes 3383296 | tf_op jit(solution)/shard_map/dot_general | solution.py:32
  47.2 0.3 multiply_subtract_fusion
  47.5 0.5 fusion.4
  48.0 6.7 %all_to_all.35 = f32[4,3,2,2,2,256]{5,4,3,2,1,0:T(2,128)S(1)} all-to-all(f32[4,3,2,2,2,256]{5,4,3,2,1,0:T(2,128)S(1)} %copy.76), channel_id=1, replica_groups=mesh['sta'=8,'tm'=4] {'tm'}, dimensions={0} | all-to-all | bytes 196608 | tf_op jit(solution)/shard_map/all_to_all | solution.py:189
  54.8 0.6 %reshape.361 = f32[3,2,2,512]{3,2,1,0:T(2,128)} reshape(f32[3,2,2,2,256]{4,3,2,1,0:T(2,128)S(1)} %reduce_sum.20) | data formatting | bytes 49152 | tf_op jit(solution)/shard_map/reshape | solution.py:191
  (41 shorter events, 0.8 us)
Async XLA Ops:
  1.3 8.0 %copy-start = (s32[3,2]{0,1:T(2,128)S(1)}, s32[3,2]{0,1:T(2,128)}, u32[]{:S(2)}) copy-start(s32[3,2]{0,1:T(2,128)} %param.4) | copy-start | bytes 76
  2.4 7.9 %all-to-all-start = ((f32[4,1,8192]{2,1,0:T(1,128)}), f32[4,1,8192]{2,1,0:T(1,128)S(1)}, u32[]{:S(2)}, u32[]{:S(2)}) async-start(f32[4,1,8192]{2,1,0:T(1,128)} %reshape.370), calls=%async_computation | async-start | bytes 262144 | tf_op jit(solution)/shard_map/all_to_all | solution.py:46
  14.5 7.9 %all-to-all-start.1 = ((f32[4,1,8448]{2,1,0:T(1,128)}), f32[4,1,8448]{2,1,0:T(1,128)S(1)}, u32[]{:S(2)}, u32[]{:S(2)}) async-start(f32[4,1,8448]{2,1,0:T(1,128)} %reshape.372), calls=%async_computation.1 | async-start | bytes 270336 | tf_op jit(solution)/shard_map/all_to_all | solution.py:73
  26.0 8.9 %collective-permute-start = (f32[34,2,2,256]{3,2,1,0:T(2,128)S(1)}, f32[34,2,2,256]{3,2,1,0:T(2,128)S(1)}, u32[]{:S(2)}, u32[]{:S(2)}) collective-permute-start(f32[34,2,2,256]{3,2,1,0:T(2,128)S(1)} %constant_dynamic-update-slice_fusion), channel_id=1, source_target_pairs={{4,0},{8,4},{12,8},{16,12},{20,16},{24,20},{28,24},{5,1},{9,5},{13... | collective-permute-start | bytes 417800 | tf_op jit(solution)/shard_map/ppermute | solution.py:22
  28.0 8.1 %collective-permute-start.1 = (f32[34,2,2,256]{3,2,1,0:T(2,128)S(1)}, f32[34,2,2,256]{3,2,1,0:T(2,128)S(1)}, u32[]{:S(2)}, u32[]{:S(2)}) collective-permute-start(f32[34,2,2,256]{3,2,1,0:T(2,128)S(1)} %constant_dynamic-update-slice_fusion), channel_id=1, source_target_pairs={{8,0},{12,4},{16,8},{20,12},{24,16},{28,20},{9,1},{13,5},{17,9},{2... | collective-permute-start | bytes 417800 | tf_op jit(solution)/shard_map/ppermute | solution.py:22
  29.3 14.6 %collective-permute-start.2 = (f32[34,2,2,256]{3,2,1,0:T(2,128)S(1)}, f32[34,2,2,256]{3,2,1,0:T(2,128)S(1)}, u32[]{:S(2)}, u32[]{:S(2)}) collective-permute-start(f32[34,2,2,256]{3,2,1,0:T(2,128)S(1)} %constant_dynamic-update-slice_fusion), channel_id=1, source_target_pairs={{12,0},{16,4},{20,8},{24,12},{28,16},{13,1},{17,5},{21,9},{25,13},... | collective-permute-start | bytes 417800 | tf_op jit(solution)/shard_map/ppermute | solution.py:22

commit v10 on v9

--- a/solution.py
+++ b/solution.py
@@ -42,8 +42,10 @@
     rows_local = factor_a // time_devices
     cols_local = factor_b // time_devices
     series = stations * hour_count
-    arranged = records.reshape(series, rows_local, factor_b).transpose(1, 0, 2)
-    spread = lax.all_to_all(arranged, "tm", split_axis=2, concat_axis=0, tiled=True)
+    arranged = records.reshape(series, rows_local, time_devices, cols_local).transpose(2, 1, 0, 3)
+    spread = lax.all_to_all(
+        arranged.reshape(time_devices, -1), "tm", split_axis=0, concat_axis=0, tiled=True
+    ).reshape(factor_a, series, cols_local)
     index_a = jnp.arange(factor_a, dtype=jnp.int32)
     index_b = jnp.arange(factor_b, dtype=jnp.int32)
     paired = rows_local == 2 * BAND and factor_a == 2 * BAND * time_devices
@@ -186,7 +188,9 @@
         preferred_element_type=jnp.float32,
     )
     lag_block = lag_block * live_mask[None, :, None, None, None, None]
-    gathered = lax.all_to_all(lag_block, "tm", split_axis=0, concat_axis=0, tiled=True)
+    gathered = lax.all_to_all(
+        lag_block.reshape(time_devices, -1), "tm", split_axis=0, concat_axis=0, tiled=True
+    )
     total = jnp.sum(gathered, axis=0)
     return total.reshape(slot_total, stations, stations, 2 * LAGS * factor_b // time_devices)
 

time: 55.8 us -> 54.5 us (0.977)
  other arithmetic: 9.65 us -> 8.73 us
    unnamed x13 -> x10, local copies, waits for them, and re-layouts: 2.35 us -> 1.21 us
    all_to_all x1 -> x0, other arithmetic: 0.98 us -> none  [local(): lax.all_to_all(arranged, 'tm', split_axis=2, concat_axis=0, tiled=True)]
where the time goes in v10:
time: 54.5 us; the launch traced here: 54 us
  waiting for transfers between devices  16.6 us (30%)
  starting transfers between devices  11.4 us (21%)
  other arithmetic  8.73 us (16%)
  blocking collectives  6.67 us (12%)
  local copies, waits for them, and re-layouts  6.11 us (11%)
  matrix products  3.28 us (6%)
  between operations  1.24 us (2%)
    ppermute x3, waiting for transfers between devices, passed_along(): return lax.ppermute(block, axis, route)  11.4 us
    all_to_all x1, blocking collectives, local(): lax.all_to_all(lag_block.reshape(time_devices, -1), 'tm', split_axis=0, c...  6.67 us
    ppermute x3, starting transfers between devices, passed_along(): return lax.ppermute(block, axis, route)  4.7 us
    all_to_all x1, waiting for transfers between devices, local(): lax.all_to_all(outgoing, 'tm', split_axis=0, concat_axis=4, tiled=True)  4.53 us
    all_to_all x1, starting transfers between devices, local(): lax.all_to_all(outgoing, 'tm', split_axis=0, concat_axis=4, tiled=True)  3.33 us
    all_to_all x1, starting transfers between devices, local(): lax.all_to_all(arranged.reshape(time_devices, -1), 'tm', split_axis=0, co...  3.32 us
    dot_general x4, matrix products, matmul(): jnp.dot(left_mat, right_mat, precision=highest, preferred_element_type=jn...  2.78 us
    sin x3, other arithmetic, angles(): return (jnp.cos(radians), jnp.sin(radians))  2.07 us
  transfers between devices with their start and end apart: 5, of which 5 were waited for; matrix products, arithmetic and copies ran while one was open for 9% of the time, Pallas kernels for 0%

profile of v10, /device:TPU:2, one launch (start us, length us, event | category | flops | bytes accessed | tf_op | source)
XLA Modules:
  0.0 54.0 jit_solution(3913258631095211691)
XLA Ops:
  0.0 1.3 %reduce.2 = f32[2,16384]{1,0:T(2,128)S(1)} reduce(f32[2,1,16384]{2,1,0:T(1,128)} %param.3, f32[]{:T(128)} %constant.109), dimensions={1}, to_apply=%param.3.reduce_sub_computation | reduce | bytes 262148 | tf_op args[0]
  1.3 0.2 reshape.359
  1.5 0.2 copy.63
  1.7 0.9 %all_to_all.30 = f32[4,1,8192]{2,1,0:T(1,128)} reshape(f32[4,64,2,64]{3,2,1,0:T(2,128)S(1)} %bitcast.124) | data formatting | bytes 262144 | tf_op jit(solution)/shard_map/all_to_all | solution.py:46
  2.7 3.3 %all-to-all-start = ((f32[4,1,8192]{2,1,0:T(1,128)}), f32[4,1,8192]{2,1,0:T(1,128)S(1)}, u32[]{:S(2)}, u32[]{:S(2)}) async-start(f32[4,1,8192]{2,1,0:T(1,128)} %all_to_all.30), calls=%async_computation | async-start | bytes 262144 | tf_op jit(solution)/shard_map/all_to_all | solution.py:46
  6.0 1.0 %fusion.47 = (f32[256,256]{0,1:T(8,128)S(1)}, f32[256,256]{0,1:T(8,128)S(1)}) fusion(), kind=kLoop, calls=%fused_computation.92 | loop fusion | flops 983040 | bytes 524288 | tf_op jit(solution)/shard_map/cos | solution.py:28
  7.1 1.0 %fusion.46 = f32[256,256]{0,1:T(8,128)S(1)} fusion(), kind=kLoop, calls=%fused_computation.91 | loop fusion | flops 917504 | bytes 262144 | tf_op jit(solution)/shard_map/sin | solution.py:28
  8.1 0.5 fusion.60
  8.7 0.1 slice.159
  8.8 0.1 pad_add_fusion.1
  8.8 0.1 rev.16
  9.6 0.1 pad_add_fusion
  9.7 0.1 fusion.7
  9.8 0.8 %all-to-all-done = f32[4,1,8192]{2,1,0:T(1,128)S(1)} async-done(((f32[4,1,8192]{2,1,0:T(1,128)}), f32[4,1,8192]{2,1,0:T(1,128)S(1)}, u32[]{:S(2)}, u32[]{:S(2)}) %all-to-all-start) | async-done | bytes 131104 | tf_op jit(solution)/shard_map/all_to_all | solution.py:46
  10.6 0.3 fusion.21
  10.9 0.1 copy.26
  11.1 0.1 copy.27
  11.2 0.1 multiply_add_fusion.2
  11.5 0.1 copy.31
  11.6 0.9 %reshape.375 = f32[4,1,8448]{2,1,0:T(1,128)} reshape(f32[4,33,2,2,64]{4,3,2,1,0:T(2,128)S(1)} %copy.31) | data formatting | bytes 270336
  12.6 3.3 %all-to-all-start.1 = ((f32[4,1,8448]{2,1,0:T(1,128)}), f32[4,1,8448]{2,1,0:T(1,128)S(1)}, u32[]{:S(2)}, u32[]{:S(2)}) async-start(f32[4,1,8448]{2,1,0:T(1,128)} %reshape.375), calls=%async_computation.1 | async-start | bytes 270336 | tf_op jit(solution)/shard_map/all_to_all | solution.py:75
  15.9 0.1 pad_add_fusion.2
  16.0 4.5 %all-to-all-done.1 = f32[4,1,8448]{2,1,0:T(1,128)S(1)} async-done(((f32[4,1,8448]{2,1,0:T(1,128)}), f32[4,1,8448]{2,1,0:T(1,128)S(1)}, u32[]{:S(2)}, u32[]{:S(2)}) %all-to-all-start.1) | async-done | bytes 135200 | tf_op jit(solution)/shard_map/all_to_all | solution.py:75
  20.5 0.5 broadcast.512
  21.0 1.0 %reduce.3 = f32[4,8448]{1,0:T(4,128)S(1)} reduce(f32[4,1,8448]{2,1,0:T(1,128)S(1)} %all-to-all-done.1, f32[]{:T(128)} %broadcast.512), dimensions={1}, to_apply=%all_to_all.25.reduce_sub_computation | reduce | bytes 270340 | tf_op jit(solution)/shard_map/all_to_all | solution.py:75
  22.0 0.2 reshape.376
  22.3 0.1 copy.32
  22.3 0.1 copy.49
  22.4 0.2 reshape.373
  22.6 0.1 fusion.83
  22.7 0.2 reshape.361
  22.9 0.1 multiply_subtract_fusion.3
  23.1 0.2 maximum_maximum_fusion.1
  23.3 0.6 %fusion.5 = f32[128,512]{1,0:T(8,128)S(1)} fusion(f32[128,512]{1,0:T(8,128)S(1)} %bitcast.131, f32[256,256]{0,1:T(8,128)S(1)} %get-tuple-element.52, f32[256,256]{0,1:T(8,128)S(1)} %fusion.46, f32[256,256]{0,1:T(8,128)S(1)} %get-tuple-element.53), kind=kOutput, calls=%fused_computation.14 | convolution fusion | flops 202113024 | bytes 1310720 | tf_op jit(solution)/shard_map/dot_general | solution.py:32
  24.0 0.2 reshape.363
  24.1 0.1 slice.138
  24.3 0.3 fusion.51
  24.6 1.9 %collective-permute-start = (f32[34,2,2,256]{3,2,1,0:T(2,128)S(1)}, f32[34,2,2,256]{3,2,1,0:T(2,128)S(1)}, u32[]{:S(2)}, u32[]{:S(2)}) collective-permute-start(f32[34,2,2,256]{3,2,1,0:T(2,128)S(1)} %constant_dynamic-update-slice_fusion), channel_id=1, source_target_pairs={{4,0},{8,4},{12,8},{16,12},{20,16},{24,20},{28,24},{5,1},{9,5},{13... | collective-permute-start | bytes 417800 | tf_op jit(solution)/shard_map/ppermute | solution.py:22
  26.5 1.3 %collective-permute-start.1 = (f32[34,2,2,256]{3,2,1,0:T(2,128)S(1)}, f32[34,2,2,256]{3,2,1,0:T(2,128)S(1)}, u32[]{:S(2)}, u32[]{:S(2)}) collective-permute-start(f32[34,2,2,256]{3,2,1,0:T(2,128)S(1)} %constant_dynamic-update-slice_fusion), channel_id=1, source_target_pairs={{8,0},{12,4},{16,8},{20,12},{24,16},{28,20},{9,1},{13,5},{17,9},{2... | collective-permute-start | bytes 417800 | tf_op jit(solution)/shard_map/ppermute | solution.py:22
  27.8 1.5 %collective-permute-start.2 = (f32[34,2,2,256]{3,2,1,0:T(2,128)S(1)}, f32[34,2,2,256]{3,2,1,0:T(2,128)S(1)}, u32[]{:S(2)}, u32[]{:S(2)}) collective-permute-start(f32[34,2,2,256]{3,2,1,0:T(2,128)S(1)} %constant_dynamic-update-slice_fusion), channel_id=1, source_target_pairs={{12,0},{16,4},{20,8},{24,12},{28,16},{13,1},{17,5},{21,9},{25,13},... | collective-permute-start | bytes 417800 | tf_op jit(solution)/shard_map/ppermute | solution.py:22
  29.3 1.0 %fusion.48 = (f32[256,256]{0,1:T(8,128)S(1)}, f32[256,256]{0,1:T(8,128)S(1)}, f32[256,256]{0,1:T(8,128)S(1)}) fusion(s32[256]{0:T(256)S(1)} %iota_subtract_fusion), kind=kLoop, calls=%fused_computation.93 | loop fusion | flops 983040 | bytes 787456 | tf_op jit(solution)/shard_map/sin | solution.py:28
  30.3 0.3 fusion.63
  30.7 0.1 fusion.69
  30.8 0.1 maximum_maximum_fusion
  30.9 2.5 %collective-permute-done = f32[34,2,2,256]{3,2,1,0:T(2,128)S(1)} collective-permute-done((f32[34,2,2,256]{3,2,1,0:T(2,128)S(1)}, f32[34,2,2,256]{3,2,1,0:T(2,128)S(1)}, u32[]{:S(2)}, u32[]{:S(2)}) %collective-permute-start) | collective-permute-done | bytes 139296 | tf_op jit(solution)/shard_map/ppermute | solution.py:22
  33.5 1.1 %collective-permute-done.1 = f32[34,2,2,256]{3,2,1,0:T(2,128)S(1)} collective-permute-done((f32[34,2,2,256]{3,2,1,0:T(2,128)S(1)}, f32[34,2,2,256]{3,2,1,0:T(2,128)S(1)}, u32[]{:S(2)}, u32[]{:S(2)}) %collective-permute-start.1) | collective-permute-done | bytes 139296 | tf_op jit(solution)/shard_map/ppermute | solution.py:22
  34.6 7.7 %collective-permute-done.2 = f32[34,2,2,256]{3,2,1,0:T(2,128)S(1)} collective-permute-done((f32[34,2,2,256]{3,2,1,0:T(2,128)S(1)}, f32[34,2,2,256]{3,2,1,0:T(2,128)S(1)}, u32[]{:S(2)}, u32[]{:S(2)}) %collective-permute-start.2) | collective-permute-done | bytes 139296 | tf_op jit(solution)/shard_map/ppermute | solution.py:22
  42.4 0.2 select_select_fusion.1
  42.7 0.2 rev.14
  42.9 0.2 rev.15
  43.2 0.2 fusion.26
  43.4 0.1 maximum_bitcast_fusion.4
  43.4 0.1 slice_bitcast_fusion.3
  43.5 0.1 maximum_bitcast_fusion.5
  43.6 0.1 slice_bitcast_fusion.2
  43.7 0.2 multiply_add_fusion.1
  43.9 1.0 %fusion.12 = f32[3,33,2,2,2,256]{5,1,4,3,2,0:T(8,128)S(1)} fusion(f32[2,256,512,1,1,1]{2,1,0,5,4,3:T(8,128)S(1)} %bitcast.118, f32[3,64,2,2,256]{4,1,3,2,0:T(8,128)S(1)} %get-tuple-element.11, f32[3,64,2,2,256]{4,1,3,2,0:T(8,128)S(1)} %get-tuple-element.12), kind=kOutput, calls=%fused_computation.21 | convolution fusion | flops 623056896 | bytes 3432448 | tf_op jit(solution)/shard_map/dot_general | solution.py:32
  44.9 0.8 %fusion.18 = f32[3,31,2,2,2,256]{5,1,4,3,2,0:T(8,128)S(1)} fusion(f32[2,256,512,1,1,1]{2,1,0,5,4,3:T(8,128)S(1)} %bitcast.119, f32[3,64,2,2,256]{4,1,3,2,0:T(8,128)S(1)} %get-tuple-element.12, f32[3,64,2,2,256]{4,1,3,2,0:T(8,128)S(1)} %get-tuple-element.11), kind=kOutput, calls=%fused_computation.28 | convolution fusion | flops 585295872 | bytes 3383296 | tf_op jit(solution)/shard_map/dot_general | solution.py:32
  45.7 0.3 multiply_subtract_fusion
  46.0 0.5 fusion.3
  46.5 0.1 copy.42
  46.6 6.7 %all_to_all.34 = f32[4,1,6144]{2,1,0:T(1,128)S(1)} all-to-all(f32[4,1,6144]{2,1,0:T(1,128)S(1)} %copy.42), channel_id=1, replica_groups=mesh['sta'=8,'tm'=4] {'tm'}, dimensions={0} | all-to-all | bytes 196608 | tf_op jit(solution)/shard_map/all_to_all | solution.py:191
  53.3 0.1 reduce_sum.20
  53.4 0.6 %reshape.366 = f32[3,2,2,512]{3,2,1,0:T(2,128)} reshape(f32[6144]{0:T(1024)S(1)} %reduce_sum.20) | data formatting | bytes 49152 | tf_op jit(solution)/shard_map/reshape | solution.py:195
  (36 shorter events, 0.6 us)
Async XLA Ops:
  1.5 8.1 %copy-start = (s32[3,2]{0,1:T(2,128)S(1)}, s32[3,2]{0,1:T(2,128)}, u32[]{:S(2)}) copy-start(s32[3,2]{0,1:T(2,128)} %param.4) | copy-start | bytes 76
  2.7 7.9 %all-to-all-start = ((f32[4,1,8192]{2,1,0:T(1,128)}), f32[4,1,8192]{2,1,0:T(1,128)S(1)}, u32[]{:S(2)}, u32[]{:S(2)}) async-start(f32[4,1,8192]{2,1,0:T(1,128)} %all_to_all.30), calls=%async_computation | async-start | bytes 262144 | tf_op jit(solution)/shard_map/all_to_all | solution.py:46
  12.6 7.9 %all-to-all-start.1 = ((f32[4,1,8448]{2,1,0:T(1,128)}), f32[4,1,8448]{2,1,0:T(1,128)S(1)}, u32[]{:S(2)}, u32[]{:S(2)}) async-start(f32[4,1,8448]{2,1,0:T(1,128)} %reshape.375), calls=%async_computation.1 | async-start | bytes 270336 | tf_op jit(solution)/shard_map/all_to_all | solution.py:75
  24.6 8.9 %collective-permute-start = (f32[34,2,2,256]{3,2,1,0:T(2,128)S(1)}, f32[34,2,2,256]{3,2,1,0:T(2,128)S(1)}, u32[]{:S(2)}, u32[]{:S(2)}) collective-permute-start(f32[34,2,2,256]{3,2,1,0:T(2,128)S(1)} %constant_dynamic-update-slice_fusion), channel_id=1, source_target_pairs={{4,0},{8,4},{12,8},{16,12},{20,16},{24,20},{28,24},{5,1},{9,5},{13... | collective-permute-start | bytes 417800 | tf_op jit(solution)/shard_map/ppermute | solution.py:22
  26.5 8.1 %collective-permute-start.1 = (f32[34,2,2,256]{3,2,1,0:T(2,128)S(1)}, f32[34,2,2,256]{3,2,1,0:T(2,128)S(1)}, u32[]{:S(2)}, u32[]{:S(2)}) collective-permute-start(f32[34,2,2,256]{3,2,1,0:T(2,128)S(1)} %constant_dynamic-update-slice_fusion), channel_id=1, source_target_pairs={{8,0},{12,4},{16,8},{20,12},{24,16},{28,20},{9,1},{13,5},{17,9},{2... | collective-permute-start | bytes 417800 | tf_op jit(solution)/shard_map/ppermute | solution.py:22
  27.8 14.6 %collective-permute-start.2 = (f32[34,2,2,256]{3,2,1,0:T(2,128)S(1)}, f32[34,2,2,256]{3,2,1,0:T(2,128)S(1)}, u32[]{:S(2)}, u32[]{:S(2)}) collective-permute-start(f32[34,2,2,256]{3,2,1,0:T(2,128)S(1)} %constant_dynamic-update-slice_fusion), channel_id=1, source_target_pairs={{12,0},{16,4},{20,8},{24,12},{28,16},{13,1},{17,5},{21,9},{25,13},... | collective-permute-start | bytes 417800 | tf_op jit(solution)/shard_map/ppermute | solution.py:22

commit v11 on v10

--- a/solution.py
+++ b/solution.py
@@ -72,8 +72,11 @@
         bands = twisted.reshape(2, time_devices, BAND, series, 2, cols_local)
         grouped = jnp.stack([bands[0], bands[1][::-1]], axis=1)
         outgoing = grouped.reshape(time_devices, rows_local, series, 2, cols_local)[:, : BAND + 1]
-        incoming = lax.all_to_all(outgoing, "tm", split_axis=0, concat_axis=4, tiled=True).reshape(
-            BAND + 1, series, 2, factor_b
+        incoming = (
+            lax.all_to_all(outgoing.reshape(time_devices, -1), "tm", split_axis=0, concat_axis=0, tiled=True)
+            .reshape(time_devices, BAND + 1, series, 2, cols_local)
+            .transpose(1, 2, 3, 0, 4)
+            .reshape(BAND + 1, series, 2, factor_b)
         )
         unit_row = lax.optimization_barrier((jnp.ones((1,), jnp.int32), spread))[0]
         phase_cos, phase_sin = angles(unit_row, index_b, factor_b)

time: 54.5 us -> 53.3 us (0.978)
  other arithmetic: 8.73 us -> 8.08 us
    unnamed x10 -> x8, local copies, waits for them, and re-layouts: 1.21 us -> 0.06 us
    all_to_all x1, other arithmetic: 1 us -> 0.35 us  [local(): lax.all_to_all(outgoing.reshape(time_devices, -1), 'tm', split_axis=0, co...]
where the time goes in v11:
time: 53.3 us; the launch traced here: 52.9 us
  waiting for transfers between devices  16.7 us (31%)
  starting transfers between devices  11.3 us (21%)
  other arithmetic  8.08 us (15%)
  blocking collectives  6.67 us (13%)
  local copies, waits for them, and re-layouts  5.6 us (11%)
  matrix products  3.28 us (6%)
  between operations  1.24 us (2%)
    ppermute x3, waiting for transfers between devices, passed_along(): return lax.ppermute(block, axis, route)  11.4 us
    all_to_all x1, blocking collectives, local(): lax.all_to_all(lag_block.reshape(time_devices, -1), 'tm', split_axis=0, c...  6.67 us
    ppermute x3, starting transfers between devices, passed_along(): return lax.ppermute(block, axis, route)  4.7 us
    all_to_all x1, waiting for transfers between devices, local(): lax.all_to_all(outgoing.reshape(time_devices, -1), 'tm', split_axis=0, co...  4.53 us
    all_to_all x1, starting transfers between devices, local(): lax.all_to_all(outgoing.reshape(time_devices, -1), 'tm', split_axis=0, co...  3.33 us
    all_to_all x1, starting transfers between devices, local(): lax.all_to_all(arranged.reshape(time_devices, -1), 'tm', split_axis=0, co...  3.32 us
    dot_general x4, matrix products, matmul(): jnp.dot(left_mat, right_mat, precision=highest, preferred_element_type=jn...  2.78 us
    sin x3, other arithmetic, angles(): return (jnp.cos(radians), jnp.sin(radians))  2.07 us
  transfers between devices with their start and end apart: 5, of which 5 were waited for; matrix products, arithmetic and copies ran while one was open for 9% of the time, Pallas kernels for 0%

profile of v11, /device:TPU:2, one launch (start us, length us, event | category | flops | bytes accessed | tf_op | source)
XLA Modules:
  0.0 52.9 jit_solution(10287683303308234244)
XLA Ops:
  0.0 1.3 %reduce.2 = f32[2,16384]{1,0:T(2,128)S(1)} reduce(f32[2,1,16384]{2,1,0:T(1,128)} %param.3, f32[]{:T(128)} %constant.109), dimensions={1}, to_apply=%param.3.reduce_sub_computation | reduce | bytes 262148 | tf_op args[0]
  1.3 0.2 reshape.366
  1.5 0.2 copy.79
  1.7 0.9 %all_to_all.24 = f32[4,1,8192]{2,1,0:T(1,128)} reshape(f32[4,64,2,64]{3,2,1,0:T(2,128)S(1)} %bitcast.122) | data formatting | bytes 262144 | tf_op jit(solution)/shard_map/all_to_all | solution.py:46
  2.7 3.3 %all-to-all-start = ((f32[4,1,8192]{2,1,0:T(1,128)}), f32[4,1,8192]{2,1,0:T(1,128)S(1)}, u32[]{:S(2)}, u32[]{:S(2)}) async-start(f32[4,1,8192]{2,1,0:T(1,128)} %all_to_all.24), calls=%async_computation | async-start | bytes 262144 | tf_op jit(solution)/shard_map/all_to_all | solution.py:46
  6.0 1.0 %fusion.47 = (f32[256,256]{0,1:T(8,128)S(1)}, f32[256,256]{0,1:T(8,128)S(1)}) fusion(), kind=kLoop, calls=%fused_computation.92 | loop fusion | flops 983040 | bytes 524288 | tf_op jit(solution)/shard_map/cos | solution.py:28
  7.1 1.0 %fusion.46 = f32[256,256]{0,1:T(8,128)S(1)} fusion(), kind=kLoop, calls=%fused_computation.91 | loop fusion | flops 917504 | bytes 262144 | tf_op jit(solution)/shard_map/sin | solution.py:28
  8.1 0.5 %fusion.60 = (f32[256,64]{1,0:T(8,128)S(1)}, f32[256,64]{1,0:T(8,128)S(1)}) fusion(s32[64]{0:T(128)S(1)} %iota_add_fusion.2), kind=kLoop, calls=%fused_computation.108 | loop fusion | flops 229376 | bytes 131328 | tf_op jit(solution)/shard_map/cos | solution.py:28
  8.7 0.1 slice.159
  8.8 0.1 pad_add_fusion.1
  8.8 0.1 rev.16
  9.6 0.1 pad_add_fusion
  9.7 0.1 fusion.7
  9.8 0.8 %all-to-all-done = f32[4,1,8192]{2,1,0:T(1,128)S(1)} async-done(((f32[4,1,8192]{2,1,0:T(1,128)}), f32[4,1,8192]{2,1,0:T(1,128)S(1)}, u32[]{:S(2)}, u32[]{:S(2)}) %all-to-all-start) | async-done | bytes 131104 | tf_op jit(solution)/shard_map/all_to_all | solution.py:46
  10.6 0.3 fusion.21
  10.9 0.1 copy.41
  11.1 0.1 copy.42
  11.2 0.1 multiply_add_fusion.2
  11.3 0.1 pad_maximum_fusion.7
  11.5 0.1 copy.46
  11.6 0.9 %all_to_all.25 = f32[4,1,8448]{2,1,0:T(1,128)} reshape(f32[4,33,2,2,64]{4,3,2,1,0:T(2,128)S(1)} %copy.46) | data formatting | bytes 270336 | tf_op jit(solution)/shard_map/all_to_all | solution.py:76
  12.6 3.3 %all-to-all-start.1 = ((f32[4,1,8448]{2,1,0:T(1,128)}), f32[4,1,8448]{2,1,0:T(1,128)S(1)}, u32[]{:S(2)}, u32[]{:S(2)}) async-start(f32[4,1,8448]{2,1,0:T(1,128)} %all_to_all.25), calls=%async_computation.1 | async-start | bytes 270336 | tf_op jit(solution)/shard_map/all_to_all | solution.py:76
  15.9 0.1 pad_add_fusion.2
  16.0 4.5 %all-to-all-done.1 = f32[4,1,8448]{2,1,0:T(1,128)S(1)} async-done(((f32[4,1,8448]{2,1,0:T(1,128)}), f32[4,1,8448]{2,1,0:T(1,128)S(1)}, u32[]{:S(2)}, u32[]{:S(2)}) %all-to-all-start.1) | async-done | bytes 135200 | tf_op jit(solution)/shard_map/all_to_all | solution.py:76
  20.5 0.4 reduce.3
  20.9 0.2 reshape.368
  21.1 0.1 copy.48
  21.2 0.1 copy.65
  21.3 0.2 reshape.381
  21.5 0.1 fusion.83
  21.6 0.2 reshape.369
  21.8 0.1 multiply_subtract_fusion.3
  21.9 0.2 maximum_maximum_fusion.1
  22.1 0.6 %fusion.5 = f32[128,512]{1,0:T(8,128)S(1)} fusion(f32[128,512]{1,0:T(8,128)S(1)} %bitcast.129, f32[256,256]{0,1:T(8,128)S(1)} %get-tuple-element.52, f32[256,256]{0,1:T(8,128)S(1)} %fusion.46, f32[256,256]{0,1:T(8,128)S(1)} %get-tuple-element.53), kind=kOutput, calls=%fused_computation.14 | convolution fusion | flops 202113024 | bytes 1310720 | tf_op jit(solution)/shard_map/dot_general | solution.py:32
  22.8 0.2 reshape.371
  23.0 0.1 slice.138
  23.1 0.3 fusion.51
  23.4 1.9 %collective-permute-start = (f32[34,2,2,256]{3,2,1,0:T(2,128)S(1)}, f32[34,2,2,256]{3,2,1,0:T(2,128)S(1)}, u32[]{:S(2)}, u32[]{:S(2)}) collective-permute-start(f32[34,2,2,256]{3,2,1,0:T(2,128)S(1)} %constant_dynamic-update-slice_fusion), channel_id=1, source_target_pairs={{4,0},{8,4},{12,8},{16,12},{20,16},{24,20},{28,24},{5,1},{9,5},{13... | collective-permute-start | bytes 417800 | tf_op jit(solution)/shard_map/ppermute | solution.py:22
  25.3 1.3 %collective-permute-start.1 = (f32[34,2,2,256]{3,2,1,0:T(2,128)S(1)}, f32[34,2,2,256]{3,2,1,0:T(2,128)S(1)}, u32[]{:S(2)}, u32[]{:S(2)}) collective-permute-start(f32[34,2,2,256]{3,2,1,0:T(2,128)S(1)} %constant_dynamic-update-slice_fusion), channel_id=1, source_target_pairs={{8,0},{12,4},{16,8},{20,12},{24,16},{28,20},{9,1},{13,5},{17,9},{2... | collective-permute-start | bytes 417800 | tf_op jit(solution)/shard_map/ppermute | solution.py:22
  26.6 1.5 %collective-permute-start.2 = (f32[34,2,2,256]{3,2,1,0:T(2,128)S(1)}, f32[34,2,2,256]{3,2,1,0:T(2,128)S(1)}, u32[]{:S(2)}, u32[]{:S(2)}) collective-permute-start(f32[34,2,2,256]{3,2,1,0:T(2,128)S(1)} %constant_dynamic-update-slice_fusion), channel_id=1, source_target_pairs={{12,0},{16,4},{20,8},{24,12},{28,16},{13,1},{17,5},{21,9},{25,13},... | collective-permute-start | bytes 417800 | tf_op jit(solution)/shard_map/ppermute | solution.py:22
  28.1 1.0 %fusion.48 = (f32[256,256]{0,1:T(8,128)S(1)}, f32[256,256]{0,1:T(8,128)S(1)}, f32[256,256]{0,1:T(8,128)S(1)}) fusion(s32[256]{0:T(256)S(1)} %iota_subtract_fusion), kind=kLoop, calls=%fused_computation.93 | loop fusion | flops 983040 | bytes 787456 | tf_op jit(solution)/shard_map/sin | solution.py:28
  29.2 0.3 fusion.63
  29.5 0.1 fusion.69
  29.7 0.1 maximum_maximum_fusion
  29.8 2.5 %collective-permute-done = f32[34,2,2,256]{3,2,1,0:T(2,128)S(1)} collective-permute-done((f32[34,2,2,256]{3,2,1,0:T(2,128)S(1)}, f32[34,2,2,256]{3,2,1,0:T(2,128)S(1)}, u32[]{:S(2)}, u32[]{:S(2)}) %collective-permute-start) | collective-permute-done | bytes 139296 | tf_op jit(solution)/shard_map/ppermute | solution.py:22
  32.4 1.1 %collective-permute-done.1 = f32[34,2,2,256]{3,2,1,0:T(2,128)S(1)} collective-permute-done((f32[34,2,2,256]{3,2,1,0:T(2,128)S(1)}, f32[34,2,2,256]{3,2,1,0:T(2,128)S(1)}, u32[]{:S(2)}, u32[]{:S(2)}) %collective-permute-start.1) | collective-permute-done | bytes 139296 | tf_op jit(solution)/shard_map/ppermute | solution.py:22
  33.5 7.7 %collective-permute-done.2 = f32[34,2,2,256]{3,2,1,0:T(2,128)S(1)} collective-permute-done((f32[34,2,2,256]{3,2,1,0:T(2,128)S(1)}, f32[34,2,2,256]{3,2,1,0:T(2,128)S(1)}, u32[]{:S(2)}, u32[]{:S(2)}) %collective-permute-start.2) | collective-permute-done | bytes 139296 | tf_op jit(solution)/shard_map/ppermute | solution.py:22
  41.2 0.2 select_select_fusion.1
  41.5 0.2 rev.14
  41.7 0.2 rev.15
  42.0 0.2 fusion.26
  42.2 0.1 maximum_bitcast_fusion.4
  42.3 0.1 slice_bitcast_fusion.3
  42.4 0.1 maximum_bitcast_fusion.5
  42.5 0.1 slice_bitcast_fusion.2
  42.5 0.2 multiply_add_fusion.1
  42.7 1.0 %fusion.12 = f32[3,33,2,2,2,256]{5,1,4,3,2,0:T(8,128)S(1)} fusion(f32[2,256,512,1,1,1]{2,1,0,5,4,3:T(8,128)S(1)} %bitcast.116, f32[3,64,2,2,256]{4,1,3,2,0:T(8,128)S(1)} %get-tuple-element.11, f32[3,64,2,2,256]{4,1,3,2,0:T(8,128)S(1)} %get-tuple-element.12), kind=kOutput, calls=%fused_computation.21 | convolution fusion | flops 623056896 | bytes 3432448 | tf_op jit(solution)/shard_map/dot_general | solution.py:32
  43.7 0.8 %fusion.18 = f32[3,31,2,2,2,256]{5,1,4,3,2,0:T(8,128)S(1)} fusion(f32[2,256,512,1,1,1]{2,1,0,5,4,3:T(8,128)S(1)} %bitcast.117, f32[3,64,2,2,256]{4,1,3,2,0:T(8,128)S(1)} %get-tuple-element.12, f32[3,64,2,2,256]{4,1,3,2,0:T(8,128)S(1)} %get-tuple-element.11), kind=kOutput, calls=%fused_computation.28 | convolution fusion | flops 585295872 | bytes 3383296 | tf_op jit(solution)/shard_map/dot_general | solution.py:32
  44.6 0.3 multiply_subtract_fusion
  44.9 0.5 fusion.3
  45.4 0.1 copy.58
  45.5 6.7 %all_to_all.29 = f32[4,1,6144]{2,1,0:T(1,128)S(1)} all-to-all(f32[4,1,6144]{2,1,0:T(1,128)S(1)} %copy.58), channel_id=1, replica_groups=mesh['sta'=8,'tm'=4] {'tm'}, dimensions={0} | all-to-all | bytes 196608 | tf_op jit(solution)/shard_map/all_to_all | solution.py:194
  52.1 0.1 reduce_sum.20
  52.2 0.6 %reshape.374 = f32[3,2,2,512]{3,2,1,0:T(2,128)} reshape(f32[6144]{0:T(1024)S(1)} %reduce_sum.20) | data formatting | bytes 49152 | tf_op jit(solution)/shard_map/reshape | solution.py:198
  (35 shorter events, 0.6 us)
Async XLA Ops:
  1.5 8.1 %copy-start = (s32[3,2]{0,1:T(2,128)S(1)}, s32[3,2]{0,1:T(2,128)}, u32[]{:S(2)}) copy-start(s32[3,2]{0,1:T(2,128)} %param.4) | copy-start | bytes 76
  2.7 7.9 %all-to-all-start = ((f32[4,1,8192]{2,1,0:T(1,128)}), f32[4,1,8192]{2,1,0:T(1,128)S(1)}, u32[]{:S(2)}, u32[]{:S(2)}) async-start(f32[4,1,8192]{2,1,0:T(1,128)} %all_to_all.24), calls=%async_computation | async-start | bytes 262144 | tf_op jit(solution)/shard_map/all_to_all | solution.py:46
  12.6 7.9 %all-to-all-start.1 = ((f32[4,1,8448]{2,1,0:T(1,128)}), f32[4,1,8448]{2,1,0:T(1,128)S(1)}, u32[]{:S(2)}, u32[]{:S(2)}) async-start(f32[4,1,8448]{2,1,0:T(1,128)} %all_to_all.25), calls=%async_computation.1 | async-start | bytes 270336 | tf_op jit(solution)/shard_map/all_to_all | solution.py:76
  23.4 8.9 %collective-permute-start = (f32[34,2,2,256]{3,2,1,0:T(2,128)S(1)}, f32[34,2,2,256]{3,2,1,0:T(2,128)S(1)}, u32[]{:S(2)}, u32[]{:S(2)}) collective-permute-start(f32[34,2,2,256]{3,2,1,0:T(2,128)S(1)} %constant_dynamic-update-slice_fusion), channel_id=1, source_target_pairs={{4,0},{8,4},{12,8},{16,12},{20,16},{24,20},{28,24},{5,1},{9,5},{13... | collective-permute-start | bytes 417800 | tf_op jit(solution)/shard_map/ppermute | solution.py:22
  25.3 8.1 %collective-permute-start.1 = (f32[34,2,2,256]{3,2,1,0:T(2,128)S(1)}, f32[34,2,2,256]{3,2,1,0:T(2,128)S(1)}, u32[]{:S(2)}, u32[]{:S(2)}) collective-permute-start(f32[34,2,2,256]{3,2,1,0:T(2,128)S(1)} %constant_dynamic-update-slice_fusion), channel_id=1, source_target_pairs={{8,0},{12,4},{16,8},{20,12},{24,16},{28,20},{9,1},{13,5},{17,9},{2... | collective-permute-start | bytes 417800 | tf_op jit(solution)/shard_map/ppermute | solution.py:22
  26.6 14.6 %collective-permute-start.2 = (f32[34,2,2,256]{3,2,1,0:T(2,128)S(1)}, f32[34,2,2,256]{3,2,1,0:T(2,128)S(1)}, u32[]{:S(2)}, u32[]{:S(2)}) collective-permute-start(f32[34,2,2,256]{3,2,1,0:T(2,128)S(1)} %constant_dynamic-update-slice_fusion), channel_id=1, source_target_pairs={{12,0},{16,4},{20,8},{24,12},{28,16},{13,1},{17,5},{21,9},{25,13},... | collective-permute-start | bytes 417800 | tf_op jit(solution)/shard_map/ppermute | solution.py:22

commit v12 on v11

--- a/solution.py
+++ b/solution.py
@@ -111,11 +111,7 @@
         sent = jnp.concatenate([spec.reshape(rows_local, series, 2, factor_b)[: BAND + 1], scale_row])
     else:
         sent = whitened
-    if paired:
-        row_ids = jnp.concatenate([k1_ids[: BAND + 1], k1_ids[BAND + 1 :][::-1]])
-    else:
-        row_ids = k1_ids
-    row_ids, turned_index = lax.optimization_barrier((row_ids, factor_b - 1 - index_b, sent))[:2]
+    k1_ids = lax.optimization_barrier((k1_ids, sent))[0]
     arrived = {}
     for distance in range(REACH, 0, -1):
         arrived[distance] = passed_along(sent, "sta", -distance)
@@ -131,44 +127,52 @@
             result = jnp.where(pick == distance, nearby[distance], result)
         return result
 
-    def domain(block):
-        if not paired:
-            return block
-        spec_part = block[:, : BAND + 1]
-        scale_low = block[:, BAND + 1, :, 0][:, None, :, None, :]
-        scale_high = block[:, BAND + 1, :, 1]
-        scale_turned = scale_high[:, :, ::-1][:, None, :, None, :]
-        conj_sign = (1 - 2 * lax.iota(jnp.int32, 2)).astype(jnp.float32)[None, None, None, :, None]
-        low = spec_part[:, :BAND] * scale_low
-        middle = spec_part[:, BAND:] * scale_high[:, None, :, None, :]
-        high = spec_part[:, 1:BAND] * conj_sign * scale_turned
-        return jnp.concatenate([low, middle, high], axis=1)
-
-    spec_shape = (slot_total, rows_local, stations, hour_count, 2, factor_b)
-    left_spec = domain(chosen(first_off)).reshape(spec_shape)
-    right_spec = domain(chosen(second_off)).reshape(spec_shape)
+    def inverse_of(cosines, sines):
+        return jnp.concatenate(
+            [jnp.concatenate([cosines, sines], axis=1), jnp.concatenate([-sines, cosines], axis=1)],
+            axis=0,
+        )
+
+    left_block = chosen(first_off)
+    right_block = chosen(second_off)
+    if paired:
+        kept = BAND + 1
+        spec_shape = (slot_total, kept, stations, hour_count, 2, factor_b)
+        scale_shape = (slot_total, stations, hour_count, factor_b)
+        left_spec = left_block[:, :kept].reshape(spec_shape)
+        right_spec = right_block[:, :kept].reshape(spec_shape)
+
+        def weight(left_scale, right_scale):
+            return left_scale[:, None, :, None] * right_scale[:, None, None, :]
+
+        left_low = left_block[:, kept, :, 0].reshape(scale_shape)
+        left_high = left_block[:, kept, :, 1].reshape(scale_shape)
+        right_low = right_block[:, kept, :, 0].reshape(scale_shape)
+        right_high = right_block[:, kept, :, 1].reshape(scale_shape)
+        weight_low = weight(left_low, right_low)
+        weight_high = weight(left_high, right_high)
+        weight_paired = weight_low + weight(left_high[..., ::-1], right_high[..., ::-1])
+        row_weight = jnp.concatenate(
+            [weight_low, jnp.broadcast_to(weight_paired, (slot_total, BAND - 1) + weight_paired.shape[2:]), weight_high],
+            axis=1,
+        )
+    else:
+        kept = rows_local
+        spec_shape = (slot_total, kept, stations, hour_count, 2, factor_b)
+        left_spec = left_block.reshape(spec_shape)
+        right_spec = right_block.reshape(spec_shape)
+        row_weight = jnp.ones((1, 1, 1, 1, 1, 1), jnp.float32)
     left_real = left_spec[:, :, :, None, :, 0]
     left_imag = left_spec[:, :, :, None, :, 1]
     right_real = right_spec[:, :, None, :, :, 0]
     right_imag = right_spec[:, :, None, :, :, 1]
-    cross_real = jnp.sum(left_real * right_real + left_imag * right_imag, axis=4)
-    cross_imag = jnp.sum(left_imag * right_real - left_real * right_imag, axis=4)
+    cross_real = jnp.sum((left_real * right_real + left_imag * right_imag) * row_weight, axis=4)
+    cross_imag = jnp.sum((left_imag * right_real - left_real * right_imag) * row_weight, axis=4)
     cross = jnp.concatenate([cross_real, cross_imag], axis=-1)
-
-    def inverse_of(cosines, sines):
-        return jnp.concatenate(
-            [jnp.concatenate([cosines, sines], axis=1), jnp.concatenate([-sines, cosines], axis=1)],
-            axis=0,
-        )
-
-    lag_shape = (slot_total, -1, stations, stations, 2, factor_b)
-    if paired:
-        cosine_r, sine_r = angles(turned_index, index_b, factor_b)
-        lag_low = matmul(cross[:, : BAND + 1].reshape(-1, 2 * factor_b), inverse_of(cosine_b, sine_b))
-        lag_high = matmul(cross[:, BAND + 1 :].reshape(-1, 2 * factor_b), inverse_of(cosine_r, sine_r))
-        lag = jnp.concatenate([lag_low.reshape(lag_shape), lag_high.reshape(lag_shape)], axis=1)
-    else:
-        lag = matmul(cross.reshape(-1, 2 * factor_b), inverse_of(cosine_b, sine_b)).reshape(lag_shape)
+    lag = matmul(cross.reshape(-1, 2 * factor_b), inverse_of(cosine_b, sine_b)).reshape(
+        slot_total, kept, stations, stations, 2, factor_b
+    )
+    row_ids = k1_ids[:kept]
     lag_real, lag_imag = lag[:, :, :, :, 0], lag[:, :, :, :, 1]
     cosine_u, sine_u = angles(row_ids, index_b, SAMPLES)
     turn_real = lag_real * cosine_u[None, :, None, None, :] - lag_imag * sine_u[None, :, None, None, :]
@@ -178,7 +182,7 @@
     )
     cosine_l, sine_l = angles(lag_ids, row_ids, factor_a)
     lag_weights = jnp.concatenate([cosine_l, -sine_l], axis=1).reshape(
-        time_devices, 2 * LAGS // time_devices, 2 * rows_local
+        time_devices, 2 * LAGS // time_devices, 2 * kept
     )
     turned = jnp.concatenate([turn_real, turn_imag], axis=1)
     scale_out = 1.0 / math.sqrt(SAMPLES * hour_count)

time: 53.3 us -> 51.9 us (0.974)
  other arithmetic: 8.08 us -> 6.27 us
  waiting for transfers between devices: 16.7 us -> 18.3 us
  matrix products: 3.28 us -> 2.32 us
    ppermute x3, waiting for transfers between devices: 11.4 us -> 12.8 us  [passed_along(): return lax.ppermute(block, axis, route)]
    sin x3 -> x2, other arithmetic: 2.07 us -> 1.02 us  [angles(): return (jnp.cos(radians), jnp.sin(radians))]
    dot_general x4 -> x3, matrix products: 2.78 us -> 1.94 us  [matmul(): jnp.dot(left_mat, right_mat, precision=highest, preferred_element_type=jn...]
  transfers between devices with their start and end apart: 5 -> 5, of which waited for: 5 -> 5; matrix products, arithmetic and copies ran while one was open for 9% -> 6% of each run, Pallas kernels for 0% -> 0%
where the time goes in v12:
time: 51.9 us; the launch traced here: 51.4 us
  waiting for transfers between devices  18.3 us (35%)
  starting transfers between devices  11.2 us (22%)
  blocking collectives  6.67 us (13%)
  other arithmetic  6.27 us (12%)
  local copies, waits for them, and re-layouts  5.49 us (11%)
  matrix products  2.32 us (4%)
  between operations  1.2 us (2%)
    ppermute x3, waiting for transfers between devices, passed_along(): return lax.ppermute(block, axis, route)  12.8 us
    all_to_all x1, blocking collectives, local(): lax.all_to_all(lag_block.reshape(time_devices, -1), 'tm', split_axis=0, c...  6.67 us
    all_to_all x1, waiting for transfers between devices, local(): lax.all_to_all(outgoing.reshape(time_devices, -1), 'tm', split_axis=0, co...  4.53 us
    ppermute x3, starting transfers between devices, passed_along(): return lax.ppermute(block, axis, route)  4.52 us
    all_to_all x1, starting transfers between devices, local(): lax.all_to_all(outgoing.reshape(time_devices, -1), 'tm', split_axis=0, co...  3.33 us
    all_to_all x1, starting transfers between devices, local(): lax.all_to_all(arranged.reshape(time_devices, -1), 'tm', split_axis=0, co...  3.32 us
    cos x4, other arithmetic, angles(): return (jnp.cos(radians), jnp.sin(radians))  1.95 us
    dot_general x3, matrix products, matmul(): jnp.dot(left_mat, right_mat, precision=highest, preferred_element_type=jn...  1.94 us
  transfers between devices with their start and end apart: 5, of which 5 were waited for; matrix products, arithmetic and copies ran while one was open for 6% of the time, Pallas kernels for 0%

profile of v12, /device:TPU:2, one launch (start us, length us, event | category | flops | bytes accessed | tf_op | source)
XLA Modules:
  0.0 51.4 jit_solution(9278041152050928292)
XLA Ops:
  0.0 1.3 %reduce.2 = f32[2,16384]{1,0:T(2,128)S(1)} reduce(f32[2,1,16384]{2,1,0:T(1,128)} %param.3, f32[]{:T(128)} %constant.101), dimensions={1}, to_apply=%param.3.reduce_sub_computation | reduce | bytes 262148 | tf_op args[0]
  1.3 0.2 reshape.418
  1.5 0.2 copy.81
  1.7 0.9 %all_to_all.24 = f32[4,1,8192]{2,1,0:T(1,128)} reshape(f32[4,64,2,64]{3,2,1,0:T(2,128)S(1)} %bitcast.116) | data formatting | bytes 262144 | tf_op jit(solution)/shard_map/all_to_all | solution.py:46
  2.7 3.3 %all-to-all-start = ((f32[4,1,8192]{2,1,0:T(1,128)}), f32[4,1,8192]{2,1,0:T(1,128)S(1)}, u32[]{:S(2)}, u32[]{:S(2)}) async-start(f32[4,1,8192]{2,1,0:T(1,128)} %all_to_all.24), calls=%async_computation | async-start | bytes 262144 | tf_op jit(solution)/shard_map/all_to_all | solution.py:46
  6.0 1.0 %fusion.31 = (f32[256,256]{0,1:T(8,128)S(1)}, f32[256,256]{0,1:T(8,128)S(1)}) fusion(), kind=kLoop, calls=%fused_computation.67 | loop fusion | flops 983040 | bytes 524288 | tf_op jit(solution)/shard_map/cos | solution.py:28
  7.0 1.0 %fusion.30 = f32[256,256]{0,1:T(8,128)S(1)} fusion(), kind=kLoop, calls=%fused_computation.66 | loop fusion | flops 917504 | bytes 262144 | tf_op jit(solution)/shard_map/sin | solution.py:28
  8.0 0.5 %fusion.36 = (f32[256,64]{1,0:T(8,128)S(1)}, f32[256,64]{1,0:T(8,128)S(1)}) fusion(s32[64]{0:T(128)S(1)} %iota_add_fusion.2), kind=kLoop, calls=%fused_computation.72 | loop fusion | flops 229376 | bytes 131328 | tf_op jit(solution)/shard_map/cos | solution.py:28
  8.6 0.1 fusion.54
  8.6 0.0 copy-start
  9.3 0.0 copy-done
  9.4 0.1 pad_add_fusion
  9.4 0.1 fusion.3
  9.6 1.0 %all-to-all-done = f32[4,1,8192]{2,1,0:T(1,128)S(1)} async-done(((f32[4,1,8192]{2,1,0:T(1,128)}), f32[4,1,8192]{2,1,0:T(1,128)S(1)}, u32[]{:S(2)}, u32[]{:S(2)}) %all-to-all-start) | async-done | bytes 131104 | tf_op jit(solution)/shard_map/all_to_all | solution.py:46
  10.6 0.3 fusion.11
  10.9 0.1 copy.41
  11.0 0.1 copy.42
  11.2 0.1 multiply_add_fusion.1
  11.3 0.1 pad_maximum_fusion.5
  11.4 0.1 copy.46
  11.6 0.9 %all_to_all.25 = f32[4,1,8448]{2,1,0:T(1,128)} reshape(f32[4,33,2,2,64]{4,3,2,1,0:T(2,128)S(1)} %copy.46) | data formatting | bytes 270336 | tf_op jit(solution)/shard_map/all_to_all | solution.py:76
  12.5 3.3 %all-to-all-start.1 = ((f32[4,1,8448]{2,1,0:T(1,128)}), f32[4,1,8448]{2,1,0:T(1,128)S(1)}, u32[]{:S(2)}, u32[]{:S(2)}) async-start(f32[4,1,8448]{2,1,0:T(1,128)} %all_to_all.25), calls=%async_computation.1 | async-start | bytes 270336 | tf_op jit(solution)/shard_map/all_to_all | solution.py:76
  15.8 0.1 pad_add_fusion.1
  15.9 4.5 %all-to-all-done.1 = f32[4,1,8448]{2,1,0:T(1,128)S(1)} async-done(((f32[4,1,8448]{2,1,0:T(1,128)}), f32[4,1,8448]{2,1,0:T(1,128)S(1)}, u32[]{:S(2)}, u32[]{:S(2)}) %all-to-all-start.1) | async-done | bytes 135200 | tf_op jit(solution)/shard_map/all_to_all | solution.py:76
  20.5 0.4 reduce.3
  20.8 0.2 reshape.420
  21.1 0.1 copy.48
  21.1 0.1 copy.63
  21.2 0.2 reshape.431
  21.4 0.1 fusion.63
  21.5 0.2 reshape.421
  21.8 0.1 multiply_subtract_fusion.2
  21.9 0.2 maximum_maximum_fusion
  22.1 0.6 %fusion.1 = f32[128,512]{1,0:T(8,128)S(1)} fusion(f32[128,512]{1,0:T(8,128)S(1)} %bitcast.123, f32[256,256]{0,1:T(8,128)S(1)} %get-tuple-element.45, f32[256,256]{0,1:T(8,128)S(1)} %fusion.30, f32[256,256]{0,1:T(8,128)S(1)} %get-tuple-element.46), kind=kOutput, calls=%fused_computation.6 | convolution fusion | flops 202113024 | bytes 1310720 | tf_op jit(solution)/shard_map/dot_general | solution.py:32
  22.8 0.2 reshape.423
  23.0 0.1 slice.109
  23.1 0.3 fusion.33
  23.4 1.9 %collective-permute-start = (f32[34,2,2,256]{3,2,1,0:T(2,128)S(1)}, f32[34,2,2,256]{3,2,1,0:T(2,128)S(1)}, u32[]{:S(2)}, u32[]{:S(2)}) collective-permute-start(f32[34,2,2,256]{3,2,1,0:T(2,128)S(1)} %constant_dynamic-update-slice_fusion), channel_id=1, source_target_pairs={{4,0},{8,4},{12,8},{16,12},{20,16},{24,20},{28,24},{5,1},{9,5},{13... | collective-permute-start | bytes 417800 | tf_op jit(solution)/shard_map/ppermute | solution.py:22
  25.3 1.3 %collective-permute-start.1 = (f32[34,2,2,256]{3,2,1,0:T(2,128)S(1)}, f32[34,2,2,256]{3,2,1,0:T(2,128)S(1)}, u32[]{:S(2)}, u32[]{:S(2)}) collective-permute-start(f32[34,2,2,256]{3,2,1,0:T(2,128)S(1)} %constant_dynamic-update-slice_fusion), channel_id=1, source_target_pairs={{8,0},{12,4},{16,8},{20,12},{24,16},{28,20},{9,1},{13,5},{17,9},{2... | collective-permute-start | bytes 417800 | tf_op jit(solution)/shard_map/ppermute | solution.py:22
  26.6 1.3 %collective-permute-start.2 = (f32[34,2,2,256]{3,2,1,0:T(2,128)S(1)}, f32[34,2,2,256]{3,2,1,0:T(2,128)S(1)}, u32[]{:S(2)}, u32[]{:S(2)}) collective-permute-start(f32[34,2,2,256]{3,2,1,0:T(2,128)S(1)} %constant_dynamic-update-slice_fusion), channel_id=1, source_target_pairs={{12,0},{16,4},{20,8},{24,12},{28,16},{13,1},{17,5},{21,9},{25,13},... | collective-permute-start | bytes 417800 | tf_op jit(solution)/shard_map/ppermute | solution.py:22
  27.9 0.2 fusion.44
  28.2 0.1 fusion.50
  28.3 4.0 %collective-permute-done = f32[34,2,2,256]{3,2,1,0:T(2,128)S(1)} collective-permute-done((f32[34,2,2,256]{3,2,1,0:T(2,128)S(1)}, f32[34,2,2,256]{3,2,1,0:T(2,128)S(1)}, u32[]{:S(2)}, u32[]{:S(2)}) %collective-permute-start) | collective-permute-done | bytes 139296 | tf_op jit(solution)/shard_map/ppermute | solution.py:22
  32.3 1.1 %collective-permute-done.1 = f32[34,2,2,256]{3,2,1,0:T(2,128)S(1)} collective-permute-done((f32[34,2,2,256]{3,2,1,0:T(2,128)S(1)}, f32[34,2,2,256]{3,2,1,0:T(2,128)S(1)}, u32[]{:S(2)}, u32[]{:S(2)}) %collective-permute-start.1) | collective-permute-done | bytes 139296 | tf_op jit(solution)/shard_map/ppermute | solution.py:22
  33.4 7.7 %collective-permute-done.2 = f32[34,2,2,256]{3,2,1,0:T(2,128)S(1)} collective-permute-done((f32[34,2,2,256]{3,2,1,0:T(2,128)S(1)}, f32[34,2,2,256]{3,2,1,0:T(2,128)S(1)}, u32[]{:S(2)}, u32[]{:S(2)}) %collective-permute-start.2) | collective-permute-done | bytes 139296 | tf_op jit(solution)/shard_map/ppermute | solution.py:22
  41.2 0.2 select_select_fusion.1
  41.7 0.2 rev.12
  41.9 0.2 rev.11
  42.2 0.2 fusion.16
  42.4 1.0 %fusion.6 = f32[3,33,2,2,2,256]{5,1,4,3,2,0:T(8,128)S(1)} fusion(f32[2,256,512,1,1,1]{2,1,0,5,4,3:T(8,128)S(1)} %bitcast.111, f32[3,33,2,2,256]{4,1,3,2,0:T(8,128)S(1)} %get-tuple-element.8, f32[3,33,2,2,256]{4,1,3,2,0:T(8,128)S(1)} %get-tuple-element.7), kind=kOutput, calls=%fused_computation.11 | convolution fusion | flops 623056896 | bytes 2670592 | tf_op jit(solution)/shard_map/dot_general | solution.py:32
  43.4 0.1 multiply_subtract_fusion
  43.5 0.4 convolution_multiply_fusion
  43.9 0.1 copy.58
  44.0 6.7 %all_to_all.29 = f32[4,1,6144]{2,1,0:T(1,128)S(1)} all-to-all(f32[4,1,6144]{2,1,0:T(1,128)S(1)} %copy.58), channel_id=1, replica_groups=mesh['sta'=8,'tm'=4] {'tm'}, dimensions={0} | all-to-all | bytes 196608 | tf_op jit(solution)/shard_map/all_to_all | solution.py:198
  50.7 0.1 reduce_sum.20
  50.8 0.6 %reshape.426 = f32[3,2,2,512]{3,2,1,0:T(2,128)} reshape(f32[6144]{0:T(1024)S(1)} %reduce_sum.20) | data formatting | bytes 49152 | tf_op jit(solution)/shard_map/reshape | solution.py:202
  (36 shorter events, 0.6 us)
Async XLA Ops:
  2.7 7.9 %all-to-all-start = ((f32[4,1,8192]{2,1,0:T(1,128)}), f32[4,1,8192]{2,1,0:T(1,128)S(1)}, u32[]{:S(2)}, u32[]{:S(2)}) async-start(f32[4,1,8192]{2,1,0:T(1,128)} %all_to_all.24), calls=%async_computation | async-start | bytes 262144 | tf_op jit(solution)/shard_map/all_to_all | solution.py:46
  8.6 0.7 %copy-start = (s32[3,2]{0,1:T(2,128)S(1)}, s32[3,2]{0,1:T(2,128)}, u32[]{:S(2)}) copy-start(s32[3,2]{0,1:T(2,128)} %param.4) | copy-start | bytes 76
  12.5 7.9 %all-to-all-start.1 = ((f32[4,1,8448]{2,1,0:T(1,128)}), f32[4,1,8448]{2,1,0:T(1,128)S(1)}, u32[]{:S(2)}, u32[]{:S(2)}) async-start(f32[4,1,8448]{2,1,0:T(1,128)} %all_to_all.25), calls=%async_computation.1 | async-start | bytes 270336 | tf_op jit(solution)/shard_map/all_to_all | solution.py:76
  23.4 8.9 %collective-permute-start = (f32[34,2,2,256]{3,2,1,0:T(2,128)S(1)}, f32[34,2,2,256]{3,2,1,0:T(2,128)S(1)}, u32[]{:S(2)}, u32[]{:S(2)}) collective-permute-start(f32[34,2,2,256]{3,2,1,0:T(2,128)S(1)} %constant_dynamic-update-slice_fusion), channel_id=1, source_target_pairs={{4,0},{8,4},{12,8},{16,12},{20,16},{24,20},{28,24},{5,1},{9,5},{13... | collective-permute-start | bytes 417800 | tf_op jit(solution)/shard_map/ppermute | solution.py:22
  25.3 8.1 %collective-permute-start.1 = (f32[34,2,2,256]{3,2,1,0:T(2,128)S(1)}, f32[34,2,2,256]{3,2,1,0:T(2,128)S(1)}, u32[]{:S(2)}, u32[]{:S(2)}) collective-permute-start(f32[34,2,2,256]{3,2,1,0:T(2,128)S(1)} %constant_dynamic-update-slice_fusion), channel_id=1, source_target_pairs={{8,0},{12,4},{16,8},{20,12},{24,16},{28,20},{9,1},{13,5},{17,9},{2... | collective-permute-start | bytes 417800 | tf_op jit(solution)/shard_map/ppermute | solution.py:22
  26.6 14.6 %collective-permute-start.2 = (f32[34,2,2,256]{3,2,1,0:T(2,128)S(1)}, f32[34,2,2,256]{3,2,1,0:T(2,128)S(1)}, u32[]{:S(2)}, u32[]{:S(2)}) collective-permute-start(f32[34,2,2,256]{3,2,1,0:T(2,128)S(1)} %constant_dynamic-update-slice_fusion), channel_id=1, source_target_pairs={{12,0},{16,4},{20,8},{24,12},{28,16},{13,1},{17,5},{21,9},{25,13},... | collective-permute-start | bytes 417800 | tf_op jit(solution)/shard_map/ppermute | solution.py:22
